TPU v7x, 256 devices: a whole 4x4x8 slice. The times are simulated.
256 devices in a mesh: tm: 8 (over x, core), sx: 8 (over z), sy: 4 (over y).
Axes of the slice: x: 4, y: 4, z: 8, core: 2. Of those that a mesh axis runs over, the one named last changes fastest.
Arguments:
- initial_saturation: float32 [32, 64, 256], P('sx', 'sy'), may hold values from 0.05 to 0.95
- permeability: float32 [32, 64, 256], P('sx', 'sy'), may hold values from 0.1 to 10
- porosity: float32 [32, 64, 256], P('sx', 'sy'), may hold values from 0.1 to 0.3
- source_rate: float32 [32, 64, 256], P('sx', 'sy'), may hold values from -3 to 3
- rock_type: int32 [16, 32, 128], P('sx', 'sy'), may hold values from 0 to 3
- water_endpoint: float32 [4], replicated, may hold values from 0.3 to 1
- oil_endpoint: float32 [4], replicated, may hold values from 0.3 to 1
Outputs:
- end_saturation: float32 [8, 32, 64, 256], P('tm', 'sx', 'sy')
- last_pressure: float32 [8, 32, 64, 256], P('tm', 'sx', 'sy')
All inputs are finite; a program needn't handle non-finite values.
Results may differ from a plain program's by a relative error of at most 0.0003.
Values sent between devices are 32-bit elements; how exact they have to be, the bound alone decides.
No kernel may reach another device: no remote copies, remote signals or barrier semaphores. Data moves between devices by JAX's collectives and lax.ppermute only.
A program may use at most 64 MiB of HBM per device.

v0:
```python
import jax
import jax.numpy as jnp
from jax import lax
from jax.sharding import PartitionSpec as P

FSTEPS = 1
NEWTON = 2
CG_ITERS = 3
SWEEPS = 3
PARAREAL = 2
ROCKS = 4


mu_water = 1.0
mu_oil = 4.0
compress = 0.05
step_dt = 0.25
damping = 0.8


def extended(array, sides, width):
    for axis, dim in sides:
        size, length = (lax.axis_size(axis), array.shape[dim])
        up = [(i, (i + 1) % size) for i in range(size - 1)]
        down = [(j, i) for i, j in up]
        last = lax.slice_in_dim(array, length - width, length, axis=dim)
        initial = lax.slice_in_dim(array, 0, width, axis=dim)
        before = lax.ppermute(last, axis, up)
        after = lax.ppermute(initial, axis, down)
        array = jnp.concatenate([before, array, after], axis=dim)
    return array


def passed_along(value, axis, steps):
    count = lax.axis_size(axis)
    initial, last = (max(0, -steps), min(count, count - steps))
    return lax.ppermute(value, axis, [(source, source + steps) for source in range(initial, last)])


def lookup(rock_cells, end_values):
    summed_total = jnp.zeros(rock_cells.shape, end_values.dtype)
    for rock_kind in range(ROCKS):
        summed_total = summed_total + jnp.where(
            rock_cells == rock_kind, end_values[rock_kind], jnp.zeros((), end_values.dtype)
        )
    return summed_total


def restrict(volume):
    return volume.reshape(
        volume.shape[0] // 2, 2, volume.shape[1] // 2, 2, volume.shape[2] // 2, 2
    ).mean(axis=(1, 3, 5))


def prolong(volume):
    first, second, third = volume.shape
    spread_out = jnp.broadcast_to(
        volume[:, None, :, None, :, None], (first, 2, second, 2, third, 2)
    )
    return spread_out.reshape(2 * first, 2 * second, 2 * third)


def pad_depth(volume):
    return jnp.pad(volume, ((0, 0), (0, 0), (1, 1)))


def face_list(padded):
    return [
        padded[2:, 1:-1, 1:-1],
        padded[:-2, 1:-1, 1:-1],
        padded[1:-1, 2:, 1:-1],
        padded[1:-1, :-2, 1:-1],
        padded[1:-1, 1:-1, 2:],
        padded[1:-1, 1:-1, :-2],
    ]


def face_mobility_values(volume):
    return face_list(pad_depth(extended(volume, (("sx", 0), ("sy", 1)), 1)))


def direction_spread(volume):
    return extended(volume, (("sx", 0), ("sy", 1)), 1)


def pressure_faces(volume):
    return face_list(pad_depth(extended(volume, (("sx", 0), ("sy", 1)), 1)))


def flow_faces(volume):
    return face_list(pad_depth(extended(volume, (("sx", 0), ("sy", 1)), 1)))


def build_face_tables(volume):
    return face_list(pad_depth(extended(volume, (("sx", 0), ("sy", 1)), 1)))


def coarse_faces(volume):
    return face_list(pad_depth(extended(volume, (("sx", 0), ("sy", 1)), 1)))


def accumulate_terms(summand_terms):
    summed_total = summand_terms[0]
    for summand_term in summand_terms[1:]:
        summed_total = summed_total + summand_term
    return summed_total


def mobilities(saturation, water_end, oil_end):
    water_mobility = water_end * saturation * saturation / mu_water
    oil_mobility = oil_end * (1.0 - saturation) * (1.0 - saturation) / mu_oil
    return (water_mobility, oil_mobility)


def fractional(saturation, water_end, oil_end):
    water_mobility, oil_mobility = mobilities(saturation, water_end, oil_end)
    mobility = water_mobility + oil_mobility
    water_slope = 2.0 * water_end * saturation / mu_water
    oil_slope = -2.0 * oil_end * (1.0 - saturation) / mu_oil
    return (
        water_mobility / mobility,
        (water_slope * oil_mobility - water_mobility * oil_slope) / (mobility * mobility),
    )


def upwind(frac, frac_beyond, outflows):
    return accumulate_terms(
        [
            jnp.maximum(outward, 0.0) * frac + jnp.minimum(outward, 0.0) * exceeding_part
            for outward, exceeding_part in zip(outflows, frac_beyond)
        ]
    )


def residual_dot(residual, precond):
    return lax.psum(jnp.sum(residual * precond), ("sx", "sy"))


def solve_pressure(source_rate, diagonal, transmissibility):
    solution = jnp.zeros_like(source_rate)
    residual = source_rate
    precond = residual / diagonal
    direction = precond
    rho_now = residual_dot(residual, precond)
    for sweep_no in range(CG_ITERS):
        spread_vec = direction_spread(direction)
        applied = diagonal * direction - accumulate_terms(
            [
                conduct_face * exceeding_part
                for conduct_face, exceeding_part in zip(
                    transmissibility, face_list(pad_depth(spread_vec))
                )
            ]
        )
        step_len = rho_now / lax.psum(jnp.sum(direction * applied), ("sx", "sy"))
        solution = solution + step_len * direction
        if sweep_no + 1 < CG_ITERS:
            residual = residual - step_len * applied
            precond = residual / diagonal
            rho_next = residual_dot(residual, precond)
            direction = precond + rho_next / rho_now * direction
            rho_now = rho_next
    return solution


def fine_step(sat_old, permeability, porosity, source_rate, water_end, oil_end):
    water_mobility, oil_mobility = mobilities(sat_old, water_end, oil_end)
    transport_field = permeability * (water_mobility + oil_mobility)
    transmissibility = [
        0.5 * (transport_field + exceeding_part)
        for exceeding_part in face_mobility_values(transport_field)
    ]
    diagonal = compress + accumulate_terms(transmissibility)
    pressure = solve_pressure(source_rate, diagonal, transmissibility)
    beside = pressure_faces(pressure)
    outflows = [
        conduct_face * (pressure - exceeding_part)
        for conduct_face, exceeding_part in zip(transmissibility, beside)
    ]
    outgoing = accumulate_terms([jnp.maximum(outward, 0.0) for outward in outflows])
    saturation = sat_old
    for newton_no in range(NEWTON):
        frac, frac_slope = fractional(saturation, water_end, oil_end)
        flux_sum = upwind(frac, flow_faces(frac), outflows)
        balance = (
            porosity * (saturation - sat_old) / step_dt
            + flux_sum
            - jnp.maximum(source_rate, 0.0)
            - jnp.minimum(source_rate, 0.0) * frac
        )
        slope_sum = porosity / step_dt + jnp.abs(frac_slope) * (
            outgoing + jnp.maximum(-source_rate, 0.0)
        )
        saturation = saturation - balance / slope_sum
    return (saturation, pressure)


def local(
    initial_saturation, permeability, porosity, source_rate, rock_type, water_endpoint, oil_endpoint
):
    slices = lax.axis_size("tm")
    slice_index = lax.axis_index("tm")
    water_coarse = lookup(rock_type, water_endpoint)
    oil_coarse = lookup(rock_type, oil_endpoint)
    water_fine = prolong(water_coarse)
    oil_fine = prolong(oil_coarse)
    start_coarse = restrict(initial_saturation)
    permeability_upscaled = restrict(permeability)
    poro_coarse = restrict(porosity)
    source_coarse = restrict(source_rate)
    water_mobility, oil_mobility = mobilities(start_coarse, water_coarse, oil_coarse)
    transport_field_upscaled = permeability_upscaled * (water_mobility + oil_mobility)
    transmissibility_upscaled = [
        (transport_field_upscaled + exceeding_part) / 8.0
        for exceeding_part in build_face_tables(transport_field_upscaled)
    ]
    diag_coarse = compress + accumulate_terms(transmissibility_upscaled)
    pressure_coarse = damping * source_coarse / diag_coarse
    for sweep_no in range(SWEEPS):
        beside = build_face_tables(pressure_coarse)
        if sweep_no + 1 < SWEEPS:
            coupled = accumulate_terms(
                [
                    conduct_face * exceeding_part
                    for conduct_face, exceeding_part in zip(transmissibility_upscaled, beside)
                ]
            )
            pressure_coarse = (
                pressure_coarse
                + damping
                * (source_coarse - (diag_coarse * pressure_coarse - coupled))
                / diag_coarse
            )
    flows_coarse = [
        conduct_face * (pressure_coarse - exceeding_part)
        for conduct_face, exceeding_part in zip(transmissibility_upscaled, beside)
    ]
    outgoing_coarse = accumulate_terms([jnp.maximum(outward, 0.0) for outward in flows_coarse])
    coarse_dt = FSTEPS * step_dt

    def coarse_step(coarse_state):
        frac, frac_slope = fractional(coarse_state, water_coarse, oil_coarse)
        flux_sum = upwind(frac, coarse_faces(frac), flows_coarse)
        balance = (
            flux_sum - jnp.maximum(source_coarse, 0.0) - jnp.minimum(source_coarse, 0.0) * frac
        )
        slope_sum = poro_coarse / coarse_dt + jnp.abs(frac_slope) * (
            outgoing_coarse + jnp.maximum(-source_coarse, 0.0)
        )
        return coarse_state - balance / slope_sum

    def chain(corrections):

        def relay_round(turn_no, coarse_state):
            coarse_image = coarse_step(coarse_state)
            if corrections is None:
                outgoing_state = coarse_image
            else:
                outgoing_state = coarse_image + corrections
            arrived = passed_along(outgoing_state, "tm", 1)
            return jnp.where(slice_index == 0, start_coarse, arrived)

        coarse_state = lax.fori_loop(0, slices - 1, relay_round, start_coarse)
        return (coarse_state, coarse_step(coarse_state))

    coarse_state, coarse_image = chain(None)
    starts = jnp.where(slice_index == 0, initial_saturation, prolong(coarse_state))
    previous_image = coarse_image
    ends = starts
    pressure = starts
    for parareal_no in range(PARAREAL):
        saturation = starts
        saturation, fine_pressure = fine_step(
            saturation, permeability, porosity, source_rate, water_fine, oil_fine
        )
        pressure = fine_pressure
        corrections = restrict(saturation) - previous_image
        coarse_state, coarse_image = chain(corrections)
        ends = prolong(coarse_image) + saturation - prolong(previous_image)
        if parareal_no + 1 < PARAREAL:
            arrived_start = passed_along(ends, "tm", 1)
            starts = jnp.where(slice_index == 0, initial_saturation, arrived_start)
        previous_image = coarse_image
    return (ends[None], pressure[None])


def solution(mesh):
    in_specs = (
        P("sx", "sy", None),
        P("sx", "sy", None),
        P("sx", "sy", None),
        P("sx", "sy", None),
        P("sx", "sy", None),
        P(),
        P(),
    )
    out_specs = (P("tm", "sx", "sy", None), P("tm", "sx", "sy", None))
    return jax.shard_map(local, mesh=mesh, in_specs=in_specs, out_specs=out_specs, check_vma=False)
```

profile of v0, /device:TPU:6, one launch (start us, length us, event | category | flops | bytes accessed | tf_op | source)
XLA Modules:
  0.0 1598.2 jit_solution(18161970518070408491)
XLA Ops:
  4.3 6.3 reshape.47
  111.8 148.0 %while.36 = (s32[]{:T(128)}, f32[2,8,128]{2,1,0:T(8,128)S(1)}, pred[]{:T(512)}, f32[2,8,128]{2,1,0:T(8,128)S(1)}, f32[2,8,128]{2,1,0:T(8,128)S(1)}, /*index=5*/f...) while((s32[]{:T(128)}, f32[2,8,128]{2,1,0:T(8,128)S(1)}, ...), condition=%wide.region_5.6_spmd, body=%wide.region_4.5_spmd.sunk | while | flops 232386 | bytes 369318 | solution.py:263
  113.1 6.0 collective-permute-start.1
  134.0 6.0 collective-permute-start.1
  155.3 6.0 collective-permute-start.1
  197.4 6.0 collective-permute-start.1
  218.7 6.0 collective-permute-start.1
  239.9 6.0 collective-permute-start.1
  267.8 6.0 collective-permute-start.32
  284.3 6.0 collective-permute-start.36
  300.1 84.8 %all-reduce.25 = (f32[]{:T(128)}, f32[]{:T(128)}) all-reduce(f32[]{:T(128)} %get-tuple-element.611, f32[]{:T(128)} %get-tuple-element.610), channel_id=1, replica_groups=mesh['tm'=8,'sx'=8,'sy'=4] {'sx','sy'}, use_global_device_ids=true, to_apply=%region_7.8 | all-reduce | flops 2 | bytes 16 | tf_op jit(solution)/shard_map/psum | solution.py:136
  386.8 70.1 %psum.86 = f32[]{:T(128)} all-reduce(f32[]{:T(128)} %get-tuple-element.738), channel_id=1, replica_groups=mesh['tm'=8,'sx'=8,'sy'=4] {'sx','sy'}, use_global_device_ids=true, to_apply=%region_11.12 | all-reduce | flops 1 | bytes 8 | tf_op jit(solution)/shard_map/psum | solution.py:136
  473.5 72.4 %psum.87 = f32[]{:T(128)} all-reduce(f32[]{:T(128)} %get-tuple-element.736), channel_id=1, replica_groups=mesh['tm'=8,'sx'=8,'sy'=4] {'sx','sy'}, use_global_device_ids=true, to_apply=%region_13.14 | all-reduce | flops 1 | bytes 8 | tf_op jit(solution)/shard_map/psum | solution.py:155
  549.0 70.1 %psum.88 = f32[]{:T(128)} all-reduce(f32[]{:T(128)} %multiply_reduce_fusion.5), channel_id=1, replica_groups=mesh['tm'=8,'sx'=8,'sy'=4] {'sx','sy'}, use_global_device_ids=true, to_apply=%region_15.16 | all-reduce | flops 1 | bytes 8 | tf_op jit(solution)/shard_map/psum | solution.py:136
  640.5 72.1 %psum.89 = f32[]{:T(128)} all-reduce(f32[]{:T(128)} %fusion.215), channel_id=1, replica_groups=mesh['tm'=8,'sx'=8,'sy'=4] {'sx','sy'}, use_global_device_ids=true, to_apply=%region_17.18 | all-reduce | flops 1 | bytes 8 | tf_op jit(solution)/shard_map/psum | solution.py:155
  761.4 145.1 %while.37 = (s32[]{:T(128)}, f32[2,8,128]{2,1,0:T(8,128)S(1)}, pred[]{:T(512)}, f32[2,8,128]{2,1,0:T(8,128)S(1)}, f32[2,8,128]{2,1,0:T(8,128)S(1)}, /*index=5*/f...) while((s32[]{:T(128)}, f32[2,8,128]{2,1,0:T(8,128)S(1)}, ...), condition=%wide.region_20.21_spmd, body=%wide.region_19.20_spmd.sunk | while | flops 234434 | bytes 377518 | solution.py:263
  844.1 6.0 collective-permute-start.6
  865.3 6.0 collective-permute-start.6
  886.6 6.0 collective-permute-start.6
  907.8 6.0 collective-permute-start.64
  941.7 6.0 collective-permute-start.69
  957.9 6.0 collective-permute-start.73
  973.7 84.9 %all-reduce.24 = (f32[]{:T(128)}, f32[]{:T(128)}) all-reduce(f32[]{:T(128)} %get-tuple-element.609, f32[]{:T(128)} %get-tuple-element.608), channel_id=1, replica_groups=mesh['tm'=8,'sx'=8,'sy'=4] {'sx','sy'}, use_global_device_ids=true, to_apply=%region_22.23 | all-reduce | flops 2 | bytes 16 | tf_op jit(solution)/shard_map/psum | solution.py:136
  1060.5 70.3 %psum.92 = f32[]{:T(128)} all-reduce(f32[]{:T(128)} %get-tuple-element.720), channel_id=1, replica_groups=mesh['tm'=8,'sx'=8,'sy'=4] {'sx','sy'}, use_global_device_ids=true, to_apply=%region_26.27 | all-reduce | flops 1 | bytes 8 | tf_op jit(solution)/shard_map/psum | solution.py:136
  1147.4 72.4 %psum.93 = f32[]{:T(128)} all-reduce(f32[]{:T(128)} %get-tuple-element.718), channel_id=1, replica_groups=mesh['tm'=8,'sx'=8,'sy'=4] {'sx','sy'}, use_global_device_ids=true, to_apply=%region_28.29 | all-reduce | flops 1 | bytes 8 | tf_op jit(solution)/shard_map/psum | solution.py:155
  1221.7 70.1 %psum.94 = f32[]{:T(128)} all-reduce(f32[]{:T(128)} %multiply_reduce_fusion), channel_id=1, replica_groups=mesh['tm'=8,'sx'=8,'sy'=4] {'sx','sy'}, use_global_device_ids=true, to_apply=%region_30.31 | all-reduce | flops 1 | bytes 8 | tf_op jit(solution)/shard_map/psum | solution.py:136
  1313.2 72.3 %psum.95 = f32[]{:T(128)} all-reduce(f32[]{:T(128)} %fusion.123), channel_id=1, replica_groups=mesh['tm'=8,'sx'=8,'sy'=4] {'sx','sy'}, use_global_device_ids=true, to_apply=%region_32.33 | all-reduce | flops 1 | bytes 8 | tf_op jit(solution)/shard_map/psum | solution.py:155
  1430.3 144.3 %while.38 = (s32[]{:T(128)}, f32[2,8,128]{2,1,0:T(8,128)S(1)}, pred[]{:T(512)}, f32[2,8,128]{2,1,0:T(8,128)S(1)}, f32[2,8,128]{2,1,0:T(8,128)S(1)}, /*index=5*/f...) while((s32[]{:T(128)}, f32[2,8,128]{2,1,0:T(8,128)S(1)}, ...), condition=%wide.region_35.36_spmd, body=%wide.region_34.35_spmd.sunk | while | flops 234434 | bytes 377518 | solution.py:263
  1512.3 6.0 collective-permute-start.11
  1533.5 6.0 collective-permute-start.11
  1554.7 6.0 collective-permute-start.11
  1576.0 6.0 collective-permute-start.97
  (629 shorter events, 727.9 us)
Async XLA Ops:
  33.4 14.1 collective-permute-start.17
  34.7 12.8 collective-permute-start.18
  77.5 14.4 collective-permute-start.27
  78.8 13.1 collective-permute-start.28
  91.9 19.6 %collective-permute-start.29 = (f32[4,1,128]{2,1,0:T(1,128)S(1)}, f32[4,1,128]{2,1,0:T(1,128)S(1)}, u32[]{:S(2)}, u32[]{:S(2)}) collective-permute-start(f32[4,1,128]{2,1,0:T(1,128)S(1)} %get-tuple-element.842), channel_id=1, source_target_pairs={{1,0},{2,1},{3,2},{5,4},{6,5},{7,6},{9,8},{10,9},{11,10},{13,12},{... | collective-permute-start | bytes 6152 | tf_op jit(solution)/shard_map/ppermute | solution.py:29
  93.2 18.3 %collective-permute-start.30 = (f32[4,1,128]{2,1,0:T(1,128)S(1)}, f32[4,1,128]{2,1,0:T(1,128)S(1)}, u32[]{:S(2)}, u32[]{:S(2)}) collective-permute-start(f32[4,1,128]{2,1,0:T(1,128)S(1)} %get-tuple-element.841), channel_id=1, source_target_pairs={{0,1},{1,2},{2,3},{4,5},{5,6},{6,7},{8,9},{9,10},{10,11},{12,13},{... | collective-permute-start | bytes 6152 | tf_op jit(solution)/shard_map/ppermute | solution.py:28
  113.1 7.3 collective-permute-start.1
  197.4 7.3 collective-permute-start.1
  218.7 7.3 collective-permute-start.1
  239.9 7.3 collective-permute-start.1
  267.8 7.5 collective-permute-start.32
  284.3 7.5 collective-permute-start.36
  471.3 268.0 %collective-permute-start.59 = (f32[1,8,128]{2,1,0:T(8,128)S(1)}, f32[1,8,128]{2,1,0:T(8,128)S(1)}, u32[]{:S(2)}, u32[]{:S(2)}) collective-permute-start(f32[1,8,128]{2,1,0:T(8,128)S(1)} %get-tuple-element.854), channel_id=1, source_target_pairs={{4,0},{8,4},{12,8},{16,12},{20,16},{24,20},{28,24},{5,1},{9,5},{13... | collective-permute-start | bytes 12296 | tf_op jit(solution)/shard_map/ppermute | solution.py:29
  547.7 191.6 %collective-permute-start.60 = (f32[1,8,128]{2,1,0:T(8,128)S(1)}, f32[1,8,128]{2,1,0:T(8,128)S(1)}, u32[]{:S(2)}, u32[]{:S(2)}) collective-permute-start(f32[1,8,128]{2,1,0:T(8,128)S(1)} %get-tuple-element.853), channel_id=1, source_target_pairs={{0,4},{4,8},{8,12},{12,16},{16,20},{20,24},{24,28},{1,5},{5,9},{9,... | collective-permute-start | bytes 12296 | tf_op jit(solution)/shard_map/ppermute | solution.py:28
  633.5 81.7 %collective-permute-start.48 = (f32[1,16,256]{2,1,0:T(8,128)S(1)}, f32[1,16,256]{2,1,0:T(8,128)S(1)}, u32[]{:S(2)}, u32[]{:S(2)}) collective-permute-start(f32[1,16,256]{2,1,0:T(8,128)S(1)} %get-tuple-element.834), channel_id=1, source_target_pairs={{4,0},{8,4},{12,8},{16,12},{20,16},{24,20},{28,24},{5,1},{9,5},{13... | collective-permute-start | bytes 49160 | tf_op jit(solution)/shard_map/ppermute | solution.py:29
  635.7 84.1 %collective-permute-start.50 = (f32[1,16,256]{2,1,0:T(8,128)S(1)}, f32[1,16,256]{2,1,0:T(8,128)S(1)}, u32[]{:S(2)}, u32[]{:S(2)}) collective-permute-start(f32[1,16,256]{2,1,0:T(8,128)S(1)} %get-tuple-element.833), channel_id=1, source_target_pairs={{0,4},{4,8},{8,12},{12,16},{16,20},{20,24},{24,28},{1,5},{5,9},{9,... | collective-permute-start | bytes 49160 | tf_op jit(solution)/shard_map/ppermute | solution.py:28
  715.2 10.5 collective-permute-start.49
  721.1 10.5 collective-permute-start.54
  733.4 12.0 collective-permute-start.55
  734.7 10.7 collective-permute-start.56
  739.3 12.2 collective-permute-start.61
  740.6 11.0 collective-permute-start.62
  915.1 12.7 collective-permute-start.65
  916.4 11.5 collective-permute-start.66
  941.7 7.5 collective-permute-start.69
  957.9 7.5 collective-permute-start.73
  1306.2 87.1 %collective-permute-start.85 = (f32[1,16,256]{2,1,0:T(8,128)S(1)}, f32[1,16,256]{2,1,0:T(8,128)S(1)}, u32[]{:S(2)}, u32[]{:S(2)}) collective-permute-start(f32[1,16,256]{2,1,0:T(8,128)S(1)} %get-tuple-element.820), channel_id=1, source_target_pairs={{4,0},{8,4},{12,8},{16,12},{20,16},{24,20},{28,24},{5,1},{9,5},{13... | collective-permute-start | bytes 49160 | tf_op jit(solution)/shard_map/ppermute | solution.py:29
  1308.4 84.9 %collective-permute-start.87 = (f32[1,16,256]{2,1,0:T(8,128)S(1)}, f32[1,16,256]{2,1,0:T(8,128)S(1)}, u32[]{:S(2)}, u32[]{:S(2)}) collective-permute-start(f32[1,16,256]{2,1,0:T(8,128)S(1)} %get-tuple-element.819), channel_id=1, source_target_pairs={{0,4},{4,8},{8,12},{12,16},{16,20},{20,24},{24,28},{1,5},{5,9},{9,... | collective-permute-start | bytes 49160 | tf_op jit(solution)/shard_map/ppermute | solution.py:28
  1387.4 11.7 collective-permute-start.84
  1388.7 10.5 collective-permute-start.86
  1393.3 11.8 collective-permute-start.89
  1394.6 10.5 collective-permute-start.91
  (162 other events, 1070.2 us)
where the time goes:
time: 1610 us; the launch traced here: 1600 us
  blocking collectives  740 us (46%)
  starting transfers between devices  571 us (35%)
  waiting for transfers between devices  156 us (10%)
  local copies, waits for them, and re-layouts  77.1 us (5%)
  other arithmetic  39 us (2%)
    psum x6, blocking collectives, residual_dot(): return lax.psum(jnp.sum(residual * precond), ('sx', 'sy'))  450 us
    ppermute x84, starting transfers between devices, extended(): before = lax.ppermute(last, axis, up)  420 us
    psum x4, blocking collectives, solve_pressure(): step_len = rho_now / lax.psum(jnp.sum(direction * applied), ('sx', 'sy'))  289 us
    ppermute x84, starting transfers between devices, extended(): after = lax.ppermute(initial, axis, down)  108 us
    ppermute x84, waiting for transfers between devices, extended(): before = lax.ppermute(last, axis, up)  88.1 us
    ppermute x22, waiting for transfers between devices, passed_along(): lax.ppermute(value, axis, [(source, source + steps) for source in range(i...  67.5 us
    ppermute x22, starting transfers between devices, passed_along(): lax.ppermute(value, axis, [(source, source + steps) for source in range(i...  42.1 us
    reshape x6, local copies, waits for them, and re-layouts, restrict(): volume.reshape(volume.shape[0] // 2, 2, volume.shape[1] // 2, 2, volume.s...  34.2 us
  transfers between devices with their start and end apart: 190, of which 90 were waited for; matrix products, arithmetic and copies ran while one was open for 3% of the time, Pallas kernels for 0%

commit v1 on v0

--- a/solution.py
+++ b/solution.py
@@ -132,34 +132,45 @@
     )
 
 
-def residual_dot(residual, precond):
-    return lax.psum(jnp.sum(residual * precond), ("sx", "sy"))
+def global_sums(values):
+    count = lax.axis_size("sx") * lax.axis_size("sy")
+    packed = jnp.broadcast_to(jnp.stack(values)[None], (count, len(values)))
+    gathered = lax.all_to_all(packed, ("sx", "sy"), 0, 0, tiled=True)
+    totals = jnp.sum(gathered, axis=0)
+    return [totals[k] for k in range(len(values))]
+
+
+def apply_operator(diagonal, transmissibility, vector):
+    spread_vec = direction_spread(vector)
+    return diagonal * vector - accumulate_terms(
+        [
+            conduct_face * exceeding_part
+            for conduct_face, exceeding_part in zip(transmissibility, face_list(pad_depth(spread_vec)))
+        ]
+    )
 
 
 def solve_pressure(source_rate, diagonal, transmissibility):
-    solution = jnp.zeros_like(source_rate)
     residual = source_rate
-    precond = residual / diagonal
-    direction = precond
-    rho_now = residual_dot(residual, precond)
+    solution = None
     for sweep_no in range(CG_ITERS):
-        spread_vec = direction_spread(direction)
-        applied = diagonal * direction - accumulate_terms(
-            [
-                conduct_face * exceeding_part
-                for conduct_face, exceeding_part in zip(
-                    transmissibility, face_list(pad_depth(spread_vec))
-                )
-            ]
-        )
-        step_len = rho_now / lax.psum(jnp.sum(direction * applied), ("sx", "sy"))
-        solution = solution + step_len * direction
+        precond = residual / diagonal
+        image = apply_operator(diagonal, transmissibility, precond)
+        rho_next, curvature = global_sums([jnp.sum(residual * precond), jnp.sum(precond * image)])
+        if sweep_no == 0:
+            step_len = rho_next / curvature
+            direction = precond
+            applied = image
+            solution = step_len * direction
+        else:
+            ratio = rho_next / rho_now
+            step_len = rho_next / (curvature - ratio * rho_next / step_len)
+            direction = precond + ratio * direction
+            applied = image + ratio * applied
+            solution = solution + step_len * direction
         if sweep_no + 1 < CG_ITERS:
             residual = residual - step_len * applied
-            precond = residual / diagonal
-            rho_next = residual_dot(residual, precond)
-            direction = precond + rho_next / rho_now * direction
-            rho_now = rho_next
+        rho_now = rho_next
     return solution
 
 

time: 1610 us -> 1010 us (0.63)
  blocking collectives: 740 us -> 74.1 us
  starting transfers between devices: 571 us -> 594 us
  waiting for transfers between devices: 156 us -> 176 us
    psum x10 -> x0, blocking collectives: 740 us -> none  [the longest x6 450 us: residual_dot(): return lax.psum(jnp.sum(residual * precond), ('sx', 'sy'))]
    all_to_all x0 -> x3, blocking collectives: none -> 74.1 us  [global_sums(): gathered = lax.all_to_all(packed, ('sx', 'sy'), 0, 0, tiled=True)]
    all_to_all x0 -> x3, starting transfers between devices: none -> 24.9 us  [global_sums(): gathered = lax.all_to_all(packed, ('sx', 'sy'), 0, 0, tiled=True)]
    all_to_all x0 -> x3, waiting for transfers between devices: none -> 17.3 us  [global_sums(): gathered = lax.all_to_all(packed, ('sx', 'sy'), 0, 0, tiled=True)]
  transfers between devices with their start and end apart: 190 -> 193, of which waited for: 90 -> 95; matrix products, arithmetic and copies ran while one was open for 3% -> 4% of each run, Pallas kernels for 0% -> 0%
where the time goes in v1:
time: 1010 us; the launch traced here: 995 us
  starting transfers between devices  594 us (59%)
  waiting for transfers between devices  176 us (17%)
  local copies, waits for them, and re-layouts  82.7 us (8%)
  blocking collectives  74.1 us (7%)
  other arithmetic  45.6 us (5%)
  between operations  21.6 us (2%)
    ppermute x84, starting transfers between devices, extended(): before = lax.ppermute(last, axis, up)  419 us
    ppermute x84, starting transfers between devices, extended(): after = lax.ppermute(initial, axis, down)  108 us
    ppermute x84, waiting for transfers between devices, extended(): before = lax.ppermute(last, axis, up)  90.6 us
    all_to_all x3, blocking collectives, global_sums(): gathered = lax.all_to_all(packed, ('sx', 'sy'), 0, 0, tiled=True)  74.1 us
    ppermute x22, waiting for transfers between devices, passed_along(): lax.ppermute(value, axis, [(source, source + steps) for source in range(i...  67.5 us
    ppermute x22, starting transfers between devices, passed_along(): lax.ppermute(value, axis, [(source, source + steps) for source in range(i...  42.1 us
    reshape x6, local copies, waits for them, and re-layouts, restrict(): volume.reshape(volume.shape[0] // 2, 2, volume.shape[1] // 2, 2, volume.s...  34.2 us
    all_to_all x3, starting transfers between devices, global_sums(): gathered = lax.all_to_all(packed, ('sx', 'sy'), 0, 0, tiled=True)  24.9 us
  transfers between devices with their start and end apart: 193, of which 95 were waited for; matrix products, arithmetic and copies ran while one was open for 4% of the time, Pallas kernels for 0%

profile of v1, /device:TPU:6, one launch (start us, length us, event | category | flops | bytes accessed | tf_op | source)
XLA Modules:
  0.0 995.0 jit_solution(14880431190072558812)
XLA Ops:
  4.2 6.4 reshape.83
  39.4 5.6 reshape.85
  83.7 5.6 reshape.86
  111.7 148.0 %while.36 = (s32[]{:T(128)}, f32[2,8,128]{2,1,0:T(8,128)S(1)}, pred[]{:T(512)}, f32[2,8,128]{2,1,0:T(8,128)S(1)}, f32[2,8,128]{2,1,0:T(8,128)S(1)}, /*index=5*/f...) while((s32[]{:T(128)}, f32[2,8,128]{2,1,0:T(8,128)S(1)}, ...), condition=%wide.region_5.6_spmd, body=%wide.region_4.5_spmd.sunk | while | flops 232386 | bytes 369318 | solution.py:274
  113.0 6.0 collective-permute-start.1
  134.0 6.0 collective-permute-start.1
  155.2 6.0 collective-permute-start.1
  176.5 5.8 collective-permute-start.1
  197.4 6.0 collective-permute-start.1
  218.6 6.0 collective-permute-start.1
  239.9 6.0 collective-permute-start.1
  267.8 6.0 collective-permute-start.32
  284.3 6.0 collective-permute-start.36
  301.6 27.8 %all_to_all.36 = f32[32,1,2]{2,1,0:T(1,128)S(1)} all-to-all(f32[32,1,2]{2,1,0:T(1,128)S(1)} %broadcast_in_dim.130), channel_id=1, replica_groups=mesh['tm'=8,'sx'=8,'sy'=4] {'sx','sy'}, dimensions={0} | all-to-all | bytes 512 | tf_op jit(solution)/shard_map/all_to_all | solution.py:138
  348.7 8.8 all-to-all-start.1
  357.6 9.7 all-to-all-done.1
  394.8 7.2 all-to-all-start.2
  455.5 5.6 reshape.90
  463.7 142.4 %while.37 = (s32[]{:T(128)}, f32[2,8,128]{2,1,0:T(8,128)S(1)}, pred[]{:T(512)}, f32[2,8,128]{2,1,0:T(8,128)S(1)}, f32[2,8,128]{2,1,0:T(8,128)S(1)}, /*index=5*/f...) while((s32[]{:T(128)}, f32[2,8,128]{2,1,0:T(8,128)S(1)}, ...), condition=%wide.region_17.18_spmd, body=%wide.region_16.17_spmd.sunk | while | flops 234434 | bytes 377518 | solution.py:274
  565.0 6.0 collective-permute-start.6
  586.2 6.0 collective-permute-start.6
  607.5 6.0 collective-permute-start.64
  641.4 6.0 collective-permute-start.69
  657.6 6.0 collective-permute-start.73
  674.9 27.8 %all_to_all.37 = f32[32,1,2]{2,1,0:T(1,128)S(1)} all-to-all(f32[32,1,2]{2,1,0:T(1,128)S(1)} %broadcast_in_dim.135), channel_id=1, replica_groups=mesh['tm'=8,'sx'=8,'sy'=4] {'sx','sy'}, dimensions={0} | all-to-all | bytes 512 | tf_op jit(solution)/shard_map/all_to_all | solution.py:138
  721.4 18.4 %all_to_all.38 = f32[32,1,2]{2,1,0:T(1,128)S(1)} all-to-all(f32[32,1,2]{2,1,0:T(1,128)S(1)} %broadcast_in_dim.136), channel_id=1, replica_groups=mesh['tm'=8,'sx'=8,'sy'=4] {'sx','sy'}, dimensions={0} | all-to-all | bytes 512 | tf_op jit(solution)/shard_map/all_to_all | solution.py:138
  762.9 8.8 all-to-all-start.5
  820.6 5.6 reshape.93
  828.8 142.7 %while.38 = (s32[]{:T(128)}, f32[2,8,128]{2,1,0:T(8,128)S(1)}, pred[]{:T(512)}, f32[2,8,128]{2,1,0:T(8,128)S(1)}, f32[2,8,128]{2,1,0:T(8,128)S(1)}, /*index=5*/f...) while((s32[]{:T(128)}, f32[2,8,128]{2,1,0:T(8,128)S(1)}, ...), condition=%wide.region_29.30_spmd, body=%wide.region_28.29_spmd.sunk | while | flops 234434 | bytes 377518 | solution.py:274
  930.3 6.0 collective-permute-start.11
  951.6 6.0 collective-permute-start.11
  972.8 6.0 collective-permute-start.97
  (650 shorter events, 732.5 us)
Async XLA Ops:
  33.4 14.1 %collective-permute-start.17 = (f32[4,1,128]{2,1,0:T(1,128)S(1)}, f32[4,1,128]{2,1,0:T(1,128)S(1)}, u32[]{:S(2)}, u32[]{:S(2)}) collective-permute-start(f32[4,1,128]{2,1,0:T(1,128)S(1)} %get-tuple-element.842), channel_id=1, source_target_pairs={{1,0},{2,1},{3,2},{5,4},{6,5},{7,6},{9,8},{10,9},{11,10},{13,12},{... | collective-permute-start | bytes 6152 | tf_op jit(solution)/shard_map/ppermute | solution.py:29
  34.7 12.8 %collective-permute-start.18 = (f32[4,1,128]{2,1,0:T(1,128)S(1)}, f32[4,1,128]{2,1,0:T(1,128)S(1)}, u32[]{:S(2)}, u32[]{:S(2)}) collective-permute-start(f32[4,1,128]{2,1,0:T(1,128)S(1)} %get-tuple-element.841), channel_id=1, source_target_pairs={{0,1},{1,2},{2,3},{4,5},{5,6},{6,7},{8,9},{9,10},{10,11},{12,13},{... | collective-permute-start | bytes 6152 | tf_op jit(solution)/shard_map/ppermute | solution.py:28
  77.5 14.4 %collective-permute-start.27 = (f32[1,8,128]{2,1,0:T(8,128)S(1)}, f32[1,8,128]{2,1,0:T(8,128)S(1)}, u32[]{:S(2)}, u32[]{:S(2)}) collective-permute-start(f32[1,8,128]{2,1,0:T(8,128)S(1)} %get-tuple-element.857), channel_id=1, source_target_pairs={{4,0},{8,4},{12,8},{16,12},{20,16},{24,20},{28,24},{5,1},{9,5},{13... | collective-permute-start | bytes 12296 | tf_op jit(solution)/shard_map/ppermute | solution.py:29
  78.8 13.1 %collective-permute-start.28 = (f32[1,8,128]{2,1,0:T(8,128)S(1)}, f32[1,8,128]{2,1,0:T(8,128)S(1)}, u32[]{:S(2)}, u32[]{:S(2)}) collective-permute-start(f32[1,8,128]{2,1,0:T(8,128)S(1)} %get-tuple-element.856), channel_id=1, source_target_pairs={{0,4},{4,8},{8,12},{12,16},{16,20},{20,24},{24,28},{1,5},{5,9},{9,... | collective-permute-start | bytes 12296 | tf_op jit(solution)/shard_map/ppermute | solution.py:28
  91.9 19.6 %collective-permute-start.29 = (f32[4,1,128]{2,1,0:T(1,128)S(1)}, f32[4,1,128]{2,1,0:T(1,128)S(1)}, u32[]{:S(2)}, u32[]{:S(2)}) collective-permute-start(f32[4,1,128]{2,1,0:T(1,128)S(1)} %get-tuple-element.836), channel_id=1, source_target_pairs={{1,0},{2,1},{3,2},{5,4},{6,5},{7,6},{9,8},{10,9},{11,10},{13,12},{... | collective-permute-start | bytes 6152 | tf_op jit(solution)/shard_map/ppermute | solution.py:29
  93.2 18.4 %collective-permute-start.30 = (f32[4,1,128]{2,1,0:T(1,128)S(1)}, f32[4,1,128]{2,1,0:T(1,128)S(1)}, u32[]{:S(2)}, u32[]{:S(2)}) collective-permute-start(f32[4,1,128]{2,1,0:T(1,128)S(1)} %get-tuple-element.835), channel_id=1, source_target_pairs={{0,1},{1,2},{2,3},{4,5},{5,6},{6,7},{8,9},{9,10},{10,11},{12,13},{... | collective-permute-start | bytes 6152 | tf_op jit(solution)/shard_map/ppermute | solution.py:28
  267.8 7.5 collective-permute-start.32
  284.3 7.5 collective-permute-start.36
  348.7 18.5 %all-to-all-start.1 = ((f32[32,1,2]{2,1,0:T(1,128)}), f32[32,1,2]{2,1,0:T(1,128)S(1)}, u32[]{:S(2)}, u32[]{:S(2)}) async-start(f32[32,1,2]{2,1,0:T(1,128)} %broadcast_in_dim.131), calls=%async_computation.1 | async-start | bytes 32768 | tf_op jit(solution)/shard_map/all_to_all | solution.py:138
  372.9 11.7 %collective-permute-start.43 = (f32[1,16,256]{2,1,0:T(8,128)S(1)}, f32[1,16,256]{2,1,0:T(8,128)S(1)}, u32[]{:S(2)}, u32[]{:S(2)}) collective-permute-start(f32[1,16,256]{2,1,0:T(8,128)S(1)} %get-tuple-element.820), channel_id=1, source_target_pairs={{4,0},{8,4},{12,8},{16,12},{20,16},{24,20},{28,24},{5,1},{9,5},{13... | collective-permute-start | bytes 49160 | tf_op jit(solution)/shard_map/ppermute | solution.py:29
  374.2 10.4 %collective-permute-start.44 = (f32[1,16,256]{2,1,0:T(8,128)S(1)}, f32[1,16,256]{2,1,0:T(8,128)S(1)}, u32[]{:S(2)}, u32[]{:S(2)}) collective-permute-start(f32[1,16,256]{2,1,0:T(8,128)S(1)} %get-tuple-element.819), channel_id=1, source_target_pairs={{0,4},{4,8},{8,12},{12,16},{16,20},{20,24},{24,28},{1,5},{5,9},{9,... | collective-permute-start | bytes 49160 | tf_op jit(solution)/shard_map/ppermute | solution.py:28
  378.8 62.9 %collective-permute-start.59 = (f32[1,8,128]{2,1,0:T(8,128)S(1)}, f32[1,8,128]{2,1,0:T(8,128)S(1)}, u32[]{:S(2)}, u32[]{:S(2)}) collective-permute-start(f32[1,8,128]{2,1,0:T(8,128)S(1)} %get-tuple-element.848), channel_id=1, source_target_pairs={{4,0},{8,4},{12,8},{16,12},{20,16},{24,20},{28,24},{5,1},{9,5},{13... | collective-permute-start | bytes 12296 | tf_op jit(solution)/shard_map/ppermute | solution.py:29
  380.1 61.7 %collective-permute-start.60 = (f32[1,8,128]{2,1,0:T(8,128)S(1)}, f32[1,8,128]{2,1,0:T(8,128)S(1)}, u32[]{:S(2)}, u32[]{:S(2)}) collective-permute-start(f32[1,8,128]{2,1,0:T(8,128)S(1)} %get-tuple-element.847), channel_id=1, source_target_pairs={{0,4},{4,8},{8,12},{12,16},{16,20},{20,24},{24,28},{1,5},{5,9},{9,... | collective-permute-start | bytes 12296 | tf_op jit(solution)/shard_map/ppermute | solution.py:28
  394.8 16.9 %all-to-all-start.2 = ((f32[32,1,2]{2,1,0:T(1,128)}), f32[32,1,2]{2,1,0:T(1,128)S(1)}, u32[]{:S(2)}, u32[]{:S(2)}) async-start(f32[32,1,2]{2,1,0:T(1,128)} %broadcast_in_dim.132), calls=%async_computation.2 | async-start | bytes 32768 | tf_op jit(solution)/shard_map/all_to_all | solution.py:138
  402.0 15.7 %collective-permute-start.48 = (f32[1,16,256]{2,1,0:T(8,128)S(1)}, f32[1,16,256]{2,1,0:T(8,128)S(1)}, u32[]{:S(2)}, u32[]{:S(2)}) collective-permute-start(f32[1,16,256]{2,1,0:T(8,128)S(1)} %get-tuple-element.828), channel_id=1, source_target_pairs={{4,0},{8,4},{12,8},{16,12},{20,16},{24,20},{28,24},{5,1},{9,5},{13... | collective-permute-start | bytes 49160 | tf_op jit(solution)/shard_map/ppermute | solution.py:29
  403.3 19.0 %collective-permute-start.50 = (f32[1,16,256]{2,1,0:T(8,128)S(1)}, f32[1,16,256]{2,1,0:T(8,128)S(1)}, u32[]{:S(2)}, u32[]{:S(2)}) collective-permute-start(f32[1,16,256]{2,1,0:T(8,128)S(1)} %get-tuple-element.827), channel_id=1, source_target_pairs={{0,4},{4,8},{8,12},{12,16},{16,20},{20,24},{24,28},{1,5},{5,9},{9,... | collective-permute-start | bytes 49160 | tf_op jit(solution)/shard_map/ppermute | solution.py:28
  417.7 10.5 %collective-permute-start.49 = (f32[1,16,256]{2,1,0:T(8,128)S(1)}, f32[1,16,256]{2,1,0:T(8,128)S(1)}, u32[]{:S(2)}, u32[]{:S(2)}) collective-permute-start(f32[1,16,256]{2,1,0:T(8,128)S(1)} %get-tuple-element.817), channel_id=1, source_target_pairs={{0,4},{4,8},{8,12},{12,16},{16,20},{20,24},{24,28},{1,5},{5,9},{9,... | collective-permute-start | bytes 49160 | tf_op jit(solution)/shard_map/ppermute | solution.py:28
  423.6 10.5 %collective-permute-start.54 = (f32[6,1,256]{2,1,0:T(1,128)S(1)}, f32[6,1,256]{2,1,0:T(1,128)S(1)}, u32[]{:S(2)}, u32[]{:S(2)}) collective-permute-start(f32[6,1,256]{2,1,0:T(1,128)S(1)} %get-tuple-element.799), channel_id=1, source_target_pairs={{0,1},{1,2},{2,3},{4,5},{5,6},{6,7},{8,9},{9,10},{10,11},{12,13},{... | collective-permute-start | bytes 18440 | tf_op jit(solution)/shard_map/ppermute | solution.py:28
  435.8 12.0 %collective-permute-start.55 = (f32[1,16,256]{2,1,0:T(8,128)S(1)}, f32[1,16,256]{2,1,0:T(8,128)S(1)}, u32[]{:S(2)}, u32[]{:S(2)}) collective-permute-start(f32[1,16,256]{2,1,0:T(8,128)S(1)} %get-tuple-element.816), channel_id=1, source_target_pairs={{4,0},{8,4},{12,8},{16,12},{20,16},{24,20},{28,24},{5,1},{9,5},{13... | collective-permute-start | bytes 49160 | tf_op jit(solution)/shard_map/ppermute | solution.py:29
  437.1 10.7 %collective-permute-start.56 = (f32[1,16,256]{2,1,0:T(8,128)S(1)}, f32[1,16,256]{2,1,0:T(8,128)S(1)}, u32[]{:S(2)}, u32[]{:S(2)}) collective-permute-start(f32[1,16,256]{2,1,0:T(8,128)S(1)} %get-tuple-element.815), channel_id=1, source_target_pairs={{0,4},{4,8},{8,12},{12,16},{16,20},{20,24},{24,28},{1,5},{5,9},{9,... | collective-permute-start | bytes 49160 | tf_op jit(solution)/shard_map/ppermute | solution.py:28
  441.7 12.2 %collective-permute-start.61 = (f32[4,1,128]{2,1,0:T(1,128)S(1)}, f32[4,1,128]{2,1,0:T(1,128)S(1)}, u32[]{:S(2)}, u32[]{:S(2)}) collective-permute-start(f32[4,1,128]{2,1,0:T(1,128)S(1)} %get-tuple-element.834), channel_id=1, source_target_pairs={{1,0},{2,1},{3,2},{5,4},{6,5},{7,6},{9,8},{10,9},{11,10},{13,12},{... | collective-permute-start | bytes 6152 | tf_op jit(solution)/shard_map/ppermute | solution.py:29
  443.0 11.0 %collective-permute-start.62 = (f32[4,1,128]{2,1,0:T(1,128)S(1)}, f32[4,1,128]{2,1,0:T(1,128)S(1)}, u32[]{:S(2)}, u32[]{:S(2)}) collective-permute-start(f32[4,1,128]{2,1,0:T(1,128)S(1)} %get-tuple-element.833), channel_id=1, source_target_pairs={{0,1},{1,2},{2,3},{4,5},{5,6},{6,7},{8,9},{9,10},{10,11},{12,13},{... | collective-permute-start | bytes 6152 | tf_op jit(solution)/shard_map/ppermute | solution.py:28
  614.8 12.8 %collective-permute-start.65 = (f32[4,1,128]{2,1,0:T(1,128)S(1)}, f32[4,1,128]{2,1,0:T(1,128)S(1)}, u32[]{:S(2)}, u32[]{:S(2)}) collective-permute-start(f32[4,1,128]{2,1,0:T(1,128)S(1)} %get-tuple-element.832), channel_id=1, source_target_pairs={{1,0},{2,1},{3,2},{5,4},{6,5},{7,6},{9,8},{10,9},{11,10},{13,12},{... | collective-permute-start | bytes 6152 | tf_op jit(solution)/shard_map/ppermute | solution.py:29
  616.1 11.5 %collective-permute-start.66 = (f32[4,1,128]{2,1,0:T(1,128)S(1)}, f32[4,1,128]{2,1,0:T(1,128)S(1)}, u32[]{:S(2)}, u32[]{:S(2)}) collective-permute-start(f32[4,1,128]{2,1,0:T(1,128)S(1)} %get-tuple-element.831), channel_id=1, source_target_pairs={{0,1},{1,2},{2,3},{4,5},{5,6},{6,7},{8,9},{9,10},{10,11},{12,13},{... | collective-permute-start | bytes 6152 | tf_op jit(solution)/shard_map/ppermute | solution.py:28
  641.4 7.5 collective-permute-start.69
  762.9 18.5 %all-to-all-start.5 = ((f32[32,1,2]{2,1,0:T(1,128)}), f32[32,1,2]{2,1,0:T(1,128)S(1)}, u32[]{:S(2)}, u32[]{:S(2)}) async-start(f32[32,1,2]{2,1,0:T(1,128)} %broadcast_in_dim.137), calls=%async_computation.5 | async-start | bytes 32768 | tf_op jit(solution)/shard_map/all_to_all | solution.py:138
  771.7 20.1 %collective-permute-start.85 = (f32[1,16,256]{2,1,0:T(8,128)S(1)}, f32[1,16,256]{2,1,0:T(8,128)S(1)}, u32[]{:S(2)}, u32[]{:S(2)}) collective-permute-start(f32[1,16,256]{2,1,0:T(8,128)S(1)} %get-tuple-element.814), channel_id=1, source_target_pairs={{4,0},{8,4},{12,8},{16,12},{20,16},{24,20},{28,24},{5,1},{9,5},{13... | collective-permute-start | bytes 49160 | tf_op jit(solution)/shard_map/ppermute | solution.py:29
  773.0 18.8 %collective-permute-start.87 = (f32[1,16,256]{2,1,0:T(8,128)S(1)}, f32[1,16,256]{2,1,0:T(8,128)S(1)}, u32[]{:S(2)}, u32[]{:S(2)}) collective-permute-start(f32[1,16,256]{2,1,0:T(8,128)S(1)} %get-tuple-element.813), channel_id=1, source_target_pairs={{0,4},{4,8},{8,12},{12,16},{16,20},{20,24},{24,28},{1,5},{5,9},{9,... | collective-permute-start | bytes 49160 | tf_op jit(solution)/shard_map/ppermute | solution.py:28
  786.0 11.8 %collective-permute-start.84 = (f32[1,16,256]{2,1,0:T(8,128)S(1)}, f32[1,16,256]{2,1,0:T(8,128)S(1)}, u32[]{:S(2)}, u32[]{:S(2)}) collective-permute-start(f32[1,16,256]{2,1,0:T(8,128)S(1)} %get-tuple-element.804), channel_id=1, source_target_pairs={{4,0},{8,4},{12,8},{16,12},{20,16},{24,20},{28,24},{5,1},{9,5},{13... | collective-permute-start | bytes 49160 | tf_op jit(solution)/shard_map/ppermute | solution.py:29
  787.3 10.5 %collective-permute-start.86 = (f32[1,16,256]{2,1,0:T(8,128)S(1)}, f32[1,16,256]{2,1,0:T(8,128)S(1)}, u32[]{:S(2)}, u32[]{:S(2)}) collective-permute-start(f32[1,16,256]{2,1,0:T(8,128)S(1)} %get-tuple-element.803), channel_id=1, source_target_pairs={{0,4},{4,8},{8,12},{12,16},{16,20},{20,24},{24,28},{1,5},{5,9},{9,... | collective-permute-start | bytes 49160 | tf_op jit(solution)/shard_map/ppermute | solution.py:28
  791.9 11.8 %collective-permute-start.89 = (f32[6,1,256]{2,1,0:T(1,128)S(1)}, f32[6,1,256]{2,1,0:T(1,128)S(1)}, u32[]{:S(2)}, u32[]{:S(2)}) collective-permute-start(f32[6,1,256]{2,1,0:T(1,128)S(1)} %get-tuple-element.786), channel_id=1, source_target_pairs={{1,0},{2,1},{3,2},{5,4},{6,5},{7,6},{9,8},{10,9},{11,10},{13,12},{... | collective-permute-start | bytes 18440 | tf_op jit(solution)/shard_map/ppermute | solution.py:29
  793.2 10.5 %collective-permute-start.91 = (f32[6,1,256]{2,1,0:T(1,128)S(1)}, f32[6,1,256]{2,1,0:T(1,128)S(1)}, u32[]{:S(2)}, u32[]{:S(2)}) collective-permute-start(f32[6,1,256]{2,1,0:T(1,128)S(1)} %get-tuple-element.785), channel_id=1, source_target_pairs={{0,1},{1,2},{2,3},{4,5},{5,6},{6,7},{8,9},{9,10},{10,11},{12,13},{... | collective-permute-start | bytes 18440 | tf_op jit(solution)/shard_map/ppermute | solution.py:28
  (166 other events, 1125.3 us)

commit v2 on v1

--- a/solution.py
+++ b/solution.py
@@ -206,52 +206,82 @@
     return (saturation, pressure)
 
 
+def gather_grid(blocks):
+    rows, cols = (lax.axis_size("sx"), lax.axis_size("sy"))
+    packed = jnp.broadcast_to(blocks[None], (rows * cols,) + blocks.shape)
+    gathered = lax.all_to_all(packed, ("sx", "sy"), 0, 0, tiled=True)
+    fields, depth_x, depth_y, depth_z = blocks.shape
+    gathered = gathered.reshape(rows, cols, fields, depth_x, depth_y, depth_z)
+    gathered = gathered.transpose(2, 0, 3, 1, 4, 5)
+    return gathered.reshape(fields, rows * depth_x, cols * depth_y, depth_z)
+
+
+def own_block(whole, shape):
+    corner = (lax.axis_index("sx") * shape[0], lax.axis_index("sy") * shape[1], 0)
+    return lax.dynamic_slice(whole, corner, shape)
+
+
+def whole_faces(volume):
+    return face_list(jnp.pad(volume, 1))
+
+
 def local(
     initial_saturation, permeability, porosity, source_rate, rock_type, water_endpoint, oil_endpoint
 ):
     slices = lax.axis_size("tm")
     slice_index = lax.axis_index("tm")
-    water_coarse = lookup(rock_type, water_endpoint)
-    oil_coarse = lookup(rock_type, oil_endpoint)
-    water_fine = prolong(water_coarse)
-    oil_fine = prolong(oil_coarse)
-    start_coarse = restrict(initial_saturation)
-    permeability_upscaled = restrict(permeability)
-    poro_coarse = restrict(porosity)
-    source_coarse = restrict(source_rate)
+    water_block = lookup(rock_type, water_endpoint)
+    oil_block = lookup(rock_type, oil_endpoint)
+    water_fine = prolong(water_block)
+    oil_fine = prolong(oil_block)
+    start_block = restrict(initial_saturation)
+    block_shape = start_block.shape
+    whole = gather_grid(
+        jnp.stack(
+            [
+                start_block,
+                restrict(permeability),
+                restrict(porosity),
+                restrict(source_rate),
+                water_block,
+                oil_block,
+            ]
+        )
+    )
+    start_coarse, permeability_upscaled, poro_coarse, source_coarse, water_coarse, oil_coarse = (
+        whole[k] for k in range(6)
+    )
     water_mobility, oil_mobility = mobilities(start_coarse, water_coarse, oil_coarse)
     transport_field_upscaled = permeability_upscaled * (water_mobility + oil_mobility)
     transmissibility_upscaled = [
         (transport_field_upscaled + exceeding_part) / 8.0
-        for exceeding_part in build_face_tables(transport_field_upscaled)
+        for exceeding_part in whole_faces(transport_field_upscaled)
     ]
     diag_coarse = compress + accumulate_terms(transmissibility_upscaled)
     pressure_coarse = damping * source_coarse / diag_coarse
-    for sweep_no in range(SWEEPS):
-        beside = build_face_tables(pressure_coarse)
-        if sweep_no + 1 < SWEEPS:
-            coupled = accumulate_terms(
-                [
-                    conduct_face * exceeding_part
-                    for conduct_face, exceeding_part in zip(transmissibility_upscaled, beside)
-                ]
-            )
-            pressure_coarse = (
-                pressure_coarse
-                + damping
-                * (source_coarse - (diag_coarse * pressure_coarse - coupled))
-                / diag_coarse
-            )
+    for sweep_no in range(SWEEPS - 1):
+        coupled = accumulate_terms(
+            [
+                conduct_face * exceeding_part
+                for conduct_face, exceeding_part in zip(
+                    transmissibility_upscaled, whole_faces(pressure_coarse)
+                )
+            ]
+        )
+        pressure_coarse = (
+            pressure_coarse
+            + damping * (source_coarse - (diag_coarse * pressure_coarse - coupled)) / diag_coarse
+        )
     flows_coarse = [
         conduct_face * (pressure_coarse - exceeding_part)
-        for conduct_face, exceeding_part in zip(transmissibility_upscaled, beside)
+        for conduct_face, exceeding_part in zip(transmissibility_upscaled, whole_faces(pressure_coarse))
     ]
     outgoing_coarse = accumulate_terms([jnp.maximum(outward, 0.0) for outward in flows_coarse])
     coarse_dt = FSTEPS * step_dt
 
     def coarse_step(coarse_state):
         frac, frac_slope = fractional(coarse_state, water_coarse, oil_coarse)
-        flux_sum = upwind(frac, coarse_faces(frac), flows_coarse)
+        flux_sum = upwind(frac, whole_faces(frac), flows_coarse)
         balance = (
             flux_sum - jnp.maximum(source_coarse, 0.0) - jnp.minimum(source_coarse, 0.0) * frac
         )
@@ -275,7 +305,9 @@
         return (coarse_state, coarse_step(coarse_state))
 
     coarse_state, coarse_image = chain(None)
-    starts = jnp.where(slice_index == 0, initial_saturation, prolong(coarse_state))
+    starts = jnp.where(
+        slice_index == 0, initial_saturation, prolong(own_block(coarse_state, block_shape))
+    )
     previous_image = coarse_image
     ends = starts
     pressure = starts
@@ -285,9 +317,13 @@
             saturation, permeability, porosity, source_rate, water_fine, oil_fine
         )
         pressure = fine_pressure
-        corrections = restrict(saturation) - previous_image
+        corrections = gather_grid(restrict(saturation)[None])[0] - previous_image
         coarse_state, coarse_image = chain(corrections)
-        ends = prolong(coarse_image) + saturation - prolong(previous_image)
+        ends = (
+            prolong(own_block(coarse_image, block_shape))
+            + saturation
+            - prolong(own_block(previous_image, block_shape))
+        )
         if parareal_no + 1 < PARAREAL:
             arrived_start = passed_along(ends, "tm", 1)
             starts = jnp.where(slice_index == 0, initial_saturation, arrived_start)

time: 1010 us -> 882 us (0.87)
  starting transfers between devices: 594 us -> 264 us
  other arithmetic: 45.6 us -> 196 us
  waiting for transfers between devices: 176 us -> 208 us
  local copies, waits for them, and re-layouts: 82.7 us -> 102 us
    ppermute x84 -> x28, starting transfers between devices: 419 us -> 130 us  [extended(): before = lax.ppermute(last, axis, up)]
    ppermute x84 -> x28, starting transfers between devices: 108 us -> 36.1 us  [extended(): after = lax.ppermute(initial, axis, down)]
    ppermute x84 -> x28, waiting for transfers between devices: 90.6 us -> 24 us  [extended(): before = lax.ppermute(last, axis, up)]
    ppermute x22, waiting for transfers between devices: 67.5 us -> 131 us  [passed_along(): lax.ppermute(value, axis, [(source, source + steps) for source in range(i...]
    all_to_all x0 -> x3, waiting for transfers between devices: none -> 44.7 us  [gather_grid(): gathered = lax.all_to_all(packed, ('sx', 'sy'), 0, 0, tiled=True)]
    all_to_all x0 -> x3, starting transfers between devices: none -> 38.5 us  [gather_grid(): gathered = lax.all_to_all(packed, ('sx', 'sy'), 0, 0, tiled=True)]
    select_n x21, other arithmetic: 0.08 us -> 35.5 us  [relay_round(): return jnp.where(slice_index == 0, start_coarse, arrived)]
    add x14, other arithmetic: 1.23 us -> 33.6 us  [relay_round(): outgoing_state = coarse_image + corrections]
  transfers between devices with their start and end apart: 193 -> 83, of which waited for: 95 -> 47; matrix products, arithmetic and copies ran while one was open for 4% -> 4% of each run, Pallas kernels for 0% -> 0%
where the time goes in v2:
time: 882 us; the launch traced here: 869 us
  starting transfers between devices  264 us (30%)
  waiting for transfers between devices  208 us (24%)
  other arithmetic  196 us (22%)
  local copies, waits for them, and re-layouts  102 us (12%)
  blocking collectives  78.9 us (9%)
  between operations  20.9 us (2%)
    ppermute x22, waiting for transfers between devices, passed_along(): lax.ppermute(value, axis, [(source, source + steps) for source in range(i...  131 us
    ppermute x28, starting transfers between devices, extended(): before = lax.ppermute(last, axis, up)  130 us
    all_to_all x4, blocking collectives, global_sums(): gathered = lax.all_to_all(packed, ('sx', 'sy'), 0, 0, tiled=True)  78.9 us
    all_to_all x3, waiting for transfers between devices, gather_grid(): gathered = lax.all_to_all(packed, ('sx', 'sy'), 0, 0, tiled=True)  44.7 us
    ppermute x22, starting transfers between devices, passed_along(): lax.ppermute(value, axis, [(source, source + steps) for source in range(i...  42 us
    all_to_all x3, starting transfers between devices, gather_grid(): gathered = lax.all_to_all(packed, ('sx', 'sy'), 0, 0, tiled=True)  38.5 us
    ppermute x28, starting transfers between devices, extended(): after = lax.ppermute(initial, axis, down)  36.1 us
    reshape x6, local copies, waits for them, and re-layouts, restrict(): volume.reshape(volume.shape[0] // 2, 2, volume.shape[1] // 2, 2, volume.s...  35.6 us
  transfers between devices with their start and end apart: 83, of which 47 were waited for; matrix products, arithmetic and copies ran while one was open for 4% of the time, Pallas kernels for 0%

profile of v2, /device:TPU:6, one launch (start us, length us, event | category | flops | bytes accessed | tf_op | source)
XLA Modules:
  0.0 869.5 jit_solution(3009480483108795628)
XLA Ops:
  2.1 6.3 reshape.152
  42.6 11.7 %all-to-all-start = ((f32[32,6,2,8,128]{4,3,2,1,0:T(8,128)}), f32[32,6,2,8,128]{4,3,2,1,0:T(8,128)S(1)}, u32[]{:S(2)}, u32[]{:S(2)}) async-start(f32[32,6,2,8,128]{4,3,2,1,0:T(8,128)} %broadcast_in_dim.143), calls=%async_computation | async-start | bytes 3145728 | tf_op jit(solution)/shard_map/all_to_all | solution.py:212
  68.6 24.8 %all-to-all-done = f32[32,6,2,8,128]{4,3,2,1,0:T(8,128)S(1)} async-done(((f32[32,6,2,8,128]{4,3,2,1,0:T(8,128)}), f32[32,6,2,8,128]{4,3,2,1,0:T(8,128)S(1)}, u32[]{:S(2)}, u32[]{:S(2)}) %all-to-all-start) | async-done | bytes 1572896 | tf_op jit(solution)/shard_map/all_to_all | solution.py:212
  97.0 91.3 %while.36 = (s32[]{:T(128)}, f32[16,32,128]{2,1,0:T(8,128)}, pred[]{:T(512)}, f32[16,32,128]{2,1,0:T(8,128)S(1)}, f32[16,32,128]{2,1,0:T(8,128)S(1)}, /*index=5*...) while((s32[]{:T(128)}, f32[16,32,128]{2,1,0:T(8,128)}, ...), condition=%wide.region_5.6_spmd, body=%wide.region_4.5_spmd.sunk | while | flops 4849666 | bytes 6815942 | solution.py:304
  102.3 6.1 collective-permute-done
  115.3 6.1 collective-permute-done
  128.4 6.1 collective-permute-done
  141.4 6.1 collective-permute-done
  154.5 6.1 collective-permute-done
  167.5 6.1 collective-permute-done
  180.6 6.1 collective-permute-done
  232.9 19.7 %all_to_all.51 = f32[32,1,2]{2,1,0:T(1,128)} all-to-all(f32[32,1,2]{2,1,0:T(1,128)S(1)} %broadcast_in_dim.147), channel_id=1, replica_groups=mesh['tm'=8,'sx'=8,'sy'=4] {'sx','sy'}, dimensions={0} | all-to-all | bytes 512 | tf_op jit(solution)/shard_map/all_to_all | solution.py:138
  275.8 18.5 %all_to_all.52 = f32[32,1,2]{2,1,0:T(1,128)} all-to-all(f32[32,1,2]{2,1,0:T(1,128)S(1)} %broadcast_in_dim.148), channel_id=1, replica_groups=mesh['tm'=8,'sx'=8,'sy'=4] {'sx','sy'}, dimensions={0} | all-to-all | bytes 512 | tf_op jit(solution)/shard_map/all_to_all | solution.py:138
  321.2 8.9 %all-to-all-start.3 = ((f32[32,1,2]{2,1,0:T(1,128)}), f32[32,1,2]{2,1,0:T(1,128)}, u32[]{:S(2)}, u32[]{:S(2)}) async-start(f32[32,1,2]{2,1,0:T(1,128)} %broadcast_in_dim.149), calls=%async_computation.3 | async-start | bytes 32768 | tf_op jit(solution)/shard_map/all_to_all | solution.py:138
  385.4 6.3 reshape.160
  395.0 13.4 %all-to-all-start.4 = ((f32[32,1,2,8,128]{4,3,2,1,0:T(8,128)}), f32[32,1,2,8,128]{4,3,2,1,0:T(8,128)}, u32[]{:S(2)}, u32[]{:S(2)}) async-start(f32[32,1,2,8,128]{4,3,2,1,0:T(8,128)} %broadcast_in_dim.150), calls=%async_computation.4 | async-start | bytes 524288 | tf_op jit(solution)/shard_map/all_to_all | solution.py:212
  410.8 9.1 %all-to-all-done.4 = f32[32,1,2,8,128]{4,3,2,1,0:T(8,128)} async-done(((f32[32,1,2,8,128]{4,3,2,1,0:T(8,128)}), f32[32,1,2,8,128]{4,3,2,1,0:T(8,128)}, u32[]{:S(2)}, u32[]{:S(2)}) %all-to-all-start.4) | async-done | bytes 262176 | tf_op jit(solution)/shard_map/all_to_all | solution.py:212
  424.2 91.9 %while.37 = (s32[]{:T(128)}, f32[16,32,128]{2,1,0:T(8,128)}, pred[]{:T(512)}, f32[16,32,128]{2,1,0:T(8,128)S(1)}, f32[16,32,128]{2,1,0:T(8,128)S(1)}, /*index=5*...) while((s32[]{:T(128)}, f32[16,32,128]{2,1,0:T(8,128)}, ...), condition=%wide.region_17.18_spmd, body=%wide.region_16.17_spmd.sunk | while | flops 4915202 | bytes 7078094 | solution.py:304
  429.6 6.1 collective-permute-done.1
  442.7 6.1 collective-permute-done.1
  455.8 6.1 collective-permute-done.1
  469.0 6.1 collective-permute-done.1
  482.1 6.1 collective-permute-done.1
  495.2 6.1 collective-permute-done.1
  575.2 21.8 %all_to_all.53 = f32[32,1,2]{2,1,0:T(1,128)} all-to-all(f32[32,1,2]{2,1,0:T(1,128)S(1)} %broadcast_in_dim.153), channel_id=1, replica_groups=mesh['tm'=8,'sx'=8,'sy'=4] {'sx','sy'}, dimensions={0} | all-to-all | bytes 512 | tf_op jit(solution)/shard_map/all_to_all | solution.py:138
  620.3 18.9 %all_to_all.54 = f32[32,1,2]{2,1,0:T(1,128)} all-to-all(f32[32,1,2]{2,1,0:T(1,128)S(1)} %broadcast_in_dim.154), channel_id=1, replica_groups=mesh['tm'=8,'sx'=8,'sy'=4] {'sx','sy'}, dimensions={0} | all-to-all | bytes 512 | tf_op jit(solution)/shard_map/all_to_all | solution.py:138
  666.3 8.7 %all-to-all-start.7 = ((f32[32,1,2]{2,1,0:T(1,128)}), f32[32,1,2]{2,1,0:T(1,128)}, u32[]{:S(2)}, u32[]{:S(2)}) async-start(f32[32,1,2]{2,1,0:T(1,128)} %broadcast_in_dim.155), calls=%async_computation.7 | async-start | bytes 32768 | tf_op jit(solution)/shard_map/all_to_all | solution.py:138
  730.4 6.3 reshape.164
  740.0 13.4 %all-to-all-start.8 = ((f32[32,1,2,8,128]{4,3,2,1,0:T(8,128)}), f32[32,1,2,8,128]{4,3,2,1,0:T(8,128)}, u32[]{:S(2)}, u32[]{:S(2)}) async-start(f32[32,1,2,8,128]{4,3,2,1,0:T(8,128)} %broadcast_in_dim.156), calls=%async_computation.8 | async-start | bytes 524288 | tf_op jit(solution)/shard_map/all_to_all | solution.py:212
  754.1 10.8 %all-to-all-done.8 = f32[32,1,2,8,128]{4,3,2,1,0:T(8,128)} async-done(((f32[32,1,2,8,128]{4,3,2,1,0:T(8,128)}), f32[32,1,2,8,128]{4,3,2,1,0:T(8,128)}, u32[]{:S(2)}, u32[]{:S(2)}) %all-to-all-start.8) | async-done | bytes 262176 | tf_op jit(solution)/shard_map/all_to_all | solution.py:212
  767.6 91.8 %while.38 = (s32[]{:T(128)}, f32[16,32,128]{2,1,0:T(8,128)}, pred[]{:T(512)}, f32[16,32,128]{2,1,0:T(8,128)S(1)}, f32[16,32,128]{2,1,0:T(8,128)S(1)}, /*index=5*...) while((s32[]{:T(128)}, f32[16,32,128]{2,1,0:T(8,128)}, ...), condition=%wide.region_29.30_spmd, body=%wide.region_28.29_spmd.sunk | while | flops 4915202 | bytes 7078094 | solution.py:304
  786.1 6.1 collective-permute-done.2
  (415 shorter events, 564.5 us)
Async XLA Ops:
  42.6 50.8 %all-to-all-start = ((f32[32,6,2,8,128]{4,3,2,1,0:T(8,128)}), f32[32,6,2,8,128]{4,3,2,1,0:T(8,128)S(1)}, u32[]{:S(2)}, u32[]{:S(2)}) async-start(f32[32,6,2,8,128]{4,3,2,1,0:T(8,128)} %broadcast_in_dim.143), calls=%async_computation | async-start | bytes 3145728 | tf_op jit(solution)/shard_map/all_to_all | solution.py:212
  100.4 8.0 collective-permute-start
  113.4 8.0 collective-permute-start
  126.5 8.0 collective-permute-start
  139.5 8.0 collective-permute-start
  152.6 8.0 collective-permute-start
  165.6 8.0 collective-permute-start
  178.7 8.0 collective-permute-start
  321.2 18.5 %all-to-all-start.3 = ((f32[32,1,2]{2,1,0:T(1,128)}), f32[32,1,2]{2,1,0:T(1,128)}, u32[]{:S(2)}, u32[]{:S(2)}) async-start(f32[32,1,2]{2,1,0:T(1,128)} %broadcast_in_dim.149), calls=%async_computation.3 | async-start | bytes 32768 | tf_op jit(solution)/shard_map/all_to_all | solution.py:138
  331.5 21.2 %collective-permute-start.20 = (f32[1,16,256]{2,1,0:T(8,128)}, f32[1,16,256]{2,1,0:T(8,128)}, u32[]{:S(2)}, u32[]{:S(2)}) collective-permute-start(f32[1,16,256]{2,1,0:T(8,128)} %get-tuple-element.840), channel_id=1, source_target_pairs={{4,0},{8,4},{12,8},{16,12},{20,16},{24,20},{28,24},{5,1},{9,5},{13... | collective-permute-start | bytes 49160 | tf_op jit(solution)/shard_map/ppermute | solution.py:29
  332.8 19.9 %collective-permute-start.22 = (f32[1,16,256]{2,1,0:T(8,128)}, f32[1,16,256]{2,1,0:T(8,128)}, u32[]{:S(2)}, u32[]{:S(2)}) collective-permute-start(f32[1,16,256]{2,1,0:T(8,128)} %get-tuple-element.839), channel_id=1, source_target_pairs={{0,4},{4,8},{8,12},{12,16},{16,20},{20,24},{24,28},{1,5},{5,9},{9,... | collective-permute-start | bytes 49160 | tf_op jit(solution)/shard_map/ppermute | solution.py:28
  346.8 12.8 %collective-permute-start.19 = (f32[1,16,256]{2,1,0:T(8,128)S(1)}, f32[1,16,256]{2,1,0:T(8,128)S(1)}, u32[]{:S(2)}, u32[]{:S(2)}) collective-permute-start(f32[1,16,256]{2,1,0:T(8,128)S(1)} %get-tuple-element.830), channel_id=1, source_target_pairs={{4,0},{8,4},{12,8},{16,12},{20,16},{24,20},{28,24},{5,1},{9,5},{13... | collective-permute-start | bytes 49160 | tf_op jit(solution)/shard_map/ppermute | solution.py:29
  348.1 11.5 %collective-permute-start.21 = (f32[1,16,256]{2,1,0:T(8,128)S(1)}, f32[1,16,256]{2,1,0:T(8,128)S(1)}, u32[]{:S(2)}, u32[]{:S(2)}) collective-permute-start(f32[1,16,256]{2,1,0:T(8,128)S(1)} %get-tuple-element.829), channel_id=1, source_target_pairs={{0,4},{4,8},{8,12},{12,16},{16,20},{20,24},{24,28},{1,5},{5,9},{9,... | collective-permute-start | bytes 49160 | tf_op jit(solution)/shard_map/ppermute | solution.py:28
  353.5 12.0 %collective-permute-start.24 = (f32[6,1,256]{2,1,0:T(1,128)S(1)}, f32[6,1,256]{2,1,0:T(1,128)S(1)}, u32[]{:S(2)}, u32[]{:S(2)}) collective-permute-start(f32[6,1,256]{2,1,0:T(1,128)S(1)} %get-tuple-element.812), channel_id=1, source_target_pairs={{1,0},{2,1},{3,2},{5,4},{6,5},{7,6},{9,8},{10,9},{11,10},{13,12},{... | collective-permute-start | bytes 18440 | tf_op jit(solution)/shard_map/ppermute | solution.py:29
  354.8 10.7 %collective-permute-start.26 = (f32[6,1,256]{2,1,0:T(1,128)S(1)}, f32[6,1,256]{2,1,0:T(1,128)S(1)}, u32[]{:S(2)}, u32[]{:S(2)}) collective-permute-start(f32[6,1,256]{2,1,0:T(1,128)S(1)} %get-tuple-element.811), channel_id=1, source_target_pairs={{0,1},{1,2},{2,3},{4,5},{5,6},{6,7},{8,9},{9,10},{10,11},{12,13},{... | collective-permute-start | bytes 18440 | tf_op jit(solution)/shard_map/ppermute | solution.py:28
  395.0 24.9 %all-to-all-start.4 = ((f32[32,1,2,8,128]{4,3,2,1,0:T(8,128)}), f32[32,1,2,8,128]{4,3,2,1,0:T(8,128)}, u32[]{:S(2)}, u32[]{:S(2)}) async-start(f32[32,1,2,8,128]{4,3,2,1,0:T(8,128)} %broadcast_in_dim.150), calls=%async_computation.4 | async-start | bytes 524288 | tf_op jit(solution)/shard_map/all_to_all | solution.py:212
  427.7 8.0 collective-permute-start.1
  453.9 8.0 collective-permute-start.1
  467.0 8.0 collective-permute-start.1
  666.3 18.3 %all-to-all-start.7 = ((f32[32,1,2]{2,1,0:T(1,128)}), f32[32,1,2]{2,1,0:T(1,128)}, u32[]{:S(2)}, u32[]{:S(2)}) async-start(f32[32,1,2]{2,1,0:T(1,128)} %broadcast_in_dim.155), calls=%async_computation.7 | async-start | bytes 32768 | tf_op jit(solution)/shard_map/all_to_all | solution.py:138
  676.4 21.3 %collective-permute-start.49 = (f32[1,16,256]{2,1,0:T(8,128)}, f32[1,16,256]{2,1,0:T(8,128)}, u32[]{:S(2)}, u32[]{:S(2)}) collective-permute-start(f32[1,16,256]{2,1,0:T(8,128)} %get-tuple-element.826), channel_id=1, source_target_pairs={{4,0},{8,4},{12,8},{16,12},{20,16},{24,20},{28,24},{5,1},{9,5},{13... | collective-permute-start | bytes 49160 | tf_op jit(solution)/shard_map/ppermute | solution.py:29
  677.7 20.1 %collective-permute-start.51 = (f32[1,16,256]{2,1,0:T(8,128)}, f32[1,16,256]{2,1,0:T(8,128)}, u32[]{:S(2)}, u32[]{:S(2)}) collective-permute-start(f32[1,16,256]{2,1,0:T(8,128)} %get-tuple-element.825), channel_id=1, source_target_pairs={{0,4},{4,8},{8,12},{12,16},{16,20},{20,24},{24,28},{1,5},{5,9},{9,... | collective-permute-start | bytes 49160 | tf_op jit(solution)/shard_map/ppermute | solution.py:28
  691.9 12.6 %collective-permute-start.48 = (f32[1,16,256]{2,1,0:T(8,128)S(1)}, f32[1,16,256]{2,1,0:T(8,128)S(1)}, u32[]{:S(2)}, u32[]{:S(2)}) collective-permute-start(f32[1,16,256]{2,1,0:T(8,128)S(1)} %get-tuple-element.816), channel_id=1, source_target_pairs={{4,0},{8,4},{12,8},{16,12},{20,16},{24,20},{28,24},{5,1},{9,5},{13... | collective-permute-start | bytes 49160 | tf_op jit(solution)/shard_map/ppermute | solution.py:29
  693.2 11.3 %collective-permute-start.50 = (f32[1,16,256]{2,1,0:T(8,128)S(1)}, f32[1,16,256]{2,1,0:T(8,128)S(1)}, u32[]{:S(2)}, u32[]{:S(2)}) collective-permute-start(f32[1,16,256]{2,1,0:T(8,128)S(1)} %get-tuple-element.815), channel_id=1, source_target_pairs={{0,4},{4,8},{8,12},{12,16},{16,20},{20,24},{24,28},{1,5},{5,9},{9,... | collective-permute-start | bytes 49160 | tf_op jit(solution)/shard_map/ppermute | solution.py:28
  698.6 11.8 %collective-permute-start.53 = (f32[6,1,256]{2,1,0:T(1,128)S(1)}, f32[6,1,256]{2,1,0:T(1,128)S(1)}, u32[]{:S(2)}, u32[]{:S(2)}) collective-permute-start(f32[6,1,256]{2,1,0:T(1,128)S(1)} %get-tuple-element.798), channel_id=1, source_target_pairs={{1,0},{2,1},{3,2},{5,4},{6,5},{7,6},{9,8},{10,9},{11,10},{13,12},{... | collective-permute-start | bytes 18440 | tf_op jit(solution)/shard_map/ppermute | solution.py:29
  699.9 10.5 %collective-permute-start.55 = (f32[6,1,256]{2,1,0:T(1,128)S(1)}, f32[6,1,256]{2,1,0:T(1,128)S(1)}, u32[]{:S(2)}, u32[]{:S(2)}) collective-permute-start(f32[6,1,256]{2,1,0:T(1,128)S(1)} %get-tuple-element.797), channel_id=1, source_target_pairs={{0,1},{1,2},{2,3},{4,5},{5,6},{6,7},{8,9},{9,10},{10,11},{12,13},{... | collective-permute-start | bytes 18440 | tf_op jit(solution)/shard_map/ppermute | solution.py:28
  740.0 25.0 %all-to-all-start.8 = ((f32[32,1,2,8,128]{4,3,2,1,0:T(8,128)}), f32[32,1,2,8,128]{4,3,2,1,0:T(8,128)}, u32[]{:S(2)}, u32[]{:S(2)}) async-start(f32[32,1,2,8,128]{4,3,2,1,0:T(8,128)} %broadcast_in_dim.156), calls=%async_computation.8 | async-start | bytes 524288 | tf_op jit(solution)/shard_map/all_to_all | solution.py:212
  771.0 8.0 collective-permute-start.2
  784.2 8.0 collective-permute-start.2
  810.4 8.0 collective-permute-start.2
  823.5 8.0 collective-permute-start.2
  849.8 8.0 collective-permute-start.2
  (79 other events, 743.1 us)

commit v3 on v2

--- a/solution.py
+++ b/solution.py
@@ -75,8 +75,24 @@
     ]
 
 
+ROW_AXES = ("sx", "sy")
+
+
+def row_halo(volume):
+    count = lax.axis_size("sx") * lax.axis_size("sy")
+    up = [(i, i + 1) for i in range(count - 1)]
+    down = [(i + 1, i) for i in range(count - 1)]
+    before = lax.ppermute(volume[-1:], ROW_AXES, up)
+    after = lax.ppermute(volume[:1], ROW_AXES, down)
+    return jnp.concatenate([before, volume, after], axis=0)
+
+
+def row_faces(volume):
+    return face_list(jnp.pad(row_halo(volume), ((0, 0), (1, 1), (1, 1))))
+
+
 def face_mobility_values(volume):
-    return face_list(pad_depth(extended(volume, (("sx", 0), ("sy", 1)), 1)))
+    return row_faces(volume)
 
 
 def direction_spread(volume):
@@ -84,11 +100,11 @@
 
 
 def pressure_faces(volume):
-    return face_list(pad_depth(extended(volume, (("sx", 0), ("sy", 1)), 1)))
+    return row_faces(volume)
 
 
 def flow_faces(volume):
-    return face_list(pad_depth(extended(volume, (("sx", 0), ("sy", 1)), 1)))
+    return row_faces(volume)
 
 
 def build_face_tables(volume):
@@ -141,11 +157,10 @@
 
 
 def apply_operator(diagonal, transmissibility, vector):
-    spread_vec = direction_spread(vector)
     return diagonal * vector - accumulate_terms(
         [
             conduct_face * exceeding_part
-            for conduct_face, exceeding_part in zip(transmissibility, face_list(pad_depth(spread_vec)))
+            for conduct_face, exceeding_part in zip(transmissibility, row_faces(vector))
         ]
     )
 
@@ -221,6 +236,46 @@
     return lax.dynamic_slice(whole, corner, shape)
 
 
+def to_rows(blocks):
+    columns = lax.axis_size("sy")
+    fields, depth_x, depth_y, depth_z = blocks.shape
+    share = depth_x // columns
+    packed = blocks.reshape(fields, columns, share, depth_y, depth_z).transpose(1, 0, 2, 3, 4)
+    got = lax.all_to_all(packed, "sy", 0, 0, tiled=True)
+    return got.transpose(1, 2, 0, 3, 4).reshape(fields, share, columns * depth_y, depth_z)
+
+
+def from_rows(rows):
+    columns = lax.axis_size("sy")
+    fields, share, length_y, depth_z = rows.shape
+    depth_y = length_y // columns
+    packed = rows.reshape(fields, share, columns, depth_y, depth_z).transpose(2, 0, 1, 3, 4)
+    got = lax.all_to_all(packed, "sy", 0, 0, tiled=True)
+    return got.transpose(1, 0, 2, 3, 4).reshape(fields, columns * share, depth_y, depth_z)
+
+
+def row_index():
+    return lax.axis_index("sx") * lax.axis_size("sy") + lax.axis_index("sy")
+
+
+def restrict_rows(rows):
+    share, length_y, depth_z = rows.shape
+    partial = rows.reshape(share, length_y // 2, 2, depth_z // 2, 2).sum(axis=(2, 4))
+    count = lax.axis_size("sx") * lax.axis_size("sy")
+    packed = jnp.broadcast_to(partial[None], (count,) + partial.shape)
+    gathered = lax.all_to_all(packed, ROW_AXES, 0, 0, tiled=True)
+    gathered = gathered.reshape(count * share // 2, 2, length_y // 2, depth_z // 2)
+    return gathered.sum(axis=1) / 8.0
+
+
+def prolong_rows(whole, share):
+    coarse_rows = (row_index() * share + jnp.arange(share)) // 2
+    picked = jnp.take(whole, coarse_rows, axis=0)
+    count, length_y, depth_z = picked.shape
+    spread_out = jnp.broadcast_to(picked[:, :, None, :, None], (count, length_y, 2, depth_z, 2))
+    return spread_out.reshape(count, 2 * length_y, 2 * depth_z)
+
+
 def whole_faces(volume):
     return face_list(jnp.pad(volume, 1))
 
@@ -232,8 +287,6 @@
     slice_index = lax.axis_index("tm")
     water_block = lookup(rock_type, water_endpoint)
     oil_block = lookup(rock_type, oil_endpoint)
-    water_fine = prolong(water_block)
-    oil_fine = prolong(oil_block)
     start_block = restrict(initial_saturation)
     block_shape = start_block.shape
     whole = gather_grid(
@@ -304,10 +357,21 @@
         coarse_state = lax.fori_loop(0, slices - 1, relay_round, start_coarse)
         return (coarse_state, coarse_step(coarse_state))
 
+    initial_rows, permeability, porosity, source_rate, water_fine, oil_fine = to_rows(
+        jnp.stack(
+            [
+                initial_saturation,
+                permeability,
+                porosity,
+                source_rate,
+                prolong(water_block),
+                prolong(oil_block),
+            ]
+        )
+    )
+    share = initial_rows.shape[0]
     coarse_state, coarse_image = chain(None)
-    starts = jnp.where(
-        slice_index == 0, initial_saturation, prolong(own_block(coarse_state, block_shape))
-    )
+    starts = jnp.where(slice_index == 0, initial_rows, prolong_rows(coarse_state, share))
     previous_image = coarse_image
     ends = starts
     pressure = starts
@@ -317,17 +381,14 @@
             saturation, permeability, porosity, source_rate, water_fine, oil_fine
         )
         pressure = fine_pressure
-        corrections = gather_grid(restrict(saturation)[None])[0] - previous_image
+        corrections = restrict_rows(saturation) - previous_image
         coarse_state, coarse_image = chain(corrections)
-        ends = (
-            prolong(own_block(coarse_image, block_shape))
-            + saturation
-            - prolong(own_block(previous_image, block_shape))
-        )
+        ends = prolong_rows(coarse_image, share) + saturation - prolong_rows(previous_image, share)
         if parareal_no + 1 < PARAREAL:
             arrived_start = passed_along(ends, "tm", 1)
-            starts = jnp.where(slice_index == 0, initial_saturation, arrived_start)
+            starts = jnp.where(slice_index == 0, initial_rows, arrived_start)
         previous_image = coarse_image
+    ends, pressure = from_rows(jnp.stack([ends, pressure]))
     return (ends[None], pressure[None])
 
 

time: 882 us -> 836 us (0.948)
  starting transfers between devices: 264 us -> 186 us
  blocking collectives: 78.9 us -> 106 us
  waiting for transfers between devices: 208 us -> 221 us
    ppermute x56 -> x28, starting transfers between devices: 166 us -> 82.6 us  [the longest x14 64.5 us: row_halo(): before = lax.ppermute(volume[-1:], ROW_AXES, up)]
    all_to_all x0 -> x2, starting transfers between devices: none -> 34.6 us  [restrict_rows(): gathered = lax.all_to_all(packed, ROW_AXES, 0, 0, tiled=True)]
    broadcast_in_dim x0 -> x10, local copies, waits for them, and re-layouts: none -> 29.7 us  [the longest x8 27.9 us: prolong_rows(): jnp.broadcast_to(picked[:, :, None, :, None], (count, length_y, 2, depth_...]
    all_to_all x3 -> x1, starting transfers between devices: 38.5 us -> 9.63 us  [gather_grid(): gathered = lax.all_to_all(packed, ('sx', 'sy'), 0, 0, tiled=True)]
    all_to_all x0 -> x2, waiting for transfers between devices: none -> 24.5 us  [restrict_rows(): gathered = lax.all_to_all(packed, ROW_AXES, 0, 0, tiled=True)]
    all_to_all x0 -> x2, blocking collectives: none -> 21.5 us  [the longest x1 12.3 us: to_rows(): got = lax.all_to_all(packed, 'sy', 0, 0, tiled=True)]
    reshape x6 -> x2, local copies, waits for them, and re-layouts: 26.8 us -> 12.5 us  [restrict_rows(): rows.reshape(share, length_y // 2, 2, depth_z // 2, 2).sum(axis=(2, 4))]
    reshape x6 -> x4, local copies, waits for them, and re-layouts: 35.6 us -> 22.9 us  [restrict(): volume.reshape(volume.shape[0] // 2, 2, volume.shape[1] // 2, 2, volume.s...]
  transfers between devices with their start and end apart: 83 -> 55, of which waited for: 47 -> 48; matrix products, arithmetic and copies ran while one was open for 4% -> 2% of each run, Pallas kernels for 0% -> 0%
where the time goes in v3:
time: 836 us; the launch traced here: 822 us
  waiting for transfers between devices  221 us (26%)
  other arithmetic  192 us (23%)
  starting transfers between devices  186 us (22%)
  blocking collectives  106 us (13%)
  local copies, waits for them, and re-layouts  95 us (11%)
  between operations  20.9 us (2%)
    ppermute x22, waiting for transfers between devices, passed_along(): lax.ppermute(value, axis, [(source, source + steps) for source in range(i...  131 us
    all_to_all x4, blocking collectives, global_sums(): gathered = lax.all_to_all(packed, ('sx', 'sy'), 0, 0, tiled=True)  84.5 us
    ppermute x14, starting transfers between devices, row_halo(): before = lax.ppermute(volume[-1:], ROW_AXES, up)  64.5 us
    ppermute x22, starting transfers between devices, passed_along(): lax.ppermute(value, axis, [(source, source + steps) for source in range(i...  42 us
    all_to_all x1, waiting for transfers between devices, gather_grid(): gathered = lax.all_to_all(packed, ('sx', 'sy'), 0, 0, tiled=True)  37.2 us
    select_n x21, other arithmetic, relay_round(): return jnp.where(slice_index == 0, start_coarse, arrived)  35.5 us
    all_to_all x2, starting transfers between devices, restrict_rows(): gathered = lax.all_to_all(packed, ROW_AXES, 0, 0, tiled=True)  34.6 us
    add x14, other arithmetic, relay_round(): outgoing_state = coarse_image + corrections  33.7 us
  transfers between devices with their start and end apart: 55, of which 48 were waited for; matrix products, arithmetic and copies ran while one was open for 2% of the time, Pallas kernels for 0%

profile of v3, /device:TPU:6, one launch (start us, length us, event | category | flops | bytes accessed | tf_op | source)
XLA Modules:
  0.0 821.8 jit_solution(16580030168810010263)
XLA Ops:
  0.7 6.3 reshape.504
  53.5 12.3 %all_to_all.61 = f32[4,6,1,16,256]{4,3,1,2,0:T(8,128)S(1)} all-to-all(f32[4,6,1,16,256]{4,3,1,2,0:T(8,128)S(1)} %copy.39), channel_id=1, replica_groups=mesh['tm'=8,'sx'=8,'sy'=4] {'sy'}, dimensions={0} | all-to-all | bytes 786432 | tf_op jit(solution)/shard_map/all_to_all | solution.py:244
  67.2 9.6 %all-to-all-start = ((f32[32,6,2,8,128]{4,3,2,1,0:T(8,128)}), f32[32,6,2,8,128]{4,3,2,1,0:T(8,128)S(1)}, u32[]{:S(2)}, u32[]{:S(2)}) async-start(f32[32,6,2,8,128]{4,3,2,1,0:T(8,128)} %broadcast_in_dim.164), calls=%async_computation | async-start | bytes 3145728 | tf_op jit(solution)/shard_map/all_to_all | solution.py:227
  77.5 37.2 %all-to-all-done = f32[32,6,2,8,128]{4,3,2,1,0:T(8,128)S(1)} async-done(((f32[32,6,2,8,128]{4,3,2,1,0:T(8,128)}), f32[32,6,2,8,128]{4,3,2,1,0:T(8,128)S(1)}, u32[]{:S(2)}, u32[]{:S(2)}) %all-to-all-start) | async-done | bytes 1572896 | tf_op jit(solution)/shard_map/all_to_all | solution.py:227
  118.4 91.5 %while.37 = (s32[]{:T(128)}, f32[16,32,128]{2,1,0:T(8,128)}, pred[]{:T(512)}, f32[16,32,128]{2,1,0:T(8,128)S(1)}, f32[16,32,128]{2,1,0:T(8,128)S(1)}, /*index=5*...) while((s32[]{:T(128)}, f32[16,32,128]{2,1,0:T(8,128)}, ...), condition=%wide.region_5.6_spmd, body=%wide.region_4.5_spmd.sunk | while | flops 4849666 | bytes 6815942 | solution.py:357
  123.7 6.1 collective-permute-done
  136.8 6.1 collective-permute-done
  149.8 6.1 collective-permute-done
  162.9 6.1 collective-permute-done
  176.0 6.1 collective-permute-done
  189.1 6.1 collective-permute-done
  202.1 6.1 collective-permute-done
  238.4 23.9 %all_to_all.62 = f32[32,1,2]{2,1,0:T(1,128)S(1)} all-to-all(f32[32,1,2]{2,1,0:T(1,128)S(1)} %broadcast_in_dim.170), channel_id=1, replica_groups=mesh['tm'=8,'sx'=8,'sy'=4] {'sx','sy'}, dimensions={0} | all-to-all | bytes 512 | tf_op jit(solution)/shard_map/all_to_all | solution.py:154
  278.1 18.9 %all_to_all.63 = f32[32,1,2]{2,1,0:T(1,128)S(1)} all-to-all(f32[32,1,2]{2,1,0:T(1,128)S(1)} %broadcast_in_dim.171), channel_id=1, replica_groups=mesh['tm'=8,'sx'=8,'sy'=4] {'sx','sy'}, dimensions={0} | all-to-all | bytes 512 | tf_op jit(solution)/shard_map/all_to_all | solution.py:154
  316.8 7.8 all-to-all-start.4
  360.6 6.3 reshape.510
  370.6 18.1 %all-to-all-start.5 = ((f32[32,1,32,128]{3,2,1,0:T(8,128)}), f32[32,1,32,128]{3,2,1,0:T(8,128)}, u32[]{:S(2)}, u32[]{:S(2)}) async-start(f32[32,1,32,128]{3,2,1,0:T(8,128)} %broadcast_in_dim.173), calls=%async_computation.5 | async-start | bytes 1048576 | tf_op jit(solution)/shard_map/all_to_all | solution.py:266
  391.1 11.4 %all-to-all-done.5 = f32[32,1,32,128]{3,2,1,0:T(8,128)} async-done(((f32[32,1,32,128]{3,2,1,0:T(8,128)}), f32[32,1,32,128]{3,2,1,0:T(8,128)}, u32[]{:S(2)}, u32[]{:S(2)}) %all-to-all-start.5) | async-done | bytes 524320 | tf_op jit(solution)/shard_map/all_to_all | solution.py:266
  407.4 92.0 %while.38 = (s32[]{:T(128)}, f32[16,32,128]{2,1,0:T(8,128)}, pred[]{:T(512)}, f32[16,32,128]{2,1,0:T(8,128)S(1)}, f32[16,32,128]{2,1,0:T(8,128)S(1)}, /*index=5*...) while((s32[]{:T(128)}, f32[16,32,128]{2,1,0:T(8,128)}, ...), condition=%wide.region_18.20_spmd, body=%wide.region_17.19_spmd.sunk | while | flops 4915202 | bytes 7078094 | solution.py:357
  412.7 6.1 collective-permute-done.1
  425.9 6.1 collective-permute-done.1
  439.0 6.1 collective-permute-done.1
  452.2 6.1 collective-permute-done.1
  465.3 6.1 collective-permute-done.1
  545.8 22.8 %all_to_all.64 = f32[32,1,2]{2,1,0:T(1,128)S(1)} all-to-all(f32[32,1,2]{2,1,0:T(1,128)S(1)} %broadcast_in_dim.180), channel_id=1, replica_groups=mesh['tm'=8,'sx'=8,'sy'=4] {'sx','sy'}, dimensions={0} | all-to-all | bytes 512 | tf_op jit(solution)/shard_map/all_to_all | solution.py:154
  584.4 18.9 %all_to_all.65 = f32[32,1,2]{2,1,0:T(1,128)S(1)} all-to-all(f32[32,1,2]{2,1,0:T(1,128)S(1)} %broadcast_in_dim.181), channel_id=1, replica_groups=mesh['tm'=8,'sx'=8,'sy'=4] {'sx','sy'}, dimensions={0} | all-to-all | bytes 512 | tf_op jit(solution)/shard_map/all_to_all | solution.py:154
  622.2 9.3 %all-to-all-start.8 = ((f32[32,1,2]{2,1,0:T(1,128)}), f32[32,1,2]{2,1,0:T(1,128)S(1)}, u32[]{:S(2)}, u32[]{:S(2)}) async-start(f32[32,1,2]{2,1,0:T(1,128)} %broadcast_in_dim.182), calls=%async_computation.8 | async-start | bytes 32768 | tf_op jit(solution)/shard_map/all_to_all | solution.py:154
  667.5 6.3 reshape.512
  677.5 16.6 %all-to-all-start.9 = ((f32[32,1,32,128]{3,2,1,0:T(8,128)}), f32[32,1,32,128]{3,2,1,0:T(8,128)}, u32[]{:S(2)}, u32[]{:S(2)}) async-start(f32[32,1,32,128]{3,2,1,0:T(8,128)} %broadcast_in_dim.183), calls=%async_computation.9 | async-start | bytes 1048576 | tf_op jit(solution)/shard_map/all_to_all | solution.py:266
  694.8 13.1 %all-to-all-done.9 = f32[32,1,32,128]{3,2,1,0:T(8,128)} async-done(((f32[32,1,32,128]{3,2,1,0:T(8,128)}), f32[32,1,32,128]{3,2,1,0:T(8,128)}, u32[]{:S(2)}, u32[]{:S(2)}) %all-to-all-start.9) | async-done | bytes 524320 | tf_op jit(solution)/shard_map/all_to_all | solution.py:266
  710.7 91.9 %while.39 = (s32[]{:T(128)}, f32[16,32,128]{2,1,0:T(8,128)}, pred[]{:T(512)}, f32[16,32,128]{2,1,0:T(8,128)S(1)}, f32[16,32,128]{2,1,0:T(8,128)S(1)}, /*index=5*...) while((s32[]{:T(128)}, f32[16,32,128]{2,1,0:T(8,128)}, ...), condition=%wide.region_31.33_spmd, body=%wide.region_30.32_spmd.sunk | while | flops 4915202 | bytes 7078094 | solution.py:357
  811.5 9.1 %all_to_all.66 = f32[4,2,1,16,256]{4,3,2,1,0:T(8,128)S(1)} all-to-all(f32[4,2,1,16,256]{4,3,2,1,0:T(8,128)S(1)} %maximum_bitcast_fusion), channel_id=1, replica_groups=mesh['tm'=8,'sx'=8,'sy'=4] {'sy'}, dimensions={0} | all-to-all | bytes 262144 | tf_op jit(solution)/shard_map/all_to_all | solution.py:253
  (351 shorter events, 479.8 us)
Async XLA Ops:
  67.2 47.6 %all-to-all-start = ((f32[32,6,2,8,128]{4,3,2,1,0:T(8,128)}), f32[32,6,2,8,128]{4,3,2,1,0:T(8,128)S(1)}, u32[]{:S(2)}, u32[]{:S(2)}) async-start(f32[32,6,2,8,128]{4,3,2,1,0:T(8,128)} %broadcast_in_dim.164), calls=%async_computation | async-start | bytes 3145728 | tf_op jit(solution)/shard_map/all_to_all | solution.py:227
  121.8 8.0 collective-permute-start
  134.9 8.0 collective-permute-start
  147.9 8.0 collective-permute-start
  161.0 8.0 collective-permute-start
  174.1 8.0 collective-permute-start
  187.1 8.0 collective-permute-start
  200.2 8.0 collective-permute-start
  316.8 17.6 %all-to-all-start.4 = ((f32[32,1,2]{2,1,0:T(1,128)}), f32[32,1,2]{2,1,0:T(1,128)S(1)}, u32[]{:S(2)}, u32[]{:S(2)}) async-start(f32[32,1,2]{2,1,0:T(1,128)} %broadcast_in_dim.172), calls=%async_computation.4 | async-start | bytes 32768 | tf_op jit(solution)/shard_map/all_to_all | solution.py:154
  326.2 20.7 %collective-permute-start.12 = (f32[1,64,256]{2,1,0:T(8,128)}, f32[1,64,256]{2,1,0:T(8,128)}, u32[]{:S(2)}, u32[]{:S(2)}) collective-permute-start(f32[1,64,256]{2,1,0:T(8,128)} %fusion.298), channel_id=1, source_target_pairs={{1,0},{2,1},{3,2},{4,3},{5,4},{6,5},{7,6},{8,7},{9,8},{10,9},{11,1... | collective-permute-start | bytes 196616 | tf_op jit(solution)/shard_map/ppermute | solution.py:86
  327.5 19.4 %collective-permute-start.14 = (f32[1,64,256]{2,1,0:T(8,128)}, f32[1,64,256]{2,1,0:T(8,128)}, u32[]{:S(2)}, u32[]{:S(2)}) collective-permute-start(f32[1,64,256]{2,1,0:T(8,128)} %fusion.298), channel_id=1, source_target_pairs={{0,1},{1,2},{2,3},{3,4},{4,5},{5,6},{6,7},{7,8},{8,9},{9,10},{10,1... | collective-permute-start | bytes 196616 | tf_op jit(solution)/shard_map/ppermute | solution.py:85
  341.0 6.9 collective-permute-start.11
  370.6 31.9 %all-to-all-start.5 = ((f32[32,1,32,128]{3,2,1,0:T(8,128)}), f32[32,1,32,128]{3,2,1,0:T(8,128)}, u32[]{:S(2)}, u32[]{:S(2)}) async-start(f32[32,1,32,128]{3,2,1,0:T(8,128)} %broadcast_in_dim.173), calls=%async_computation.5 | async-start | bytes 1048576 | tf_op jit(solution)/shard_map/all_to_all | solution.py:266
  410.8 8.0 collective-permute-start.1
  424.0 8.0 collective-permute-start.1
  437.1 8.0 collective-permute-start.1
  450.2 8.0 collective-permute-start.1
  463.4 8.0 collective-permute-start.1
  476.5 8.0 collective-permute-start.1
  489.7 8.0 collective-permute-start.1
  622.2 19.1 %all-to-all-start.8 = ((f32[32,1,2]{2,1,0:T(1,128)}), f32[32,1,2]{2,1,0:T(1,128)S(1)}, u32[]{:S(2)}, u32[]{:S(2)}) async-start(f32[32,1,2]{2,1,0:T(1,128)} %broadcast_in_dim.182), calls=%async_computation.8 | async-start | bytes 32768 | tf_op jit(solution)/shard_map/all_to_all | solution.py:154
  631.6 22.2 %collective-permute-start.27 = (f32[1,64,256]{2,1,0:T(8,128)}, f32[1,64,256]{2,1,0:T(8,128)}, u32[]{:S(2)}, u32[]{:S(2)}) collective-permute-start(f32[1,64,256]{2,1,0:T(8,128)} %get-tuple-element.743), channel_id=1, source_target_pairs={{1,0},{2,1},{3,2},{4,3},{5,4},{6,5},{7,6},{8,7},{9,8},{10,9},{11,1... | collective-permute-start | bytes 196616 | tf_op jit(solution)/shard_map/ppermute | solution.py:86
  632.9 20.9 %collective-permute-start.29 = (f32[1,64,256]{2,1,0:T(8,128)}, f32[1,64,256]{2,1,0:T(8,128)}, u32[]{:S(2)}, u32[]{:S(2)}) collective-permute-start(f32[1,64,256]{2,1,0:T(8,128)} %get-tuple-element.743), channel_id=1, source_target_pairs={{0,1},{1,2},{2,3},{3,4},{4,5},{5,6},{6,7},{7,8},{8,9},{9,10},{10,1... | collective-permute-start | bytes 196616 | tf_op jit(solution)/shard_map/ppermute | solution.py:85
  647.9 6.9 collective-permute-start.26
  677.5 30.4 %all-to-all-start.9 = ((f32[32,1,32,128]{3,2,1,0:T(8,128)}), f32[32,1,32,128]{3,2,1,0:T(8,128)}, u32[]{:S(2)}, u32[]{:S(2)}) async-start(f32[32,1,32,128]{3,2,1,0:T(8,128)} %broadcast_in_dim.183), calls=%async_computation.9 | async-start | bytes 1048576 | tf_op jit(solution)/shard_map/all_to_all | solution.py:266
  714.1 8.0 collective-permute-start.2
  727.2 8.0 collective-permute-start.2
  740.3 8.0 collective-permute-start.2
  753.5 8.0 collective-permute-start.2
  766.6 8.0 collective-permute-start.2
  779.7 8.0 collective-permute-start.2
  792.8 8.0 collective-permute-start.2
  (56 other events, 446.8 us)

commit v4 on v3

--- a/solution.py
+++ b/solution.py
@@ -370,7 +370,17 @@
         )
     )
     share = initial_rows.shape[0]
-    coarse_state, coarse_image = chain(None)
+    def own_chain(turn_no, carried):
+        coarse_state, own_state, own_image = carried
+        coarse_image = coarse_step(coarse_state)
+        mine = turn_no == slice_index
+        own_state = jnp.where(mine, coarse_state, own_state)
+        own_image = jnp.where(mine, coarse_image, own_image)
+        return (coarse_image, own_state, own_image)
+
+    _, coarse_state, coarse_image = lax.fori_loop(
+        0, slices, own_chain, (start_coarse, start_coarse, start_coarse)
+    )
     starts = jnp.where(slice_index == 0, initial_rows, prolong_rows(coarse_state, share))
     previous_image = coarse_image
     ends = starts

time: 836 us -> 781 us (0.934)
  waiting for transfers between devices: 221 us -> 169 us
  starting transfers between devices: 186 us -> 177 us
    ppermute x22 -> x15, waiting for transfers between devices: 131 us -> 88.8 us  [passed_along(): lax.ppermute(value, axis, [(source, source + steps) for source in range(i...]
    select_n x0 -> x8, other arithmetic: none -> 28.9 us  [own_chain(): own_image = jnp.where(mine, coarse_image, own_image)]
    sub x8 -> x0, other arithmetic: 17.9 us -> none  [coarse_step(): return coarse_state - balance / slope_sum]
    ppermute x22 -> x15, starting transfers between devices: 42 us -> 28.7 us  [passed_along(): lax.ppermute(value, axis, [(source, source + steps) for source in range(i...]
    select_n x21 -> x14, other arithmetic: 35.5 us -> 23.8 us  [relay_round(): return jnp.where(slice_index == 0, start_coarse, arrived)]
  transfers between devices with their start and end apart: 55 -> 48, of which waited for: 48 -> 41; matrix products, arithmetic and copies ran while one was open for 2% -> 3% of each run, Pallas kernels for 0% -> 0%
where the time goes in v4:
time: 781 us; the launch traced here: 767 us
  other arithmetic  197 us (25%)
  starting transfers between devices  177 us (23%)
  waiting for transfers between devices  169 us (22%)
  blocking collectives  106 us (14%)
  local copies, waits for them, and re-layouts  96.9 us (12%)
  between operations  21.7 us (3%)
    ppermute x15, waiting for transfers between devices, passed_along(): lax.ppermute(value, axis, [(source, source + steps) for source in range(i...  88.8 us
    all_to_all x4, blocking collectives, global_sums(): gathered = lax.all_to_all(packed, ('sx', 'sy'), 0, 0, tiled=True)  84.5 us
    ppermute x14, starting transfers between devices, row_halo(): before = lax.ppermute(volume[-1:], ROW_AXES, up)  66.6 us
    all_to_all x1, waiting for transfers between devices, gather_grid(): gathered = lax.all_to_all(packed, ('sx', 'sy'), 0, 0, tiled=True)  37.2 us
    div x27, other arithmetic, fractional(): water_mobility / mobility  35.5 us
    all_to_all x2, starting transfers between devices, restrict_rows(): gathered = lax.all_to_all(packed, ROW_AXES, 0, 0, tiled=True)  35.2 us
    add x14, other arithmetic, relay_round(): outgoing_state = coarse_image + corrections  33.6 us
    select_n x8, other arithmetic, own_chain(): own_image = jnp.where(mine, coarse_image, own_image)  28.9 us
  transfers between devices with their start and end apart: 48, of which 41 were waited for; matrix products, arithmetic and copies ran while one was open for 3% of the time, Pallas kernels for 0%

profile of v4, /device:TPU:6, one launch (start us, length us, event | category | flops | bytes accessed | tf_op | source)
XLA Modules:
  0.0 767.4 jit_solution(8327646889786791681)
XLA Ops:
  0.7 6.3 reshape.504
  53.5 12.3 %all_to_all.61 = f32[4,6,1,16,256]{4,3,1,2,0:T(8,128)S(1)} all-to-all(f32[4,6,1,16,256]{4,3,1,2,0:T(8,128)S(1)} %copy.39), channel_id=1, replica_groups=mesh['tm'=8,'sx'=8,'sy'=4] {'sy'}, dimensions={0} | all-to-all | bytes 786432 | tf_op jit(solution)/shard_map/all_to_all | solution.py:244
  67.2 9.6 %all-to-all-start = ((f32[32,6,2,8,128]{4,3,2,1,0:T(8,128)}), f32[32,6,2,8,128]{4,3,2,1,0:T(8,128)S(1)}, u32[]{:S(2)}, u32[]{:S(2)}) async-start(f32[32,6,2,8,128]{4,3,2,1,0:T(8,128)} %broadcast_in_dim.164), calls=%async_computation | async-start | bytes 3145728 | tf_op jit(solution)/shard_map/all_to_all | solution.py:227
  77.5 37.2 %all-to-all-done = f32[32,6,2,8,128]{4,3,2,1,0:T(8,128)S(1)} async-done(((f32[32,6,2,8,128]{4,3,2,1,0:T(8,128)}), f32[32,6,2,8,128]{4,3,2,1,0:T(8,128)S(1)}, u32[]{:S(2)}, u32[]{:S(2)}) %all-to-all-start) | async-done | bytes 1572896 | tf_op jit(solution)/shard_map/all_to_all | solution.py:227
  119.8 42.8 %while.44 = (s32[]{:T(128)}, f32[16,32,128]{2,1,0:T(8,128)}, f32[16,32,128]{2,1,0:T(8,128)}, f32[16,32,128]{2,1,0:T(8,128)}, f32[16,32,128]{2,1,0:T(8,128)S(1)},...) while((s32[]{:T(128)}, f32[16,32,128]{2,1,0:T(8,128)}, ...), condition=%wide.region_5.6_spmd, body=%wide.region_4.5_spmd.sunk | while | flops 4915203 | bytes 6029487 | solution.py:381
  191.8 23.9 %all_to_all.62 = f32[32,1,2]{2,1,0:T(1,128)S(1)} all-to-all(f32[32,1,2]{2,1,0:T(1,128)S(1)} %broadcast_in_dim.170), channel_id=1, replica_groups=mesh['tm'=8,'sx'=8,'sy'=4] {'sx','sy'}, dimensions={0} | all-to-all | bytes 512 | tf_op jit(solution)/shard_map/all_to_all | solution.py:154
  231.5 18.9 %all_to_all.63 = f32[32,1,2]{2,1,0:T(1,128)S(1)} all-to-all(f32[32,1,2]{2,1,0:T(1,128)S(1)} %broadcast_in_dim.171), channel_id=1, replica_groups=mesh['tm'=8,'sx'=8,'sy'=4] {'sx','sy'}, dimensions={0} | all-to-all | bytes 512 | tf_op jit(solution)/shard_map/all_to_all | solution.py:154
  269.3 9.3 %all-to-all-start.4 = ((f32[32,1,2]{2,1,0:T(1,128)}), f32[32,1,2]{2,1,0:T(1,128)S(1)}, u32[]{:S(2)}, u32[]{:S(2)}) async-start(f32[32,1,2]{2,1,0:T(1,128)} %broadcast_in_dim.172), calls=%async_computation.4 | async-start | bytes 32768 | tf_op jit(solution)/shard_map/all_to_all | solution.py:154
  314.6 6.3 reshape.510
  324.5 18.4 %all-to-all-start.5 = ((f32[32,1,32,128]{3,2,1,0:T(8,128)}), f32[32,1,32,128]{3,2,1,0:T(8,128)}, u32[]{:S(2)}, u32[]{:S(2)}) async-start(f32[32,1,32,128]{3,2,1,0:T(8,128)} %broadcast_in_dim.173), calls=%async_computation.5 | async-start | bytes 1048576 | tf_op jit(solution)/shard_map/all_to_all | solution.py:266
  359.6 91.9 %while.45 = (s32[]{:T(128)}, f32[16,32,128]{2,1,0:T(8,128)}, pred[]{:T(512)}, f32[16,32,128]{2,1,0:T(8,128)S(1)}, f32[16,32,128]{2,1,0:T(8,128)S(1)}, /*index=5*...) while((s32[]{:T(128)}, f32[16,32,128]{2,1,0:T(8,128)}, ...), condition=%wide.region_18.20_spmd, body=%wide.region_17.19_spmd.sunk | while | flops 4915202 | bytes 7078094 | solution.py:357
  365.0 6.1 collective-permute-done
  378.1 6.1 collective-permute-done
  391.2 6.1 collective-permute-done
  404.3 6.1 collective-permute-done
  417.5 6.1 collective-permute-done
  430.6 6.1 collective-permute-done
  443.7 6.1 collective-permute-done
  490.8 22.8 %all_to_all.64 = f32[32,1,2]{2,1,0:T(1,128)S(1)} all-to-all(f32[32,1,2]{2,1,0:T(1,128)S(1)} %broadcast_in_dim.180), channel_id=1, replica_groups=mesh['tm'=8,'sx'=8,'sy'=4] {'sx','sy'}, dimensions={0} | all-to-all | bytes 512 | tf_op jit(solution)/shard_map/all_to_all | solution.py:154
  529.4 18.9 %all_to_all.65 = f32[32,1,2]{2,1,0:T(1,128)S(1)} all-to-all(f32[32,1,2]{2,1,0:T(1,128)S(1)} %broadcast_in_dim.181), channel_id=1, replica_groups=mesh['tm'=8,'sx'=8,'sy'=4] {'sx','sy'}, dimensions={0} | all-to-all | bytes 512 | tf_op jit(solution)/shard_map/all_to_all | solution.py:154
  567.5 9.3 %all-to-all-start.8 = ((f32[32,1,2]{2,1,0:T(1,128)}), f32[32,1,2]{2,1,0:T(1,128)S(1)}, u32[]{:S(2)}, u32[]{:S(2)}) async-start(f32[32,1,2]{2,1,0:T(1,128)} %broadcast_in_dim.182), calls=%async_computation.8 | async-start | bytes 32768 | tf_op jit(solution)/shard_map/all_to_all | solution.py:154
  612.8 6.3 reshape.512
  622.8 16.7 %all-to-all-start.9 = ((f32[32,1,32,128]{3,2,1,0:T(8,128)}), f32[32,1,32,128]{3,2,1,0:T(8,128)}, u32[]{:S(2)}, u32[]{:S(2)}) async-start(f32[32,1,32,128]{3,2,1,0:T(8,128)} %broadcast_in_dim.183), calls=%async_computation.9 | async-start | bytes 1048576 | tf_op jit(solution)/shard_map/all_to_all | solution.py:266
  640.2 13.1 %all-to-all-done.9 = f32[32,1,32,128]{3,2,1,0:T(8,128)} async-done(((f32[32,1,32,128]{3,2,1,0:T(8,128)}), f32[32,1,32,128]{3,2,1,0:T(8,128)}, u32[]{:S(2)}, u32[]{:S(2)}) %all-to-all-start.9) | async-done | bytes 524320 | tf_op jit(solution)/shard_map/all_to_all | solution.py:266
  656.1 92.1 %while.46 = (s32[]{:T(128)}, f32[16,32,128]{2,1,0:T(8,128)}, pred[]{:T(512)}, f32[16,32,128]{2,1,0:T(8,128)S(1)}, f32[16,32,128]{2,1,0:T(8,128)S(1)}, /*index=5*...) while((s32[]{:T(128)}, f32[16,32,128]{2,1,0:T(8,128)}, ...), condition=%wide.region_31.33_spmd, body=%wide.region_30.32_spmd.sunk | while | flops 4915202 | bytes 7078094 | solution.py:357
  661.5 6.1 collective-permute-done.1
  674.6 6.1 collective-permute-done.1
  687.8 6.1 collective-permute-done.1
  700.9 6.1 collective-permute-done.1
  714.1 6.1 collective-permute-done.1
  727.2 6.1 collective-permute-done.1
  757.2 9.1 %all_to_all.66 = f32[4,2,1,16,256]{4,3,2,1,0:T(8,128)S(1)} all-to-all(f32[4,2,1,16,256]{4,3,2,1,0:T(8,128)S(1)} %maximum_bitcast_fusion), channel_id=1, replica_groups=mesh['tm'=8,'sx'=8,'sy'=4] {'sy'}, dimensions={0} | all-to-all | bytes 262144 | tf_op jit(solution)/shard_map/all_to_all | solution.py:253
  (333 shorter events, 428.0 us)
Async XLA Ops:
  67.2 47.6 %all-to-all-start = ((f32[32,6,2,8,128]{4,3,2,1,0:T(8,128)}), f32[32,6,2,8,128]{4,3,2,1,0:T(8,128)S(1)}, u32[]{:S(2)}, u32[]{:S(2)}) async-start(f32[32,6,2,8,128]{4,3,2,1,0:T(8,128)} %broadcast_in_dim.164), calls=%async_computation | async-start | bytes 3145728 | tf_op jit(solution)/shard_map/all_to_all | solution.py:227
  182.1 6.8 collective-permute-start.5
  269.3 18.9 %all-to-all-start.4 = ((f32[32,1,2]{2,1,0:T(1,128)}), f32[32,1,2]{2,1,0:T(1,128)S(1)}, u32[]{:S(2)}, u32[]{:S(2)}) async-start(f32[32,1,2]{2,1,0:T(1,128)} %broadcast_in_dim.172), calls=%async_computation.4 | async-start | bytes 32768 | tf_op jit(solution)/shard_map/all_to_all | solution.py:154
  280.2 20.7 %collective-permute-start.11 = (f32[1,64,256]{2,1,0:T(8,128)}, f32[1,64,256]{2,1,0:T(8,128)}, u32[]{:S(2)}, u32[]{:S(2)}) collective-permute-start(f32[1,64,256]{2,1,0:T(8,128)} %fusion.276), channel_id=1, source_target_pairs={{1,0},{2,1},{3,2},{4,3},{5,4},{6,5},{7,6},{8,7},{9,8},{10,9},{11,1... | collective-permute-start | bytes 196616 | tf_op jit(solution)/shard_map/ppermute | solution.py:86
  281.4 19.4 %collective-permute-start.13 = (f32[1,64,256]{2,1,0:T(8,128)}, f32[1,64,256]{2,1,0:T(8,128)}, u32[]{:S(2)}, u32[]{:S(2)}) collective-permute-start(f32[1,64,256]{2,1,0:T(8,128)} %fusion.276), channel_id=1, source_target_pairs={{0,1},{1,2},{2,3},{3,4},{4,5},{5,6},{6,7},{7,8},{8,9},{9,10},{10,1... | collective-permute-start | bytes 196616 | tf_op jit(solution)/shard_map/ppermute | solution.py:85
  295.0 6.9 collective-permute-start.10
  304.3 6.5 collective-permute-start.14
  305.6 6.8 collective-permute-start.15
  324.5 32.3 %all-to-all-start.5 = ((f32[32,1,32,128]{3,2,1,0:T(8,128)}), f32[32,1,32,128]{3,2,1,0:T(8,128)}, u32[]{:S(2)}, u32[]{:S(2)}) async-start(f32[32,1,32,128]{3,2,1,0:T(8,128)} %broadcast_in_dim.173), calls=%async_computation.5 | async-start | bytes 1048576 | tf_op jit(solution)/shard_map/all_to_all | solution.py:266
  363.0 8.0 %collective-permute-start = (f32[16,32,128]{2,1,0:T(8,128)}, f32[16,32,128]{2,1,0:T(8,128)}, u32[]{:S(2)}, u32[]{:S(2)}) collective-permute-start(f32[16,32,128]{2,1,0:T(8,128)} %fusion.331), channel_id=1, source_target_pairs={{0,32},{32,64},{64,96},{96,128},{128,160},{160,192},{192,224},{1,3... | collective-permute-start | bytes 786440 | tf_op jit(solution)/shard_map/while/body/eval_jaxpr/ppermute | solution.py:37
  376.2 8.0 %collective-permute-start = (f32[16,32,128]{2,1,0:T(8,128)}, f32[16,32,128]{2,1,0:T(8,128)}, u32[]{:S(2)}, u32[]{:S(2)}) collective-permute-start(f32[16,32,128]{2,1,0:T(8,128)} %fusion.331), channel_id=1, source_target_pairs={{0,32},{32,64},{64,96},{96,128},{128,160},{160,192},{192,224},{1,3... | collective-permute-start | bytes 786440 | tf_op jit(solution)/shard_map/while/body/eval_jaxpr/ppermute | solution.py:37
  389.3 8.0 %collective-permute-start = (f32[16,32,128]{2,1,0:T(8,128)}, f32[16,32,128]{2,1,0:T(8,128)}, u32[]{:S(2)}, u32[]{:S(2)}) collective-permute-start(f32[16,32,128]{2,1,0:T(8,128)} %fusion.331), channel_id=1, source_target_pairs={{0,32},{32,64},{64,96},{96,128},{128,160},{160,192},{192,224},{1,3... | collective-permute-start | bytes 786440 | tf_op jit(solution)/shard_map/while/body/eval_jaxpr/ppermute | solution.py:37
  402.4 8.0 %collective-permute-start = (f32[16,32,128]{2,1,0:T(8,128)}, f32[16,32,128]{2,1,0:T(8,128)}, u32[]{:S(2)}, u32[]{:S(2)}) collective-permute-start(f32[16,32,128]{2,1,0:T(8,128)} %fusion.331), channel_id=1, source_target_pairs={{0,32},{32,64},{64,96},{96,128},{128,160},{160,192},{192,224},{1,3... | collective-permute-start | bytes 786440 | tf_op jit(solution)/shard_map/while/body/eval_jaxpr/ppermute | solution.py:37
  415.6 8.0 %collective-permute-start = (f32[16,32,128]{2,1,0:T(8,128)}, f32[16,32,128]{2,1,0:T(8,128)}, u32[]{:S(2)}, u32[]{:S(2)}) collective-permute-start(f32[16,32,128]{2,1,0:T(8,128)} %fusion.331), channel_id=1, source_target_pairs={{0,32},{32,64},{64,96},{96,128},{128,160},{160,192},{192,224},{1,3... | collective-permute-start | bytes 786440 | tf_op jit(solution)/shard_map/while/body/eval_jaxpr/ppermute | solution.py:37
  428.7 8.0 %collective-permute-start = (f32[16,32,128]{2,1,0:T(8,128)}, f32[16,32,128]{2,1,0:T(8,128)}, u32[]{:S(2)}, u32[]{:S(2)}) collective-permute-start(f32[16,32,128]{2,1,0:T(8,128)} %fusion.331), channel_id=1, source_target_pairs={{0,32},{32,64},{64,96},{96,128},{128,160},{160,192},{192,224},{1,3... | collective-permute-start | bytes 786440 | tf_op jit(solution)/shard_map/while/body/eval_jaxpr/ppermute | solution.py:37
  441.8 8.0 %collective-permute-start = (f32[16,32,128]{2,1,0:T(8,128)}, f32[16,32,128]{2,1,0:T(8,128)}, u32[]{:S(2)}, u32[]{:S(2)}) collective-permute-start(f32[16,32,128]{2,1,0:T(8,128)} %fusion.331), channel_id=1, source_target_pairs={{0,32},{32,64},{64,96},{96,128},{128,160},{160,192},{192,224},{1,3... | collective-permute-start | bytes 786440 | tf_op jit(solution)/shard_map/while/body/eval_jaxpr/ppermute | solution.py:37
  479.8 6.5 collective-permute-start.19
  481.1 6.8 collective-permute-start.20
  567.5 18.9 %all-to-all-start.8 = ((f32[32,1,2]{2,1,0:T(1,128)}), f32[32,1,2]{2,1,0:T(1,128)S(1)}, u32[]{:S(2)}, u32[]{:S(2)}) async-start(f32[32,1,2]{2,1,0:T(1,128)} %broadcast_in_dim.182), calls=%async_computation.8 | async-start | bytes 32768 | tf_op jit(solution)/shard_map/all_to_all | solution.py:154
  576.8 22.3 %collective-permute-start.26 = (f32[1,64,256]{2,1,0:T(8,128)}, f32[1,64,256]{2,1,0:T(8,128)}, u32[]{:S(2)}, u32[]{:S(2)}) collective-permute-start(f32[1,64,256]{2,1,0:T(8,128)} %get-tuple-element.936), channel_id=1, source_target_pairs={{1,0},{2,1},{3,2},{4,3},{5,4},{6,5},{7,6},{8,7},{9,8},{10,9},{11,1... | collective-permute-start | bytes 196616 | tf_op jit(solution)/shard_map/ppermute | solution.py:86
  578.1 21.0 %collective-permute-start.28 = (f32[1,64,256]{2,1,0:T(8,128)}, f32[1,64,256]{2,1,0:T(8,128)}, u32[]{:S(2)}, u32[]{:S(2)}) collective-permute-start(f32[1,64,256]{2,1,0:T(8,128)} %get-tuple-element.936), channel_id=1, source_target_pairs={{0,1},{1,2},{2,3},{3,4},{4,5},{5,6},{6,7},{7,8},{8,9},{9,10},{10,1... | collective-permute-start | bytes 196616 | tf_op jit(solution)/shard_map/ppermute | solution.py:85
  593.2 6.9 collective-permute-start.25
  602.5 6.5 collective-permute-start.29
  603.8 6.8 collective-permute-start.30
  622.8 30.5 %all-to-all-start.9 = ((f32[32,1,32,128]{3,2,1,0:T(8,128)}), f32[32,1,32,128]{3,2,1,0:T(8,128)}, u32[]{:S(2)}, u32[]{:S(2)}) async-start(f32[32,1,32,128]{3,2,1,0:T(8,128)} %broadcast_in_dim.183), calls=%async_computation.9 | async-start | bytes 1048576 | tf_op jit(solution)/shard_map/all_to_all | solution.py:266
  659.6 8.0 %collective-permute-start.1 = (f32[16,32,128]{2,1,0:T(8,128)}, f32[16,32,128]{2,1,0:T(8,128)}, u32[]{:S(2)}, u32[]{:S(2)}) collective-permute-start(f32[16,32,128]{2,1,0:T(8,128)} %fusion.332), channel_id=1, source_target_pairs={{0,32},{32,64},{64,96},{96,128},{128,160},{160,192},{192,224},{1,3... | collective-permute-start | bytes 786440 | tf_op jit(solution)/shard_map/while/body/eval_jaxpr/ppermute | solution.py:37
  672.7 8.0 %collective-permute-start.1 = (f32[16,32,128]{2,1,0:T(8,128)}, f32[16,32,128]{2,1,0:T(8,128)}, u32[]{:S(2)}, u32[]{:S(2)}) collective-permute-start(f32[16,32,128]{2,1,0:T(8,128)} %fusion.332), channel_id=1, source_target_pairs={{0,32},{32,64},{64,96},{96,128},{128,160},{160,192},{192,224},{1,3... | collective-permute-start | bytes 786440 | tf_op jit(solution)/shard_map/while/body/eval_jaxpr/ppermute | solution.py:37
  685.9 8.0 %collective-permute-start.1 = (f32[16,32,128]{2,1,0:T(8,128)}, f32[16,32,128]{2,1,0:T(8,128)}, u32[]{:S(2)}, u32[]{:S(2)}) collective-permute-start(f32[16,32,128]{2,1,0:T(8,128)} %fusion.332), channel_id=1, source_target_pairs={{0,32},{32,64},{64,96},{96,128},{128,160},{160,192},{192,224},{1,3... | collective-permute-start | bytes 786440 | tf_op jit(solution)/shard_map/while/body/eval_jaxpr/ppermute | solution.py:37
  699.0 8.0 %collective-permute-start.1 = (f32[16,32,128]{2,1,0:T(8,128)}, f32[16,32,128]{2,1,0:T(8,128)}, u32[]{:S(2)}, u32[]{:S(2)}) collective-permute-start(f32[16,32,128]{2,1,0:T(8,128)} %fusion.332), channel_id=1, source_target_pairs={{0,32},{32,64},{64,96},{96,128},{128,160},{160,192},{192,224},{1,3... | collective-permute-start | bytes 786440 | tf_op jit(solution)/shard_map/while/body/eval_jaxpr/ppermute | solution.py:37
  712.2 8.0 %collective-permute-start.1 = (f32[16,32,128]{2,1,0:T(8,128)}, f32[16,32,128]{2,1,0:T(8,128)}, u32[]{:S(2)}, u32[]{:S(2)}) collective-permute-start(f32[16,32,128]{2,1,0:T(8,128)} %fusion.332), channel_id=1, source_target_pairs={{0,32},{32,64},{64,96},{96,128},{128,160},{160,192},{192,224},{1,3... | collective-permute-start | bytes 786440 | tf_op jit(solution)/shard_map/while/body/eval_jaxpr/ppermute | solution.py:37
  725.3 8.0 %collective-permute-start.1 = (f32[16,32,128]{2,1,0:T(8,128)}, f32[16,32,128]{2,1,0:T(8,128)}, u32[]{:S(2)}, u32[]{:S(2)}) collective-permute-start(f32[16,32,128]{2,1,0:T(8,128)} %fusion.332), channel_id=1, source_target_pairs={{0,32},{32,64},{64,96},{96,128},{128,160},{160,192},{192,224},{1,3... | collective-permute-start | bytes 786440 | tf_op jit(solution)/shard_map/while/body/eval_jaxpr/ppermute | solution.py:37
  738.5 8.0 %collective-permute-start.1 = (f32[16,32,128]{2,1,0:T(8,128)}, f32[16,32,128]{2,1,0:T(8,128)}, u32[]{:S(2)}, u32[]{:S(2)}) collective-permute-start(f32[16,32,128]{2,1,0:T(8,128)} %fusion.332), channel_id=1, source_target_pairs={{0,32},{32,64},{64,96},{96,128},{128,160},{160,192},{192,224},{1,3... | collective-permute-start | bytes 786440 | tf_op jit(solution)/shard_map/while/body/eval_jaxpr/ppermute | solution.py:37
  (49 other events, 401.3 us)

commit v5 on v4

--- a/solution.py
+++ b/solution.py
@@ -345,18 +345,18 @@
 
     def chain(corrections):
 
-        def relay_round(turn_no, coarse_state):
-            coarse_image = coarse_step(coarse_state)
-            if corrections is None:
-                outgoing_state = coarse_image
-            else:
-                outgoing_state = coarse_image + corrections
-            arrived = passed_along(outgoing_state, "tm", 1)
-            return jnp.where(slice_index == 0, start_coarse, arrived)
-
-        coarse_state = lax.fori_loop(0, slices - 1, relay_round, start_coarse)
+        def relay_round(turn_no, arrived):
+            coarse_state = jnp.where(slice_index == 0, start_coarse, arrived)
+            return passed_along(coarse_step(coarse_state) + corrections, "tm", 1)
+
+        arrived = lax.fori_loop(0, slices - 1, relay_round, start_coarse)
+        coarse_state = jnp.where(slice_index == 0, start_coarse, arrived)
         return (coarse_state, coarse_step(coarse_state))
 
+    coarse_state = lax.fori_loop(
+        0, slice_index, lambda turn_no, state: coarse_step(state), start_coarse
+    )
+    coarse_image = coarse_step(coarse_state)
     initial_rows, permeability, porosity, source_rate, water_fine, oil_fine = to_rows(
         jnp.stack(
             [

time: 781 us -> 759 us (0.972)
  other arithmetic: 197 us -> 175 us
    select_n x14 -> x0, other arithmetic: 23.8 us -> none  [relay_round(): return jnp.where(slice_index == 0, start_coarse, arrived)]
where the time goes in v5:
time: 759 us; the launch traced here: 746 us
  starting transfers between devices  176 us (23%)
  other arithmetic  175 us (23%)
  waiting for transfers between devices  170 us (22%)
  blocking collectives  106 us (14%)
  local copies, waits for them, and re-layouts  97.2 us (13%)
  between operations  21.4 us (3%)
    ppermute x15, waiting for transfers between devices, passed_along(): lax.ppermute(value, axis, [(source, source + steps) for source in range(i...  88.7 us
    all_to_all x4, blocking collectives, global_sums(): gathered = lax.all_to_all(packed, ('sx', 'sy'), 0, 0, tiled=True)  84.5 us
    ppermute x14, starting transfers between devices, row_halo(): before = lax.ppermute(volume[-1:], ROW_AXES, up)  66.6 us
    all_to_all x1, waiting for transfers between devices, gather_grid(): gathered = lax.all_to_all(packed, ('sx', 'sy'), 0, 0, tiled=True)  37.2 us
    div x27, other arithmetic, fractional(): water_mobility / mobility  35.9 us
    all_to_all x2, starting transfers between devices, restrict_rows(): gathered = lax.all_to_all(packed, ROW_AXES, 0, 0, tiled=True)  34.9 us
    add x14, other arithmetic, relay_round(): return passed_along(coarse_step(coarse_state) + corrections, 'tm', 1)  33.9 us
    select_n x8, other arithmetic, own_chain(): own_image = jnp.where(mine, coarse_image, own_image)  30.2 us
  transfers between devices with their start and end apart: 48, of which 41 were waited for; matrix products, arithmetic and copies ran while one was open for 3% of the time, Pallas kernels for 0%

profile of v5, /device:TPU:6, one launch (start us, length us, event | category | flops | bytes accessed | tf_op | source)
XLA Modules:
  0.0 745.8 jit_solution(17662586136491624926)
XLA Ops:
  0.7 6.3 reshape.504
  53.5 12.3 %all_to_all.61 = f32[4,6,1,16,256]{4,3,1,2,0:T(8,128)S(1)} all-to-all(f32[4,6,1,16,256]{4,3,1,2,0:T(8,128)S(1)} %copy.39), channel_id=1, replica_groups=mesh['tm'=8,'sx'=8,'sy'=4] {'sy'}, dimensions={0} | all-to-all | bytes 786432 | tf_op jit(solution)/shard_map/all_to_all | solution.py:244
  67.2 9.6 %all-to-all-start = ((f32[32,6,2,8,128]{4,3,2,1,0:T(8,128)}), f32[32,6,2,8,128]{4,3,2,1,0:T(8,128)S(1)}, u32[]{:S(2)}, u32[]{:S(2)}) async-start(f32[32,6,2,8,128]{4,3,2,1,0:T(8,128)} %broadcast_in_dim.164), calls=%async_computation | async-start | bytes 3145728 | tf_op jit(solution)/shard_map/all_to_all | solution.py:227
  77.6 37.2 %all-to-all-done = f32[32,6,2,8,128]{4,3,2,1,0:T(8,128)S(1)} async-done(((f32[32,6,2,8,128]{4,3,2,1,0:T(8,128)}), f32[32,6,2,8,128]{4,3,2,1,0:T(8,128)S(1)}, u32[]{:S(2)}, u32[]{:S(2)}) %all-to-all-start) | async-done | bytes 1572896 | tf_op jit(solution)/shard_map/all_to_all | solution.py:227
  119.8 44.2 %while.44 = (s32[]{:T(128)}, f32[16,32,128]{2,1,0:T(8,128)}, f32[16,32,128]{2,1,0:T(8,128)}, f32[16,32,128]{2,1,0:T(8,128)}, f32[16,32,128]{2,1,0:T(8,128)S(1)},...) while((s32[]{:T(128)}, f32[16,32,128]{2,1,0:T(8,128)}, ...), condition=%wide.region_5.6_spmd, body=%wide.region_4.5_spmd.sunk | while | flops 4915203 | bytes 6029487 | solution.py:381
  193.3 23.9 %all_to_all.62 = f32[32,1,2]{2,1,0:T(1,128)S(1)} all-to-all(f32[32,1,2]{2,1,0:T(1,128)S(1)} %broadcast_in_dim.170), channel_id=1, replica_groups=mesh['tm'=8,'sx'=8,'sy'=4] {'sx','sy'}, dimensions={0} | all-to-all | bytes 512 | tf_op jit(solution)/shard_map/all_to_all | solution.py:154
  233.1 18.9 %all_to_all.63 = f32[32,1,2]{2,1,0:T(1,128)S(1)} all-to-all(f32[32,1,2]{2,1,0:T(1,128)S(1)} %broadcast_in_dim.171), channel_id=1, replica_groups=mesh['tm'=8,'sx'=8,'sy'=4] {'sx','sy'}, dimensions={0} | all-to-all | bytes 512 | tf_op jit(solution)/shard_map/all_to_all | solution.py:154
  271.2 9.3 %all-to-all-start.4 = ((f32[32,1,2]{2,1,0:T(1,128)}), f32[32,1,2]{2,1,0:T(1,128)S(1)}, u32[]{:S(2)}, u32[]{:S(2)}) async-start(f32[32,1,2]{2,1,0:T(1,128)} %broadcast_in_dim.172), calls=%async_computation.4 | async-start | bytes 32768 | tf_op jit(solution)/shard_map/all_to_all | solution.py:154
  316.6 6.3 reshape.510
  326.6 18.3 %all-to-all-start.5 = ((f32[32,1,32,128]{3,2,1,0:T(8,128)}), f32[32,1,32,128]{3,2,1,0:T(8,128)}, u32[]{:S(2)}, u32[]{:S(2)}) async-start(f32[32,1,32,128]{3,2,1,0:T(8,128)} %broadcast_in_dim.173), calls=%async_computation.5 | async-start | bytes 1048576 | tf_op jit(solution)/shard_map/all_to_all | solution.py:266
  361.5 80.4 %while.45 = (s32[]{:T(128)}, f32[16,32,128]{2,1,0:T(8,128)}, pred[]{:T(512)}, f32[16,32,128]{2,1,0:T(8,128)S(1)}, f32[16,32,128]{2,1,0:T(8,128)S(1)}, /*index=5*...) while((s32[]{:T(128)}, f32[16,32,128]{2,1,0:T(8,128)}, ...), condition=%wide.region_18.20_spmd, body=%wide.region_17.19_spmd.sunk | while | flops 4980738 | bytes 6815951 | solution.py:352
  366.9 6.1 collective-permute-done
  378.4 6.1 collective-permute-done
  401.3 6.1 collective-permute-done
  412.8 6.1 collective-permute-done
  424.3 6.1 collective-permute-done
  435.8 6.1 collective-permute-done
  481.1 22.8 %all_to_all.64 = f32[32,1,2]{2,1,0:T(1,128)S(1)} all-to-all(f32[32,1,2]{2,1,0:T(1,128)S(1)} %broadcast_in_dim.180), channel_id=1, replica_groups=mesh['tm'=8,'sx'=8,'sy'=4] {'sx','sy'}, dimensions={0} | all-to-all | bytes 512 | tf_op jit(solution)/shard_map/all_to_all | solution.py:154
  519.8 18.9 %all_to_all.65 = f32[32,1,2]{2,1,0:T(1,128)S(1)} all-to-all(f32[32,1,2]{2,1,0:T(1,128)S(1)} %broadcast_in_dim.181), channel_id=1, replica_groups=mesh['tm'=8,'sx'=8,'sy'=4] {'sx','sy'}, dimensions={0} | all-to-all | bytes 512 | tf_op jit(solution)/shard_map/all_to_all | solution.py:154
  557.5 9.3 %all-to-all-start.8 = ((f32[32,1,2]{2,1,0:T(1,128)}), f32[32,1,2]{2,1,0:T(1,128)S(1)}, u32[]{:S(2)}, u32[]{:S(2)}) async-start(f32[32,1,2]{2,1,0:T(1,128)} %broadcast_in_dim.182), calls=%async_computation.8 | async-start | bytes 32768 | tf_op jit(solution)/shard_map/all_to_all | solution.py:154
  602.9 6.3 reshape.512
  612.9 16.6 %all-to-all-start.9 = ((f32[32,1,32,128]{3,2,1,0:T(8,128)}), f32[32,1,32,128]{3,2,1,0:T(8,128)}, u32[]{:S(2)}, u32[]{:S(2)}) async-start(f32[32,1,32,128]{3,2,1,0:T(8,128)} %broadcast_in_dim.183), calls=%async_computation.9 | async-start | bytes 1048576 | tf_op jit(solution)/shard_map/all_to_all | solution.py:266
  630.2 13.1 %all-to-all-done.9 = f32[32,1,32,128]{3,2,1,0:T(8,128)} async-done(((f32[32,1,32,128]{3,2,1,0:T(8,128)}), f32[32,1,32,128]{3,2,1,0:T(8,128)}, u32[]{:S(2)}, u32[]{:S(2)}) %all-to-all-start.9) | async-done | bytes 524320 | tf_op jit(solution)/shard_map/all_to_all | solution.py:266
  646.1 80.4 %while.46 = (s32[]{:T(128)}, f32[16,32,128]{2,1,0:T(8,128)}, pred[]{:T(512)}, f32[16,32,128]{2,1,0:T(8,128)S(1)}, f32[16,32,128]{2,1,0:T(8,128)S(1)}, /*index=5*...) while((s32[]{:T(128)}, f32[16,32,128]{2,1,0:T(8,128)}, ...), condition=%wide.region_31.33_spmd, body=%wide.region_30.32_spmd.sunk | while | flops 4980738 | bytes 6815951 | solution.py:352
  651.5 6.1 collective-permute-done.1
  662.9 6.1 collective-permute-done.1
  674.4 6.1 collective-permute-done.1
  685.9 6.1 collective-permute-done.1
  697.4 6.1 collective-permute-done.1
  708.9 6.1 collective-permute-done.1
  720.4 6.1 collective-permute-done.1
  735.5 9.1 %all_to_all.66 = f32[4,2,1,16,256]{4,3,2,1,0:T(8,128)S(1)} all-to-all(f32[4,2,1,16,256]{4,3,2,1,0:T(8,128)S(1)} %maximum_bitcast_fusion), channel_id=1, replica_groups=mesh['tm'=8,'sx'=8,'sy'=4] {'sy'}, dimensions={0} | all-to-all | bytes 262144 | tf_op jit(solution)/shard_map/all_to_all | solution.py:253
  (320 shorter events, 406.9 us)
Async XLA Ops:
  67.2 47.6 %all-to-all-start = ((f32[32,6,2,8,128]{4,3,2,1,0:T(8,128)}), f32[32,6,2,8,128]{4,3,2,1,0:T(8,128)S(1)}, u32[]{:S(2)}, u32[]{:S(2)}) async-start(f32[32,6,2,8,128]{4,3,2,1,0:T(8,128)} %broadcast_in_dim.164), calls=%async_computation | async-start | bytes 3145728 | tf_op jit(solution)/shard_map/all_to_all | solution.py:227
  182.2 6.5 collective-permute-start.4
  183.5 6.8 collective-permute-start.5
  271.2 19.1 %all-to-all-start.4 = ((f32[32,1,2]{2,1,0:T(1,128)}), f32[32,1,2]{2,1,0:T(1,128)S(1)}, u32[]{:S(2)}, u32[]{:S(2)}) async-start(f32[32,1,2]{2,1,0:T(1,128)} %broadcast_in_dim.172), calls=%async_computation.4 | async-start | bytes 32768 | tf_op jit(solution)/shard_map/all_to_all | solution.py:154
  282.0 20.9 %collective-permute-start.11 = (f32[1,64,256]{2,1,0:T(8,128)}, f32[1,64,256]{2,1,0:T(8,128)}, u32[]{:S(2)}, u32[]{:S(2)}) collective-permute-start(f32[1,64,256]{2,1,0:T(8,128)} %fusion.276), channel_id=1, source_target_pairs={{1,0},{2,1},{3,2},{4,3},{5,4},{6,5},{7,6},{8,7},{9,8},{10,9},{11,1... | collective-permute-start | bytes 196616 | tf_op jit(solution)/shard_map/ppermute | solution.py:86
  283.3 19.6 %collective-permute-start.13 = (f32[1,64,256]{2,1,0:T(8,128)}, f32[1,64,256]{2,1,0:T(8,128)}, u32[]{:S(2)}, u32[]{:S(2)}) collective-permute-start(f32[1,64,256]{2,1,0:T(8,128)} %fusion.276), channel_id=1, source_target_pairs={{0,1},{1,2},{2,3},{3,4},{4,5},{5,6},{6,7},{7,8},{8,9},{9,10},{10,1... | collective-permute-start | bytes 196616 | tf_op jit(solution)/shard_map/ppermute | solution.py:85
  297.0 6.9 collective-permute-start.10
  306.3 6.5 collective-permute-start.14
  307.6 6.8 collective-permute-start.15
  326.6 32.1 %all-to-all-start.5 = ((f32[32,1,32,128]{3,2,1,0:T(8,128)}), f32[32,1,32,128]{3,2,1,0:T(8,128)}, u32[]{:S(2)}, u32[]{:S(2)}) async-start(f32[32,1,32,128]{3,2,1,0:T(8,128)} %broadcast_in_dim.173), calls=%async_computation.5 | async-start | bytes 1048576 | tf_op jit(solution)/shard_map/all_to_all | solution.py:266
  365.0 8.0 %collective-permute-start = (f32[16,32,128]{2,1,0:T(8,128)}, f32[16,32,128]{2,1,0:T(8,128)}, u32[]{:S(2)}, u32[]{:S(2)}) collective-permute-start(f32[16,32,128]{2,1,0:T(8,128)} %fusion.331), channel_id=1, source_target_pairs={{0,32},{32,64},{64,96},{96,128},{128,160},{160,192},{192,224},{1,3... | collective-permute-start | bytes 786440 | tf_op jit(solution)/shard_map/while/body/eval_jaxpr/ppermute | solution.py:37
  376.5 8.0 %collective-permute-start = (f32[16,32,128]{2,1,0:T(8,128)}, f32[16,32,128]{2,1,0:T(8,128)}, u32[]{:S(2)}, u32[]{:S(2)}) collective-permute-start(f32[16,32,128]{2,1,0:T(8,128)} %fusion.331), channel_id=1, source_target_pairs={{0,32},{32,64},{64,96},{96,128},{128,160},{160,192},{192,224},{1,3... | collective-permute-start | bytes 786440 | tf_op jit(solution)/shard_map/while/body/eval_jaxpr/ppermute | solution.py:37
  387.9 8.0 %collective-permute-start = (f32[16,32,128]{2,1,0:T(8,128)}, f32[16,32,128]{2,1,0:T(8,128)}, u32[]{:S(2)}, u32[]{:S(2)}) collective-permute-start(f32[16,32,128]{2,1,0:T(8,128)} %fusion.331), channel_id=1, source_target_pairs={{0,32},{32,64},{64,96},{96,128},{128,160},{160,192},{192,224},{1,3... | collective-permute-start | bytes 786440 | tf_op jit(solution)/shard_map/while/body/eval_jaxpr/ppermute | solution.py:37
  399.4 8.0 %collective-permute-start = (f32[16,32,128]{2,1,0:T(8,128)}, f32[16,32,128]{2,1,0:T(8,128)}, u32[]{:S(2)}, u32[]{:S(2)}) collective-permute-start(f32[16,32,128]{2,1,0:T(8,128)} %fusion.331), channel_id=1, source_target_pairs={{0,32},{32,64},{64,96},{96,128},{128,160},{160,192},{192,224},{1,3... | collective-permute-start | bytes 786440 | tf_op jit(solution)/shard_map/while/body/eval_jaxpr/ppermute | solution.py:37
  410.9 8.0 %collective-permute-start = (f32[16,32,128]{2,1,0:T(8,128)}, f32[16,32,128]{2,1,0:T(8,128)}, u32[]{:S(2)}, u32[]{:S(2)}) collective-permute-start(f32[16,32,128]{2,1,0:T(8,128)} %fusion.331), channel_id=1, source_target_pairs={{0,32},{32,64},{64,96},{96,128},{128,160},{160,192},{192,224},{1,3... | collective-permute-start | bytes 786440 | tf_op jit(solution)/shard_map/while/body/eval_jaxpr/ppermute | solution.py:37
  422.4 8.0 %collective-permute-start = (f32[16,32,128]{2,1,0:T(8,128)}, f32[16,32,128]{2,1,0:T(8,128)}, u32[]{:S(2)}, u32[]{:S(2)}) collective-permute-start(f32[16,32,128]{2,1,0:T(8,128)} %fusion.331), channel_id=1, source_target_pairs={{0,32},{32,64},{64,96},{96,128},{128,160},{160,192},{192,224},{1,3... | collective-permute-start | bytes 786440 | tf_op jit(solution)/shard_map/while/body/eval_jaxpr/ppermute | solution.py:37
  433.9 8.0 %collective-permute-start = (f32[16,32,128]{2,1,0:T(8,128)}, f32[16,32,128]{2,1,0:T(8,128)}, u32[]{:S(2)}, u32[]{:S(2)}) collective-permute-start(f32[16,32,128]{2,1,0:T(8,128)} %fusion.331), channel_id=1, source_target_pairs={{0,32},{32,64},{64,96},{96,128},{128,160},{160,192},{192,224},{1,3... | collective-permute-start | bytes 786440 | tf_op jit(solution)/shard_map/while/body/eval_jaxpr/ppermute | solution.py:37
  470.2 6.5 collective-permute-start.19
  471.5 6.8 collective-permute-start.20
  557.5 19.1 %all-to-all-start.8 = ((f32[32,1,2]{2,1,0:T(1,128)}), f32[32,1,2]{2,1,0:T(1,128)S(1)}, u32[]{:S(2)}, u32[]{:S(2)}) async-start(f32[32,1,2]{2,1,0:T(1,128)} %broadcast_in_dim.182), calls=%async_computation.8 | async-start | bytes 32768 | tf_op jit(solution)/shard_map/all_to_all | solution.py:154
  566.8 22.3 %collective-permute-start.26 = (f32[1,64,256]{2,1,0:T(8,128)}, f32[1,64,256]{2,1,0:T(8,128)}, u32[]{:S(2)}, u32[]{:S(2)}) collective-permute-start(f32[1,64,256]{2,1,0:T(8,128)} %get-tuple-element.937), channel_id=1, source_target_pairs={{1,0},{2,1},{3,2},{4,3},{5,4},{6,5},{7,6},{8,7},{9,8},{10,9},{11,1... | collective-permute-start | bytes 196616 | tf_op jit(solution)/shard_map/ppermute | solution.py:86
  568.1 21.0 %collective-permute-start.28 = (f32[1,64,256]{2,1,0:T(8,128)}, f32[1,64,256]{2,1,0:T(8,128)}, u32[]{:S(2)}, u32[]{:S(2)}) collective-permute-start(f32[1,64,256]{2,1,0:T(8,128)} %get-tuple-element.937), channel_id=1, source_target_pairs={{0,1},{1,2},{2,3},{3,4},{4,5},{5,6},{6,7},{7,8},{8,9},{9,10},{10,1... | collective-permute-start | bytes 196616 | tf_op jit(solution)/shard_map/ppermute | solution.py:85
  583.3 6.9 collective-permute-start.25
  593.9 6.8 collective-permute-start.30
  612.9 30.4 %all-to-all-start.9 = ((f32[32,1,32,128]{3,2,1,0:T(8,128)}), f32[32,1,32,128]{3,2,1,0:T(8,128)}, u32[]{:S(2)}, u32[]{:S(2)}) async-start(f32[32,1,32,128]{3,2,1,0:T(8,128)} %broadcast_in_dim.183), calls=%async_computation.9 | async-start | bytes 1048576 | tf_op jit(solution)/shard_map/all_to_all | solution.py:266
  649.5 8.0 %collective-permute-start.1 = (f32[16,32,128]{2,1,0:T(8,128)}, f32[16,32,128]{2,1,0:T(8,128)}, u32[]{:S(2)}, u32[]{:S(2)}) collective-permute-start(f32[16,32,128]{2,1,0:T(8,128)} %fusion.332), channel_id=1, source_target_pairs={{0,32},{32,64},{64,96},{96,128},{128,160},{160,192},{192,224},{1,3... | collective-permute-start | bytes 786440 | tf_op jit(solution)/shard_map/while/body/eval_jaxpr/ppermute | solution.py:37
  661.0 8.0 %collective-permute-start.1 = (f32[16,32,128]{2,1,0:T(8,128)}, f32[16,32,128]{2,1,0:T(8,128)}, u32[]{:S(2)}, u32[]{:S(2)}) collective-permute-start(f32[16,32,128]{2,1,0:T(8,128)} %fusion.332), channel_id=1, source_target_pairs={{0,32},{32,64},{64,96},{96,128},{128,160},{160,192},{192,224},{1,3... | collective-permute-start | bytes 786440 | tf_op jit(solution)/shard_map/while/body/eval_jaxpr/ppermute | solution.py:37
  672.5 8.0 %collective-permute-start.1 = (f32[16,32,128]{2,1,0:T(8,128)}, f32[16,32,128]{2,1,0:T(8,128)}, u32[]{:S(2)}, u32[]{:S(2)}) collective-permute-start(f32[16,32,128]{2,1,0:T(8,128)} %fusion.332), channel_id=1, source_target_pairs={{0,32},{32,64},{64,96},{96,128},{128,160},{160,192},{192,224},{1,3... | collective-permute-start | bytes 786440 | tf_op jit(solution)/shard_map/while/body/eval_jaxpr/ppermute | solution.py:37
  684.0 8.0 %collective-permute-start.1 = (f32[16,32,128]{2,1,0:T(8,128)}, f32[16,32,128]{2,1,0:T(8,128)}, u32[]{:S(2)}, u32[]{:S(2)}) collective-permute-start(f32[16,32,128]{2,1,0:T(8,128)} %fusion.332), channel_id=1, source_target_pairs={{0,32},{32,64},{64,96},{96,128},{128,160},{160,192},{192,224},{1,3... | collective-permute-start | bytes 786440 | tf_op jit(solution)/shard_map/while/body/eval_jaxpr/ppermute | solution.py:37
  695.5 8.0 %collective-permute-start.1 = (f32[16,32,128]{2,1,0:T(8,128)}, f32[16,32,128]{2,1,0:T(8,128)}, u32[]{:S(2)}, u32[]{:S(2)}) collective-permute-start(f32[16,32,128]{2,1,0:T(8,128)} %fusion.332), channel_id=1, source_target_pairs={{0,32},{32,64},{64,96},{96,128},{128,160},{160,192},{192,224},{1,3... | collective-permute-start | bytes 786440 | tf_op jit(solution)/shard_map/while/body/eval_jaxpr/ppermute | solution.py:37
  707.0 8.0 %collective-permute-start.1 = (f32[16,32,128]{2,1,0:T(8,128)}, f32[16,32,128]{2,1,0:T(8,128)}, u32[]{:S(2)}, u32[]{:S(2)}) collective-permute-start(f32[16,32,128]{2,1,0:T(8,128)} %fusion.332), channel_id=1, source_target_pairs={{0,32},{32,64},{64,96},{96,128},{128,160},{160,192},{192,224},{1,3... | collective-permute-start | bytes 786440 | tf_op jit(solution)/shard_map/while/body/eval_jaxpr/ppermute | solution.py:37
  718.4 8.0 %collective-permute-start.1 = (f32[16,32,128]{2,1,0:T(8,128)}, f32[16,32,128]{2,1,0:T(8,128)}, u32[]{:S(2)}, u32[]{:S(2)}) collective-permute-start(f32[16,32,128]{2,1,0:T(8,128)} %fusion.332), channel_id=1, source_target_pairs={{0,32},{32,64},{64,96},{96,128},{128,160},{160,192},{192,224},{1,3... | collective-permute-start | bytes 786440 | tf_op jit(solution)/shard_map/while/body/eval_jaxpr/ppermute | solution.py:37
  (49 other events, 401.1 us)

commit v6 on v5

--- a/solution.py
+++ b/solution.py
@@ -370,17 +370,6 @@
         )
     )
     share = initial_rows.shape[0]
-    def own_chain(turn_no, carried):
-        coarse_state, own_state, own_image = carried
-        coarse_image = coarse_step(coarse_state)
-        mine = turn_no == slice_index
-        own_state = jnp.where(mine, coarse_state, own_state)
-        own_image = jnp.where(mine, coarse_image, own_image)
-        return (coarse_image, own_state, own_image)
-
-    _, coarse_state, coarse_image = lax.fori_loop(
-        0, slices, own_chain, (start_coarse, start_coarse, start_coarse)
-    )
     starts = jnp.where(slice_index == 0, initial_rows, prolong_rows(coarse_state, share))
     previous_image = coarse_image
     ends = starts

time: 759 us -> 742 us (0.978)
  other arithmetic: 175 us -> 154 us
    select_n x8 -> x0, other arithmetic: 30.2 us -> none  [own_chain(): own_image = jnp.where(mine, coarse_image, own_image)]
    sub x0 -> x7, other arithmetic: none -> 15.6 us  [coarse_step(): return coarse_state - balance / slope_sum]
    div x27 -> x26, other arithmetic: 35.9 us -> 29.9 us  [fractional(): water_mobility / mobility]
  transfers between devices with their start and end apart: 48 -> 48, of which waited for: 41 -> 41; matrix products, arithmetic and copies ran while one was open for 3% -> 2% of each run, Pallas kernels for 0% -> 0%
where the time goes in v6:
time: 742 us; the launch traced here: 729 us
  starting transfers between devices  176 us (24%)
  waiting for transfers between devices  176 us (24%)
  other arithmetic  154 us (21%)
  blocking collectives  106 us (14%)
  local copies, waits for them, and re-layouts  95 us (13%)
  between operations  20.9 us (3%)
    ppermute x15, waiting for transfers between devices, passed_along(): lax.ppermute(value, axis, [(source, source + steps) for source in range(i...  88.7 us
    all_to_all x4, blocking collectives, global_sums(): gathered = lax.all_to_all(packed, ('sx', 'sy'), 0, 0, tiled=True)  84.5 us
    ppermute x14, starting transfers between devices, row_halo(): before = lax.ppermute(volume[-1:], ROW_AXES, up)  66.7 us
    all_to_all x1, waiting for transfers between devices, gather_grid(): gathered = lax.all_to_all(packed, ('sx', 'sy'), 0, 0, tiled=True)  37.2 us
    all_to_all x2, starting transfers between devices, restrict_rows(): gathered = lax.all_to_all(packed, ROW_AXES, 0, 0, tiled=True)  34.8 us
    add x14, other arithmetic, relay_round(): return passed_along(coarse_step(coarse_state) + corrections, 'tm', 1)  34 us
    div x26, other arithmetic, fractional(): water_mobility / mobility  29.9 us
    ppermute x15, starting transfers between devices, passed_along(): lax.ppermute(value, axis, [(source, source + steps) for source in range(i...  28.7 us
  transfers between devices with their start and end apart: 48, of which 41 were waited for; matrix products, arithmetic and copies ran while one was open for 2% of the time, Pallas kernels for 0%

profile of v6, /device:TPU:6, one launch (start us, length us, event | category | flops | bytes accessed | tf_op | source)
XLA Modules:
  0.0 729.0 jit_solution(17216351910287997328)
XLA Ops:
  0.7 6.3 reshape.504
  53.5 12.3 %all_to_all.61 = f32[4,6,1,16,256]{4,3,1,2,0:T(8,128)S(1)} all-to-all(f32[4,6,1,16,256]{4,3,1,2,0:T(8,128)S(1)} %copy.39), channel_id=1, replica_groups=mesh['tm'=8,'sx'=8,'sy'=4] {'sy'}, dimensions={0} | all-to-all | bytes 786432 | tf_op jit(solution)/shard_map/all_to_all | solution.py:244
  67.2 9.6 %all-to-all-start = ((f32[32,6,2,8,128]{4,3,2,1,0:T(8,128)}), f32[32,6,2,8,128]{4,3,2,1,0:T(8,128)S(1)}, u32[]{:S(2)}, u32[]{:S(2)}) async-start(f32[32,6,2,8,128]{4,3,2,1,0:T(8,128)} %broadcast_in_dim.164), calls=%async_computation | async-start | bytes 3145728 | tf_op jit(solution)/shard_map/all_to_all | solution.py:227
  77.5 37.2 %all-to-all-done = f32[32,6,2,8,128]{4,3,2,1,0:T(8,128)S(1)} async-done(((f32[32,6,2,8,128]{4,3,2,1,0:T(8,128)}), f32[32,6,2,8,128]{4,3,2,1,0:T(8,128)S(1)}, u32[]{:S(2)}, u32[]{:S(2)}) %all-to-all-start) | async-done | bytes 1572896 | tf_op jit(solution)/shard_map/all_to_all | solution.py:227
  118.4 20.2 %while.37 = (s32[]{:T(128)}, f32[16,32,128]{2,1,0:T(8,128)}, s32[]{:T(128)}, f32[16,32,128]{2,1,0:T(8,128)S(1)}, f32[16,32,128]{2,1,0:T(8,128)S(1)}, /*index=5*/...) while((s32[]{:T(128)}, f32[16,32,128]{2,1,0:T(8,128)}, ...), condition=%wide.region_5.6_spmd, body=%wide.region_4.5_spmd.sunk | while | flops 4784130 | bytes 4980885 | solution.py:356
  167.7 24.0 %all_to_all.62 = f32[32,1,2]{2,1,0:T(1,128)S(1)} all-to-all(f32[32,1,2]{2,1,0:T(1,128)S(1)} %broadcast_in_dim.170), channel_id=1, replica_groups=mesh['tm'=8,'sx'=8,'sy'=4] {'sx','sy'}, dimensions={0} | all-to-all | bytes 512 | tf_op jit(solution)/shard_map/all_to_all | solution.py:154
  207.5 18.9 %all_to_all.63 = f32[32,1,2]{2,1,0:T(1,128)S(1)} all-to-all(f32[32,1,2]{2,1,0:T(1,128)S(1)} %broadcast_in_dim.171), channel_id=1, replica_groups=mesh['tm'=8,'sx'=8,'sy'=4] {'sx','sy'}, dimensions={0} | all-to-all | bytes 512 | tf_op jit(solution)/shard_map/all_to_all | solution.py:154
  245.3 9.3 %all-to-all-start.4 = ((f32[32,1,2]{2,1,0:T(1,128)}), f32[32,1,2]{2,1,0:T(1,128)S(1)}, u32[]{:S(2)}, u32[]{:S(2)}) async-start(f32[32,1,2]{2,1,0:T(1,128)} %broadcast_in_dim.172), calls=%async_computation.4 | async-start | bytes 32768 | tf_op jit(solution)/shard_map/all_to_all | solution.py:154
  290.5 6.3 reshape.510
  300.5 18.3 %all-to-all-start.5 = ((f32[32,1,32,128]{3,2,1,0:T(8,128)}), f32[32,1,32,128]{3,2,1,0:T(8,128)}, u32[]{:S(2)}, u32[]{:S(2)}) async-start(f32[32,1,32,128]{3,2,1,0:T(8,128)} %broadcast_in_dim.173), calls=%async_computation.5 | async-start | bytes 1048576 | tf_op jit(solution)/shard_map/all_to_all | solution.py:266
  321.2 11.4 %all-to-all-done.5 = f32[32,1,32,128]{3,2,1,0:T(8,128)} async-done(((f32[32,1,32,128]{3,2,1,0:T(8,128)}), f32[32,1,32,128]{3,2,1,0:T(8,128)}, u32[]{:S(2)}, u32[]{:S(2)}) %all-to-all-start.5) | async-done | bytes 524320 | tf_op jit(solution)/shard_map/all_to_all | solution.py:266
  337.5 80.5 %while.38 = (s32[]{:T(128)}, f32[16,32,128]{2,1,0:T(8,128)}, pred[]{:T(512)}, f32[16,32,128]{2,1,0:T(8,128)S(1)}, f32[16,32,128]{2,1,0:T(8,128)S(1)}, /*index=5*...) while((s32[]{:T(128)}, f32[16,32,128]{2,1,0:T(8,128)}, ...), condition=%wide.region_18.20_spmd, body=%wide.region_17.19_spmd.sunk | while | flops 4980738 | bytes 6815951 | solution.py:352
  342.9 6.1 collective-permute-done
  354.4 6.1 collective-permute-done
  365.9 6.1 collective-permute-done
  377.4 6.1 collective-permute-done
  388.9 6.1 collective-permute-done
  400.4 6.1 collective-permute-done
  411.9 6.1 collective-permute-done
  464.5 22.8 %all_to_all.64 = f32[32,1,2]{2,1,0:T(1,128)S(1)} all-to-all(f32[32,1,2]{2,1,0:T(1,128)S(1)} %broadcast_in_dim.180), channel_id=1, replica_groups=mesh['tm'=8,'sx'=8,'sy'=4] {'sx','sy'}, dimensions={0} | all-to-all | bytes 512 | tf_op jit(solution)/shard_map/all_to_all | solution.py:154
  503.1 18.9 %all_to_all.65 = f32[32,1,2]{2,1,0:T(1,128)S(1)} all-to-all(f32[32,1,2]{2,1,0:T(1,128)S(1)} %broadcast_in_dim.181), channel_id=1, replica_groups=mesh['tm'=8,'sx'=8,'sy'=4] {'sx','sy'}, dimensions={0} | all-to-all | bytes 512 | tf_op jit(solution)/shard_map/all_to_all | solution.py:154
  540.9 9.3 %all-to-all-start.8 = ((f32[32,1,2]{2,1,0:T(1,128)}), f32[32,1,2]{2,1,0:T(1,128)S(1)}, u32[]{:S(2)}, u32[]{:S(2)}) async-start(f32[32,1,2]{2,1,0:T(1,128)} %broadcast_in_dim.182), calls=%async_computation.8 | async-start | bytes 32768 | tf_op jit(solution)/shard_map/all_to_all | solution.py:154
  586.2 6.3 reshape.512
  596.1 16.6 %all-to-all-start.9 = ((f32[32,1,32,128]{3,2,1,0:T(8,128)}), f32[32,1,32,128]{3,2,1,0:T(8,128)}, u32[]{:S(2)}, u32[]{:S(2)}) async-start(f32[32,1,32,128]{3,2,1,0:T(8,128)} %broadcast_in_dim.183), calls=%async_computation.9 | async-start | bytes 1048576 | tf_op jit(solution)/shard_map/all_to_all | solution.py:266
  613.4 13.1 %all-to-all-done.9 = f32[32,1,32,128]{3,2,1,0:T(8,128)} async-done(((f32[32,1,32,128]{3,2,1,0:T(8,128)}), f32[32,1,32,128]{3,2,1,0:T(8,128)}, u32[]{:S(2)}, u32[]{:S(2)}) %all-to-all-start.9) | async-done | bytes 524320 | tf_op jit(solution)/shard_map/all_to_all | solution.py:266
  629.3 80.4 %while.39 = (s32[]{:T(128)}, f32[16,32,128]{2,1,0:T(8,128)}, pred[]{:T(512)}, f32[16,32,128]{2,1,0:T(8,128)S(1)}, f32[16,32,128]{2,1,0:T(8,128)S(1)}, /*index=5*...) while((s32[]{:T(128)}, f32[16,32,128]{2,1,0:T(8,128)}, ...), condition=%wide.region_31.33_spmd, body=%wide.region_30.32_spmd.sunk | while | flops 4980738 | bytes 6815951 | solution.py:352
  634.7 6.1 collective-permute-done.1
  657.7 6.1 collective-permute-done.1
  669.2 6.1 collective-permute-done.1
  680.6 6.1 collective-permute-done.1
  692.1 6.1 collective-permute-done.1
  718.8 9.1 %all_to_all.66 = f32[4,2,1,16,256]{4,3,2,1,0:T(8,128)S(1)} all-to-all(f32[4,2,1,16,256]{4,3,2,1,0:T(8,128)S(1)} %maximum_bitcast_fusion), channel_id=1, replica_groups=mesh['tm'=8,'sx'=8,'sy'=4] {'sy'}, dimensions={0} | all-to-all | bytes 262144 | tf_op jit(solution)/shard_map/all_to_all | solution.py:253
  (315 shorter events, 385.4 us)
Async XLA Ops:
  67.2 47.6 %all-to-all-start = ((f32[32,6,2,8,128]{4,3,2,1,0:T(8,128)}), f32[32,6,2,8,128]{4,3,2,1,0:T(8,128)S(1)}, u32[]{:S(2)}, u32[]{:S(2)}) async-start(f32[32,6,2,8,128]{4,3,2,1,0:T(8,128)} %broadcast_in_dim.164), calls=%async_computation | async-start | bytes 3145728 | tf_op jit(solution)/shard_map/all_to_all | solution.py:227
  149.3 6.9 collective-permute-start.3
  156.5 6.8 collective-permute-start.4
  157.8 6.9 collective-permute-start.5
  245.3 19.1 %all-to-all-start.4 = ((f32[32,1,2]{2,1,0:T(1,128)}), f32[32,1,2]{2,1,0:T(1,128)S(1)}, u32[]{:S(2)}, u32[]{:S(2)}) async-start(f32[32,1,2]{2,1,0:T(1,128)} %broadcast_in_dim.172), calls=%async_computation.4 | async-start | bytes 32768 | tf_op jit(solution)/shard_map/all_to_all | solution.py:154
  256.1 20.7 %collective-permute-start.11 = (f32[1,64,256]{2,1,0:T(8,128)}, f32[1,64,256]{2,1,0:T(8,128)}, u32[]{:S(2)}, u32[]{:S(2)}) collective-permute-start(f32[1,64,256]{2,1,0:T(8,128)} %fusion.298), channel_id=1, source_target_pairs={{1,0},{2,1},{3,2},{4,3},{5,4},{6,5},{7,6},{8,7},{9,8},{10,9},{11,1... | collective-permute-start | bytes 196616 | tf_op jit(solution)/shard_map/ppermute | solution.py:86
  257.4 19.4 %collective-permute-start.13 = (f32[1,64,256]{2,1,0:T(8,128)}, f32[1,64,256]{2,1,0:T(8,128)}, u32[]{:S(2)}, u32[]{:S(2)}) collective-permute-start(f32[1,64,256]{2,1,0:T(8,128)} %fusion.298), channel_id=1, source_target_pairs={{0,1},{1,2},{2,3},{3,4},{4,5},{5,6},{6,7},{7,8},{8,9},{9,10},{10,1... | collective-permute-start | bytes 196616 | tf_op jit(solution)/shard_map/ppermute | solution.py:85
  270.9 6.9 collective-permute-start.10
  280.3 6.5 collective-permute-start.14
  281.6 6.8 collective-permute-start.15
  300.5 32.1 %all-to-all-start.5 = ((f32[32,1,32,128]{3,2,1,0:T(8,128)}), f32[32,1,32,128]{3,2,1,0:T(8,128)}, u32[]{:S(2)}, u32[]{:S(2)}) async-start(f32[32,1,32,128]{3,2,1,0:T(8,128)} %broadcast_in_dim.173), calls=%async_computation.5 | async-start | bytes 1048576 | tf_op jit(solution)/shard_map/all_to_all | solution.py:266
  341.0 8.0 %collective-permute-start = (f32[16,32,128]{2,1,0:T(8,128)}, f32[16,32,128]{2,1,0:T(8,128)}, u32[]{:S(2)}, u32[]{:S(2)}) collective-permute-start(f32[16,32,128]{2,1,0:T(8,128)} %fusion.355), channel_id=1, source_target_pairs={{0,32},{32,64},{64,96},{96,128},{128,160},{160,192},{192,224},{1,3... | collective-permute-start | bytes 786440 | tf_op jit(solution)/shard_map/while/body/eval_jaxpr/ppermute | solution.py:37
  352.5 8.0 %collective-permute-start = (f32[16,32,128]{2,1,0:T(8,128)}, f32[16,32,128]{2,1,0:T(8,128)}, u32[]{:S(2)}, u32[]{:S(2)}) collective-permute-start(f32[16,32,128]{2,1,0:T(8,128)} %fusion.355), channel_id=1, source_target_pairs={{0,32},{32,64},{64,96},{96,128},{128,160},{160,192},{192,224},{1,3... | collective-permute-start | bytes 786440 | tf_op jit(solution)/shard_map/while/body/eval_jaxpr/ppermute | solution.py:37
  364.0 8.0 %collective-permute-start = (f32[16,32,128]{2,1,0:T(8,128)}, f32[16,32,128]{2,1,0:T(8,128)}, u32[]{:S(2)}, u32[]{:S(2)}) collective-permute-start(f32[16,32,128]{2,1,0:T(8,128)} %fusion.355), channel_id=1, source_target_pairs={{0,32},{32,64},{64,96},{96,128},{128,160},{160,192},{192,224},{1,3... | collective-permute-start | bytes 786440 | tf_op jit(solution)/shard_map/while/body/eval_jaxpr/ppermute | solution.py:37
  375.5 8.0 %collective-permute-start = (f32[16,32,128]{2,1,0:T(8,128)}, f32[16,32,128]{2,1,0:T(8,128)}, u32[]{:S(2)}, u32[]{:S(2)}) collective-permute-start(f32[16,32,128]{2,1,0:T(8,128)} %fusion.355), channel_id=1, source_target_pairs={{0,32},{32,64},{64,96},{96,128},{128,160},{160,192},{192,224},{1,3... | collective-permute-start | bytes 786440 | tf_op jit(solution)/shard_map/while/body/eval_jaxpr/ppermute | solution.py:37
  387.0 8.0 %collective-permute-start = (f32[16,32,128]{2,1,0:T(8,128)}, f32[16,32,128]{2,1,0:T(8,128)}, u32[]{:S(2)}, u32[]{:S(2)}) collective-permute-start(f32[16,32,128]{2,1,0:T(8,128)} %fusion.355), channel_id=1, source_target_pairs={{0,32},{32,64},{64,96},{96,128},{128,160},{160,192},{192,224},{1,3... | collective-permute-start | bytes 786440 | tf_op jit(solution)/shard_map/while/body/eval_jaxpr/ppermute | solution.py:37
  398.5 8.0 %collective-permute-start = (f32[16,32,128]{2,1,0:T(8,128)}, f32[16,32,128]{2,1,0:T(8,128)}, u32[]{:S(2)}, u32[]{:S(2)}) collective-permute-start(f32[16,32,128]{2,1,0:T(8,128)} %fusion.355), channel_id=1, source_target_pairs={{0,32},{32,64},{64,96},{96,128},{128,160},{160,192},{192,224},{1,3... | collective-permute-start | bytes 786440 | tf_op jit(solution)/shard_map/while/body/eval_jaxpr/ppermute | solution.py:37
  410.0 8.0 %collective-permute-start = (f32[16,32,128]{2,1,0:T(8,128)}, f32[16,32,128]{2,1,0:T(8,128)}, u32[]{:S(2)}, u32[]{:S(2)}) collective-permute-start(f32[16,32,128]{2,1,0:T(8,128)} %fusion.355), channel_id=1, source_target_pairs={{0,32},{32,64},{64,96},{96,128},{128,160},{160,192},{192,224},{1,3... | collective-permute-start | bytes 786440 | tf_op jit(solution)/shard_map/while/body/eval_jaxpr/ppermute | solution.py:37
  454.7 6.8 collective-permute-start.20
  540.9 19.1 %all-to-all-start.8 = ((f32[32,1,2]{2,1,0:T(1,128)}), f32[32,1,2]{2,1,0:T(1,128)S(1)}, u32[]{:S(2)}, u32[]{:S(2)}) async-start(f32[32,1,2]{2,1,0:T(1,128)} %broadcast_in_dim.182), calls=%async_computation.8 | async-start | bytes 32768 | tf_op jit(solution)/shard_map/all_to_all | solution.py:154
  550.2 22.2 %collective-permute-start.26 = (f32[1,64,256]{2,1,0:T(8,128)}, f32[1,64,256]{2,1,0:T(8,128)}, u32[]{:S(2)}, u32[]{:S(2)}) collective-permute-start(f32[1,64,256]{2,1,0:T(8,128)} %get-tuple-element.731), channel_id=1, source_target_pairs={{1,0},{2,1},{3,2},{4,3},{5,4},{6,5},{7,6},{8,7},{9,8},{10,9},{11,1... | collective-permute-start | bytes 196616 | tf_op jit(solution)/shard_map/ppermute | solution.py:86
  551.5 20.9 %collective-permute-start.28 = (f32[1,64,256]{2,1,0:T(8,128)}, f32[1,64,256]{2,1,0:T(8,128)}, u32[]{:S(2)}, u32[]{:S(2)}) collective-permute-start(f32[1,64,256]{2,1,0:T(8,128)} %get-tuple-element.731), channel_id=1, source_target_pairs={{0,1},{1,2},{2,3},{3,4},{4,5},{5,6},{6,7},{7,8},{8,9},{9,10},{10,1... | collective-permute-start | bytes 196616 | tf_op jit(solution)/shard_map/ppermute | solution.py:85
  566.5 6.9 collective-permute-start.25
  577.2 6.8 collective-permute-start.30
  596.1 30.4 %all-to-all-start.9 = ((f32[32,1,32,128]{3,2,1,0:T(8,128)}), f32[32,1,32,128]{3,2,1,0:T(8,128)}, u32[]{:S(2)}, u32[]{:S(2)}) async-start(f32[32,1,32,128]{3,2,1,0:T(8,128)} %broadcast_in_dim.183), calls=%async_computation.9 | async-start | bytes 1048576 | tf_op jit(solution)/shard_map/all_to_all | solution.py:266
  632.8 8.0 %collective-permute-start.1 = (f32[16,32,128]{2,1,0:T(8,128)}, f32[16,32,128]{2,1,0:T(8,128)}, u32[]{:S(2)}, u32[]{:S(2)}) collective-permute-start(f32[16,32,128]{2,1,0:T(8,128)} %fusion.356), channel_id=1, source_target_pairs={{0,32},{32,64},{64,96},{96,128},{128,160},{160,192},{192,224},{1,3... | collective-permute-start | bytes 786440 | tf_op jit(solution)/shard_map/while/body/eval_jaxpr/ppermute | solution.py:37
  644.3 8.0 %collective-permute-start.1 = (f32[16,32,128]{2,1,0:T(8,128)}, f32[16,32,128]{2,1,0:T(8,128)}, u32[]{:S(2)}, u32[]{:S(2)}) collective-permute-start(f32[16,32,128]{2,1,0:T(8,128)} %fusion.356), channel_id=1, source_target_pairs={{0,32},{32,64},{64,96},{96,128},{128,160},{160,192},{192,224},{1,3... | collective-permute-start | bytes 786440 | tf_op jit(solution)/shard_map/while/body/eval_jaxpr/ppermute | solution.py:37
  655.7 8.0 %collective-permute-start.1 = (f32[16,32,128]{2,1,0:T(8,128)}, f32[16,32,128]{2,1,0:T(8,128)}, u32[]{:S(2)}, u32[]{:S(2)}) collective-permute-start(f32[16,32,128]{2,1,0:T(8,128)} %fusion.356), channel_id=1, source_target_pairs={{0,32},{32,64},{64,96},{96,128},{128,160},{160,192},{192,224},{1,3... | collective-permute-start | bytes 786440 | tf_op jit(solution)/shard_map/while/body/eval_jaxpr/ppermute | solution.py:37
  667.2 8.0 %collective-permute-start.1 = (f32[16,32,128]{2,1,0:T(8,128)}, f32[16,32,128]{2,1,0:T(8,128)}, u32[]{:S(2)}, u32[]{:S(2)}) collective-permute-start(f32[16,32,128]{2,1,0:T(8,128)} %fusion.356), channel_id=1, source_target_pairs={{0,32},{32,64},{64,96},{96,128},{128,160},{160,192},{192,224},{1,3... | collective-permute-start | bytes 786440 | tf_op jit(solution)/shard_map/while/body/eval_jaxpr/ppermute | solution.py:37
  678.7 8.0 %collective-permute-start.1 = (f32[16,32,128]{2,1,0:T(8,128)}, f32[16,32,128]{2,1,0:T(8,128)}, u32[]{:S(2)}, u32[]{:S(2)}) collective-permute-start(f32[16,32,128]{2,1,0:T(8,128)} %fusion.356), channel_id=1, source_target_pairs={{0,32},{32,64},{64,96},{96,128},{128,160},{160,192},{192,224},{1,3... | collective-permute-start | bytes 786440 | tf_op jit(solution)/shard_map/while/body/eval_jaxpr/ppermute | solution.py:37
  690.2 8.0 %collective-permute-start.1 = (f32[16,32,128]{2,1,0:T(8,128)}, f32[16,32,128]{2,1,0:T(8,128)}, u32[]{:S(2)}, u32[]{:S(2)}) collective-permute-start(f32[16,32,128]{2,1,0:T(8,128)} %fusion.356), channel_id=1, source_target_pairs={{0,32},{32,64},{64,96},{96,128},{128,160},{160,192},{192,224},{1,3... | collective-permute-start | bytes 786440 | tf_op jit(solution)/shard_map/while/body/eval_jaxpr/ppermute | solution.py:37
  701.7 8.0 %collective-permute-start.1 = (f32[16,32,128]{2,1,0:T(8,128)}, f32[16,32,128]{2,1,0:T(8,128)}, u32[]{:S(2)}, u32[]{:S(2)}) collective-permute-start(f32[16,32,128]{2,1,0:T(8,128)} %fusion.356), channel_id=1, source_target_pairs={{0,32},{32,64},{64,96},{96,128},{128,160},{160,192},{192,224},{1,3... | collective-permute-start | bytes 786440 | tf_op jit(solution)/shard_map/while/body/eval_jaxpr/ppermute | solution.py:37
  (49 other events, 402.6 us)

commit v7 on v6

--- a/solution.py
+++ b/solution.py
@@ -58,6 +58,43 @@
         volume[:, None, :, None, :, None], (first, 2, second, 2, third, 2)
     )
     return spread_out.reshape(2 * first, 2 * second, 2 * third)
+
+
+def pair_matrix(count):
+    rows = lax.broadcasted_iota(jnp.int32, (count, 2 * count), 0)
+    cols = lax.broadcasted_iota(jnp.int32, (count, 2 * count), 1)
+    return (cols // 2 == rows).astype(jnp.float32)
+
+
+def sum_pairs_yz(volume):
+    length_y, depth_z = volume.shape[-2:]
+    lead = volume.shape[:-2]
+    flat = volume.reshape((-1, length_y, depth_z))
+    half_z = jnp.einsum("bkz,wz->bkw", flat, pair_matrix(depth_z // 2), precision=lax.Precision.HIGHEST)
+    half_y = jnp.einsum("yk,bkw->byw", pair_matrix(length_y // 2), half_z, precision=lax.Precision.HIGHEST)
+    return half_y.reshape(lead + (length_y // 2, depth_z // 2))
+
+
+def spread_yz(volume):
+    length_y, depth_z = volume.shape[-2:]
+    lead = volume.shape[:-2]
+    flat = volume.reshape((-1, length_y, depth_z))
+    wide_z = jnp.einsum("bkz,zw->bkw", flat, pair_matrix(depth_z), precision=lax.Precision.HIGHEST)
+    wide_y = jnp.einsum("ky,bkw->byw", pair_matrix(length_y), wide_z, precision=lax.Precision.HIGHEST)
+    return wide_y.reshape(lead + (2 * length_y, 2 * depth_z))
+
+
+def restrict_blocks(volume):
+    fields, length_x, length_y, depth_z = volume.shape
+    paired_x = volume.reshape(fields, length_x // 2, 2, length_y, depth_z).sum(axis=2)
+    return sum_pairs_yz(paired_x) / 8.0
+
+
+def prolong_blocks(volume):
+    fields, length_x, length_y, depth_z = volume.shape
+    spread = spread_yz(volume)
+    spread = jnp.broadcast_to(spread[:, :, None], (fields, length_x, 2) + spread.shape[2:])
+    return spread.reshape((fields, 2 * length_x) + spread.shape[3:])
 
 
 def pad_depth(volume):
@@ -260,7 +297,7 @@
 
 def restrict_rows(rows):
     share, length_y, depth_z = rows.shape
-    partial = rows.reshape(share, length_y // 2, 2, depth_z // 2, 2).sum(axis=(2, 4))
+    partial = sum_pairs_yz(rows)
     count = lax.axis_size("sx") * lax.axis_size("sy")
     packed = jnp.broadcast_to(partial[None], (count,) + partial.shape)
     gathered = lax.all_to_all(packed, ROW_AXES, 0, 0, tiled=True)
@@ -270,10 +307,7 @@
 
 def prolong_rows(whole, share):
     coarse_rows = (row_index() * share + jnp.arange(share)) // 2
-    picked = jnp.take(whole, coarse_rows, axis=0)
-    count, length_y, depth_z = picked.shape
-    spread_out = jnp.broadcast_to(picked[:, :, None, :, None], (count, length_y, 2, depth_z, 2))
-    return spread_out.reshape(count, 2 * length_y, 2 * depth_z)
+    return spread_yz(jnp.take(whole, coarse_rows, axis=0))
 
 
 def whole_faces(volume):
@@ -287,20 +321,8 @@
     slice_index = lax.axis_index("tm")
     water_block = lookup(rock_type, water_endpoint)
     oil_block = lookup(rock_type, oil_endpoint)
-    start_block = restrict(initial_saturation)
-    block_shape = start_block.shape
-    whole = gather_grid(
-        jnp.stack(
-            [
-                start_block,
-                restrict(permeability),
-                restrict(porosity),
-                restrict(source_rate),
-                water_block,
-                oil_block,
-            ]
-        )
-    )
+    restricted = restrict_blocks(jnp.stack([initial_saturation, permeability, porosity, source_rate]))
+    whole = gather_grid(jnp.concatenate([restricted, jnp.stack([water_block, oil_block])]))
     start_coarse, permeability_upscaled, poro_coarse, source_coarse, water_coarse, oil_coarse = (
         whole[k] for k in range(6)
     )
@@ -357,17 +379,9 @@
         0, slice_index, lambda turn_no, state: coarse_step(state), start_coarse
     )
     coarse_image = coarse_step(coarse_state)
+    water_fine, oil_fine = prolong_blocks(jnp.stack([water_block, oil_block]))
     initial_rows, permeability, porosity, source_rate, water_fine, oil_fine = to_rows(
-        jnp.stack(
-            [
-                initial_saturation,
-                permeability,
-                porosity,
-                source_rate,
-                prolong(water_block),
-                prolong(oil_block),
-            ]
-        )
+        jnp.stack([initial_saturation, permeability, porosity, source_rate, water_fine, oil_fine])
     )
     share = initial_rows.shape[0]
     starts = jnp.where(slice_index == 0, initial_rows, prolong_rows(coarse_state, share))

time: 742 us -> 655 us (0.88); the launches traced: 729 us -> 649 us
  local copies, waits for them, and re-layouts: 95 us -> 28 us
  other arithmetic: 154 us -> 127 us
  waiting for transfers between devices: 176 us -> 191 us
  blocking collectives: 106 us -> 96.2 us
    reshape x6 -> x0, local copies, waits for them, and re-layouts: 35.4 us -> none  [the longest x4 22.9 us: restrict(): volume.reshape(volume.shape[0] // 2, 2, volume.shape[1] // 2, 2, volume.s...]
    broadcast_in_dim x10 -> x2, local copies, waits for them, and re-layouts: 33 us -> 0.01 us  [prolong_blocks(): jnp.broadcast_to(spread[:, :, None], (fields, length_x, 2) + spread.shape...]
    reduce_sum x6 -> x1, other arithmetic: 15.8 us -> 0.02 us  [restrict_blocks(): volume.reshape(fields, length_x // 2, 2, length_y, depth_z).sum(axis=2)]
    all_to_all x1 -> x0, blocking collectives: 12.3 us -> none  [to_rows(): got = lax.all_to_all(packed, 'sy', 0, 0, tiled=True)]
    ppermute x14, waiting for transfers between devices: 3.19 us -> 11.2 us  [row_halo(): after = lax.ppermute(volume[:1], ROW_AXES, down)]
    all_to_all x0 -> x1, waiting for transfers between devices: none -> 7.61 us  [to_rows(): got = lax.all_to_all(packed, 'sy', 0, 0, tiled=True)]
    unnamed x74 -> x168, local copies, waits for them, and re-layouts: 3.01 us -> 10.5 us
    div x26 -> x25, other arithmetic: 29.9 us -> 27.5 us  [fractional(): water_mobility / mobility]
  transfers between devices with their start and end apart: 48 -> 49, of which waited for: 41 -> 43; matrix products, arithmetic and copies ran while one was open for 2% -> 2% of each run, Pallas kernels for 0% -> 0%
where the time goes in v7:
time: 655 us; the launch traced here: 649 us
  waiting for transfers between devices  191 us (29%)
  starting transfers between devices  179 us (27%)
  other arithmetic  127 us (19%)
  blocking collectives  96.2 us (15%)
  local copies, waits for them, and re-layouts  28 us (4%)
  between operations  21.9 us (3%)
  matrix products  6.73 us (1%)
    ppermute x15, waiting for transfers between devices, passed_along(): lax.ppermute(value, axis, [(source, source + steps) for source in range(i...  88.7 us
    all_to_all x4, blocking collectives, global_sums(): gathered = lax.all_to_all(packed, ('sx', 'sy'), 0, 0, tiled=True)  87 us
    ppermute x14, starting transfers between devices, row_halo(): before = lax.ppermute(volume[-1:], ROW_AXES, up)  62.4 us
    all_to_all x1, waiting for transfers between devices, gather_grid(): gathered = lax.all_to_all(packed, ('sx', 'sy'), 0, 0, tiled=True)  36.9 us
    all_to_all x2, starting transfers between devices, restrict_rows(): gathered = lax.all_to_all(packed, ROW_AXES, 0, 0, tiled=True)  36.9 us
    add x14, other arithmetic, relay_round(): return passed_along(coarse_step(coarse_state) + corrections, 'tm', 1)  33.8 us
    ppermute x15, starting transfers between devices, passed_along(): lax.ppermute(value, axis, [(source, source + steps) for source in range(i...  28.7 us
    div x25, other arithmetic, fractional(): water_mobility / mobility  27.5 us
  transfers between devices with their start and end apart: 49, of which 43 were waited for; matrix products, arithmetic and copies ran while one was open for 2% of the time, Pallas kernels for 0%

profile of v7, /device:TPU:6, one launch (start us, length us, event | category | flops | bytes accessed | tf_op | source)
XLA Modules:
  0.0 649.5 jit_solution(12596923312564883459)
XLA Ops:
  21.9 7.6 %all-to-all-done.1 = f32[4,6,1,16,256]{4,3,1,2,0:T(8,128)S(1)} async-done(((f32[4,6,1,16,256]{4,3,1,2,0:T(8,128)}), f32[4,6,1,16,256]{4,3,1,2,0:T(8,128)S(1)}, u32[]{:S(2)}, u32[]{:S(2)}) %all-to-all-start.1) | async-done | bytes 393248 | tf_op jit(solution)/shard_map/all_to_all | solution.py:281
  30.9 9.5 %all-to-all-start = ((f32[32,6,2,8,128]{4,3,2,1,0:T(8,128)}), f32[32,6,2,8,128]{4,3,2,1,0:T(8,128)S(1)}, u32[]{:S(2)}, u32[]{:S(2)}) async-start(f32[32,6,2,8,128]{4,3,2,1,0:T(8,128)} %broadcast_in_dim.123), calls=%async_computation | async-start | bytes 3145728 | tf_op jit(solution)/shard_map/all_to_all | solution.py:264
  41.1 36.9 %all-to-all-done = f32[32,6,2,8,128]{4,3,2,1,0:T(8,128)S(1)} async-done(((f32[32,6,2,8,128]{4,3,2,1,0:T(8,128)}), f32[32,6,2,8,128]{4,3,2,1,0:T(8,128)S(1)}, u32[]{:S(2)}, u32[]{:S(2)}) %all-to-all-start) | async-done | bytes 1572896 | tf_op jit(solution)/shard_map/all_to_all | solution.py:264
  81.6 20.1 %while.37 = (s32[]{:T(128)}, f32[16,32,128]{2,1,0:T(8,128)}, s32[]{:T(128)}, f32[16,32,128]{2,1,0:T(8,128)S(1)}, f32[16,32,128]{2,1,0:T(8,128)S(1)}, /*index=5*/...) while((s32[]{:T(128)}, f32[16,32,128]{2,1,0:T(8,128)}, ...), condition=%wide.region_2.3_spmd, body=%wide.region_1.2_spmd.sunk | while | flops 4784130 | bytes 4980885 | solution.py:378
  125.0 24.8 %all_to_all.61 = f32[32,1,2]{2,1,0:T(1,128)S(1)} all-to-all(f32[32,1,2]{2,1,0:T(1,128)S(1)} %broadcast_in_dim.128), channel_id=1, replica_groups=mesh['tm'=8,'sx'=8,'sy'=4] {'sx','sy'}, dimensions={0} | all-to-all | bytes 512 | tf_op jit(solution)/shard_map/all_to_all | solution.py:191
  165.8 18.9 %all_to_all.62 = f32[32,1,2]{2,1,0:T(1,128)S(1)} all-to-all(f32[32,1,2]{2,1,0:T(1,128)S(1)} %broadcast_in_dim.129), channel_id=1, replica_groups=mesh['tm'=8,'sx'=8,'sy'=4] {'sx','sy'}, dimensions={0} | all-to-all | bytes 512 | tf_op jit(solution)/shard_map/all_to_all | solution.py:191
  203.7 9.3 %all-to-all-start.4 = ((f32[32,1,2]{2,1,0:T(1,128)}), f32[32,1,2]{2,1,0:T(1,128)S(1)}, u32[]{:S(2)}, u32[]{:S(2)}) async-start(f32[32,1,2]{2,1,0:T(1,128)} %broadcast_in_dim.130), calls=%async_computation.4 | async-start | bytes 32768 | tf_op jit(solution)/shard_map/all_to_all | solution.py:191
  249.8 16.7 %all-to-all-start.5 = ((f32[32,1,32,128]{3,2,1,0:T(8,128)}), f32[32,1,32,128]{3,2,1,0:T(8,128)}, u32[]{:S(2)}, u32[]{:S(2)}) async-start(f32[32,1,32,128]{3,2,1,0:T(8,128)} %broadcast_in_dim.132), calls=%async_computation.5 | async-start | bytes 1048576 | tf_op jit(solution)/shard_map/all_to_all | solution.py:303
  269.0 11.2 %all-to-all-done.5 = f32[32,1,32,128]{3,2,1,0:T(8,128)} async-done(((f32[32,1,32,128]{3,2,1,0:T(8,128)}), f32[32,1,32,128]{3,2,1,0:T(8,128)}, u32[]{:S(2)}, u32[]{:S(2)}) %all-to-all-start.5) | async-done | bytes 524320 | tf_op jit(solution)/shard_map/all_to_all | solution.py:303
  285.3 80.4 %while.38 = (s32[]{:T(128)}, f32[16,32,128]{2,1,0:T(8,128)}, pred[]{:T(512)}, f32[16,32,128]{2,1,0:T(8,128)S(1)}, f32[16,32,128]{2,1,0:T(8,128)S(1)}, /*index=5*...) while((s32[]{:T(128)}, f32[16,32,128]{2,1,0:T(8,128)}, ...), condition=%wide.region_14.16_spmd, body=%wide.region_13.15_spmd.sunk | while | flops 4980738 | bytes 6815951 | solution.py:374
  290.7 6.1 collective-permute-done
  302.2 6.1 collective-permute-done
  313.7 6.1 collective-permute-done
  325.2 6.1 collective-permute-done
  336.7 6.1 collective-permute-done
  348.2 6.1 collective-permute-done
  359.7 6.1 collective-permute-done
  395.4 24.5 %all_to_all.63 = f32[32,1,2]{2,1,0:T(1,128)S(1)} all-to-all(f32[32,1,2]{2,1,0:T(1,128)S(1)} %broadcast_in_dim.133), channel_id=1, replica_groups=mesh['tm'=8,'sx'=8,'sy'=4] {'sx','sy'}, dimensions={0} | all-to-all | bytes 512 | tf_op jit(solution)/shard_map/all_to_all | solution.py:191
  435.6 18.9 %all_to_all.64 = f32[32,1,2]{2,1,0:T(1,128)S(1)} all-to-all(f32[32,1,2]{2,1,0:T(1,128)S(1)} %broadcast_in_dim.134), channel_id=1, replica_groups=mesh['tm'=8,'sx'=8,'sy'=4] {'sx','sy'}, dimensions={0} | all-to-all | bytes 512 | tf_op jit(solution)/shard_map/all_to_all | solution.py:191
  473.5 9.3 %all-to-all-start.8 = ((f32[32,1,2]{2,1,0:T(1,128)}), f32[32,1,2]{2,1,0:T(1,128)S(1)}, u32[]{:S(2)}, u32[]{:S(2)}) async-start(f32[32,1,2]{2,1,0:T(1,128)} %broadcast_in_dim.135), calls=%async_computation.8 | async-start | bytes 32768 | tf_op jit(solution)/shard_map/all_to_all | solution.py:191
  484.1 5.2 collective-permute-start.28
  519.4 20.1 %all-to-all-start.9 = ((f32[32,1,32,128]{3,2,1,0:T(8,128)}), f32[32,1,32,128]{3,2,1,0:T(8,128)}, u32[]{:S(2)}, u32[]{:S(2)}) async-start(f32[32,1,32,128]{3,2,1,0:T(8,128)} %broadcast_in_dim.137), calls=%async_computation.9 | async-start | bytes 1048576 | tf_op jit(solution)/shard_map/all_to_all | solution.py:303
  540.2 13.1 %all-to-all-done.9 = f32[32,1,32,128]{3,2,1,0:T(8,128)} async-done(((f32[32,1,32,128]{3,2,1,0:T(8,128)}), f32[32,1,32,128]{3,2,1,0:T(8,128)}, u32[]{:S(2)}, u32[]{:S(2)}) %all-to-all-start.9) | async-done | bytes 524320 | tf_op jit(solution)/shard_map/all_to_all | solution.py:303
  556.2 80.3 %while.39 = (s32[]{:T(128)}, f32[16,32,128]{2,1,0:T(8,128)}, pred[]{:T(512)}, f32[16,32,128]{2,1,0:T(8,128)S(1)}, f32[16,32,128]{2,1,0:T(8,128)S(1)}, /*index=5*...) while((s32[]{:T(128)}, f32[16,32,128]{2,1,0:T(8,128)}, ...), condition=%wide.region_26.28_spmd, body=%wide.region_25.27_spmd.sunk | while | flops 4980738 | bytes 6815951 | solution.py:374
  561.6 6.1 collective-permute-done.1
  573.0 6.1 collective-permute-done.1
  584.5 6.1 collective-permute-done.1
  596.0 6.1 collective-permute-done.1
  607.5 6.1 collective-permute-done.1
  618.9 6.1 collective-permute-done.1
  630.4 6.1 collective-permute-done.1
  639.7 9.1 %all_to_all.65 = f32[4,2,1,16,256]{4,3,2,1,0:T(8,128)S(1)} all-to-all(f32[4,2,1,16,256]{4,3,2,1,0:T(8,128)S(1)} %maximum_bitcast_fusion), channel_id=1, replica_groups=mesh['tm'=8,'sx'=8,'sy'=4] {'sy'}, dimensions={0} | all-to-all | bytes 262144 | tf_op jit(solution)/shard_map/all_to_all | solution.py:290
  (402 shorter events, 307.2 us)
Async XLA Ops:
  17.0 12.5 %all-to-all-start.1 = ((f32[4,6,1,16,256]{4,3,1,2,0:T(8,128)}), f32[4,6,1,16,256]{4,3,1,2,0:T(8,128)S(1)}, u32[]{:S(2)}, u32[]{:S(2)}) async-start(f32[4,6,1,16,256]{4,3,1,2,0:T(8,128)} %bitcast.39), calls=%async_computation.1 | async-start | bytes 786432 | tf_op jit(solution)/shard_map/all_to_all | solution.py:281
  30.9 47.1 %all-to-all-start = ((f32[32,6,2,8,128]{4,3,2,1,0:T(8,128)}), f32[32,6,2,8,128]{4,3,2,1,0:T(8,128)S(1)}, u32[]{:S(2)}, u32[]{:S(2)}) async-start(f32[32,6,2,8,128]{4,3,2,1,0:T(8,128)} %broadcast_in_dim.123), calls=%async_computation | async-start | bytes 3145728 | tf_op jit(solution)/shard_map/all_to_all | solution.py:264
  115.8 6.4 collective-permute-start.5
  203.7 19.1 %all-to-all-start.4 = ((f32[32,1,2]{2,1,0:T(1,128)}), f32[32,1,2]{2,1,0:T(1,128)S(1)}, u32[]{:S(2)}, u32[]{:S(2)}) async-start(f32[32,1,2]{2,1,0:T(1,128)} %broadcast_in_dim.130), calls=%async_computation.4 | async-start | bytes 32768 | tf_op jit(solution)/shard_map/all_to_all | solution.py:191
  213.1 22.7 %collective-permute-start.11 = (f32[1,64,256]{2,1,0:T(8,128)}, f32[1,64,256]{2,1,0:T(8,128)}, u32[]{:S(2)}, u32[]{:S(2)}) collective-permute-start(f32[1,64,256]{2,1,0:T(8,128)} %get-tuple-element.795), channel_id=1, source_target_pairs={{1,0},{2,1},{3,2},{4,3},{5,4},{6,5},{7,6},{8,7},{9,8},{10,9},{11,1... | collective-permute-start | bytes 196616 | tf_op jit(solution)/shard_map/ppermute | solution.py:123
  214.4 21.4 %collective-permute-start.13 = (f32[1,64,256]{2,1,0:T(8,128)}, f32[1,64,256]{2,1,0:T(8,128)}, u32[]{:S(2)}, u32[]{:S(2)}) collective-permute-start(f32[1,64,256]{2,1,0:T(8,128)} %get-tuple-element.795), channel_id=1, source_target_pairs={{0,1},{1,2},{2,3},{3,4},{4,5},{5,6},{6,7},{7,8},{8,9},{9,10},{10,1... | collective-permute-start | bytes 196616 | tf_op jit(solution)/shard_map/ppermute | solution.py:122
  229.7 7.1 %collective-permute-start.10 = (f32[1,64,256]{2,1,0:T(8,128)S(1)}, f32[1,64,256]{2,1,0:T(8,128)S(1)}, u32[]{:S(2)}, u32[]{:S(2)}) collective-permute-start(f32[1,64,256]{2,1,0:T(8,128)S(1)} %multiply_add_fusion.1), channel_id=1, source_target_pairs={{1,0},{2,1},{3,2},{4,3},{5,4},{6,5},{7,6},{8,7},{9,8},{10,9},{11,1... | collective-permute-start | bytes 196616 | tf_op jit(solution)/shard_map/ppermute | solution.py:123
  239.3 6.5 %collective-permute-start.14 = (f32[1,64,256]{2,1,0:T(8,128)S(1)}, f32[1,64,256]{2,1,0:T(8,128)S(1)}, u32[]{:S(2)}, u32[]{:S(2)}) collective-permute-start(f32[1,64,256]{2,1,0:T(8,128)S(1)} %get-tuple-element.747), channel_id=1, source_target_pairs={{1,0},{2,1},{3,2},{4,3},{5,4},{6,5},{7,6},{8,7},{9,8},{10,9},{11,1... | collective-permute-start | bytes 196616 | tf_op jit(solution)/shard_map/ppermute | solution.py:123
  240.6 6.8 %collective-permute-start.15 = (f32[1,64,256]{2,1,0:T(8,128)S(1)}, f32[1,64,256]{2,1,0:T(8,128)S(1)}, u32[]{:S(2)}, u32[]{:S(2)}) collective-permute-start(f32[1,64,256]{2,1,0:T(8,128)S(1)} %get-tuple-element.747), channel_id=1, source_target_pairs={{0,1},{1,2},{2,3},{3,4},{4,5},{5,6},{6,7},{7,8},{8,9},{9,10},{10,1... | collective-permute-start | bytes 196616 | tf_op jit(solution)/shard_map/ppermute | solution.py:122
  249.8 30.4 %all-to-all-start.5 = ((f32[32,1,32,128]{3,2,1,0:T(8,128)}), f32[32,1,32,128]{3,2,1,0:T(8,128)}, u32[]{:S(2)}, u32[]{:S(2)}) async-start(f32[32,1,32,128]{3,2,1,0:T(8,128)} %broadcast_in_dim.132), calls=%async_computation.5 | async-start | bytes 1048576 | tf_op jit(solution)/shard_map/all_to_all | solution.py:303
  288.8 8.0 %collective-permute-start = (f32[16,32,128]{2,1,0:T(8,128)}, f32[16,32,128]{2,1,0:T(8,128)}, u32[]{:S(2)}, u32[]{:S(2)}) collective-permute-start(f32[16,32,128]{2,1,0:T(8,128)} %fusion.468), channel_id=1, source_target_pairs={{0,32},{32,64},{64,96},{96,128},{128,160},{160,192},{192,224},{1,3... | collective-permute-start | bytes 786440 | tf_op jit(solution)/shard_map/while/body/eval_jaxpr/ppermute | solution.py:37
  300.3 8.0 %collective-permute-start = (f32[16,32,128]{2,1,0:T(8,128)}, f32[16,32,128]{2,1,0:T(8,128)}, u32[]{:S(2)}, u32[]{:S(2)}) collective-permute-start(f32[16,32,128]{2,1,0:T(8,128)} %fusion.468), channel_id=1, source_target_pairs={{0,32},{32,64},{64,96},{96,128},{128,160},{160,192},{192,224},{1,3... | collective-permute-start | bytes 786440 | tf_op jit(solution)/shard_map/while/body/eval_jaxpr/ppermute | solution.py:37
  311.8 8.0 %collective-permute-start = (f32[16,32,128]{2,1,0:T(8,128)}, f32[16,32,128]{2,1,0:T(8,128)}, u32[]{:S(2)}, u32[]{:S(2)}) collective-permute-start(f32[16,32,128]{2,1,0:T(8,128)} %fusion.468), channel_id=1, source_target_pairs={{0,32},{32,64},{64,96},{96,128},{128,160},{160,192},{192,224},{1,3... | collective-permute-start | bytes 786440 | tf_op jit(solution)/shard_map/while/body/eval_jaxpr/ppermute | solution.py:37
  323.3 8.0 %collective-permute-start = (f32[16,32,128]{2,1,0:T(8,128)}, f32[16,32,128]{2,1,0:T(8,128)}, u32[]{:S(2)}, u32[]{:S(2)}) collective-permute-start(f32[16,32,128]{2,1,0:T(8,128)} %fusion.468), channel_id=1, source_target_pairs={{0,32},{32,64},{64,96},{96,128},{128,160},{160,192},{192,224},{1,3... | collective-permute-start | bytes 786440 | tf_op jit(solution)/shard_map/while/body/eval_jaxpr/ppermute | solution.py:37
  334.8 8.0 %collective-permute-start = (f32[16,32,128]{2,1,0:T(8,128)}, f32[16,32,128]{2,1,0:T(8,128)}, u32[]{:S(2)}, u32[]{:S(2)}) collective-permute-start(f32[16,32,128]{2,1,0:T(8,128)} %fusion.468), channel_id=1, source_target_pairs={{0,32},{32,64},{64,96},{96,128},{128,160},{160,192},{192,224},{1,3... | collective-permute-start | bytes 786440 | tf_op jit(solution)/shard_map/while/body/eval_jaxpr/ppermute | solution.py:37
  346.3 8.0 %collective-permute-start = (f32[16,32,128]{2,1,0:T(8,128)}, f32[16,32,128]{2,1,0:T(8,128)}, u32[]{:S(2)}, u32[]{:S(2)}) collective-permute-start(f32[16,32,128]{2,1,0:T(8,128)} %fusion.468), channel_id=1, source_target_pairs={{0,32},{32,64},{64,96},{96,128},{128,160},{160,192},{192,224},{1,3... | collective-permute-start | bytes 786440 | tf_op jit(solution)/shard_map/while/body/eval_jaxpr/ppermute | solution.py:37
  357.7 8.0 %collective-permute-start = (f32[16,32,128]{2,1,0:T(8,128)}, f32[16,32,128]{2,1,0:T(8,128)}, u32[]{:S(2)}, u32[]{:S(2)}) collective-permute-start(f32[16,32,128]{2,1,0:T(8,128)} %fusion.468), channel_id=1, source_target_pairs={{0,32},{32,64},{64,96},{96,128},{128,160},{160,192},{192,224},{1,3... | collective-permute-start | bytes 786440 | tf_op jit(solution)/shard_map/while/body/eval_jaxpr/ppermute | solution.py:37
  473.5 19.1 %all-to-all-start.8 = ((f32[32,1,2]{2,1,0:T(1,128)}), f32[32,1,2]{2,1,0:T(1,128)S(1)}, u32[]{:S(2)}, u32[]{:S(2)}) async-start(f32[32,1,2]{2,1,0:T(1,128)} %broadcast_in_dim.135), calls=%async_computation.8 | async-start | bytes 32768 | tf_op jit(solution)/shard_map/all_to_all | solution.py:191
  482.8 22.5 %collective-permute-start.26 = (f32[1,64,256]{2,1,0:T(8,128)}, f32[1,64,256]{2,1,0:T(8,128)}, u32[]{:S(2)}, u32[]{:S(2)}) collective-permute-start(f32[1,64,256]{2,1,0:T(8,128)} %get-tuple-element.731), channel_id=1, source_target_pairs={{1,0},{2,1},{3,2},{4,3},{5,4},{6,5},{7,6},{8,7},{9,8},{10,9},{11,1... | collective-permute-start | bytes 196616 | tf_op jit(solution)/shard_map/ppermute | solution.py:123
  484.1 21.2 %collective-permute-start.28 = (f32[1,64,256]{2,1,0:T(8,128)}, f32[1,64,256]{2,1,0:T(8,128)}, u32[]{:S(2)}, u32[]{:S(2)}) collective-permute-start(f32[1,64,256]{2,1,0:T(8,128)} %get-tuple-element.731), channel_id=1, source_target_pairs={{0,1},{1,2},{2,3},{3,4},{4,5},{5,6},{6,7},{7,8},{8,9},{9,10},{10,1... | collective-permute-start | bytes 196616 | tf_op jit(solution)/shard_map/ppermute | solution.py:122
  499.3 7.1 %collective-permute-start.25 = (f32[1,64,256]{2,1,0:T(8,128)S(1)}, f32[1,64,256]{2,1,0:T(8,128)S(1)}, u32[]{:S(2)}, u32[]{:S(2)}) collective-permute-start(f32[1,64,256]{2,1,0:T(8,128)S(1)} %multiply_add_fusion), channel_id=1, source_target_pairs={{1,0},{2,1},{3,2},{4,3},{5,4},{6,5},{7,6},{8,7},{9,8},{10,9},{11,1... | collective-permute-start | bytes 196616 | tf_op jit(solution)/shard_map/ppermute | solution.py:123
  500.8 6.4 collective-permute-start.27
  508.9 6.5 %collective-permute-start.29 = (f32[1,64,256]{2,1,0:T(8,128)S(1)}, f32[1,64,256]{2,1,0:T(8,128)S(1)}, u32[]{:S(2)}, u32[]{:S(2)}) collective-permute-start(f32[1,64,256]{2,1,0:T(8,128)S(1)} %get-tuple-element.729), channel_id=1, source_target_pairs={{1,0},{2,1},{3,2},{4,3},{5,4},{6,5},{7,6},{8,7},{9,8},{10,9},{11,1... | collective-permute-start | bytes 196616 | tf_op jit(solution)/shard_map/ppermute | solution.py:123
  510.2 6.8 %collective-permute-start.30 = (f32[1,64,256]{2,1,0:T(8,128)S(1)}, f32[1,64,256]{2,1,0:T(8,128)S(1)}, u32[]{:S(2)}, u32[]{:S(2)}) collective-permute-start(f32[1,64,256]{2,1,0:T(8,128)S(1)} %get-tuple-element.729), channel_id=1, source_target_pairs={{0,1},{1,2},{2,3},{3,4},{4,5},{5,6},{6,7},{7,8},{8,9},{9,10},{10,1... | collective-permute-start | bytes 196616 | tf_op jit(solution)/shard_map/ppermute | solution.py:122
  519.4 33.9 %all-to-all-start.9 = ((f32[32,1,32,128]{3,2,1,0:T(8,128)}), f32[32,1,32,128]{3,2,1,0:T(8,128)}, u32[]{:S(2)}, u32[]{:S(2)}) async-start(f32[32,1,32,128]{3,2,1,0:T(8,128)} %broadcast_in_dim.137), calls=%async_computation.9 | async-start | bytes 1048576 | tf_op jit(solution)/shard_map/all_to_all | solution.py:303
  559.6 8.0 %collective-permute-start.1 = (f32[16,32,128]{2,1,0:T(8,128)}, f32[16,32,128]{2,1,0:T(8,128)}, u32[]{:S(2)}, u32[]{:S(2)}) collective-permute-start(f32[16,32,128]{2,1,0:T(8,128)} %fusion.469), channel_id=1, source_target_pairs={{0,32},{32,64},{64,96},{96,128},{128,160},{160,192},{192,224},{1,3... | collective-permute-start | bytes 786440 | tf_op jit(solution)/shard_map/while/body/eval_jaxpr/ppermute | solution.py:37
  571.1 8.0 %collective-permute-start.1 = (f32[16,32,128]{2,1,0:T(8,128)}, f32[16,32,128]{2,1,0:T(8,128)}, u32[]{:S(2)}, u32[]{:S(2)}) collective-permute-start(f32[16,32,128]{2,1,0:T(8,128)} %fusion.469), channel_id=1, source_target_pairs={{0,32},{32,64},{64,96},{96,128},{128,160},{160,192},{192,224},{1,3... | collective-permute-start | bytes 786440 | tf_op jit(solution)/shard_map/while/body/eval_jaxpr/ppermute | solution.py:37
  582.6 8.0 %collective-permute-start.1 = (f32[16,32,128]{2,1,0:T(8,128)}, f32[16,32,128]{2,1,0:T(8,128)}, u32[]{:S(2)}, u32[]{:S(2)}) collective-permute-start(f32[16,32,128]{2,1,0:T(8,128)} %fusion.469), channel_id=1, source_target_pairs={{0,32},{32,64},{64,96},{96,128},{128,160},{160,192},{192,224},{1,3... | collective-permute-start | bytes 786440 | tf_op jit(solution)/shard_map/while/body/eval_jaxpr/ppermute | solution.py:37
  594.1 8.0 %collective-permute-start.1 = (f32[16,32,128]{2,1,0:T(8,128)}, f32[16,32,128]{2,1,0:T(8,128)}, u32[]{:S(2)}, u32[]{:S(2)}) collective-permute-start(f32[16,32,128]{2,1,0:T(8,128)} %fusion.469), channel_id=1, source_target_pairs={{0,32},{32,64},{64,96},{96,128},{128,160},{160,192},{192,224},{1,3... | collective-permute-start | bytes 786440 | tf_op jit(solution)/shard_map/while/body/eval_jaxpr/ppermute | solution.py:37
  605.5 8.0 %collective-permute-start.1 = (f32[16,32,128]{2,1,0:T(8,128)}, f32[16,32,128]{2,1,0:T(8,128)}, u32[]{:S(2)}, u32[]{:S(2)}) collective-permute-start(f32[16,32,128]{2,1,0:T(8,128)} %fusion.469), channel_id=1, source_target_pairs={{0,32},{32,64},{64,96},{96,128},{128,160},{160,192},{192,224},{1,3... | collective-permute-start | bytes 786440 | tf_op jit(solution)/shard_map/while/body/eval_jaxpr/ppermute | solution.py:37
  617.0 8.0 %collective-permute-start.1 = (f32[16,32,128]{2,1,0:T(8,128)}, f32[16,32,128]{2,1,0:T(8,128)}, u32[]{:S(2)}, u32[]{:S(2)}) collective-permute-start(f32[16,32,128]{2,1,0:T(8,128)} %fusion.469), channel_id=1, source_target_pairs={{0,32},{32,64},{64,96},{96,128},{128,160},{160,192},{192,224},{1,3... | collective-permute-start | bytes 786440 | tf_op jit(solution)/shard_map/while/body/eval_jaxpr/ppermute | solution.py:37
  628.5 8.0 %collective-permute-start.1 = (f32[16,32,128]{2,1,0:T(8,128)}, f32[16,32,128]{2,1,0:T(8,128)}, u32[]{:S(2)}, u32[]{:S(2)}) collective-permute-start(f32[16,32,128]{2,1,0:T(8,128)} %fusion.469), channel_id=1, source_target_pairs={{0,32},{32,64},{64,96},{96,128},{128,160},{160,192},{192,224},{1,3... | collective-permute-start | bytes 786440 | tf_op jit(solution)/shard_map/while/body/eval_jaxpr/ppermute | solution.py:37
  (97 other events, 1294.0 us)

commit v8 on v7

--- a/solution.py
+++ b/solution.py
@@ -193,13 +193,19 @@
     return [totals[k] for k in range(len(values))]
 
 
+def extended_faces(extended):
+    return face_list(jnp.pad(extended, ((0, 0), (1, 1), (1, 1))))
+
+
 def apply_operator(diagonal, transmissibility, vector):
-    return diagonal * vector - accumulate_terms(
+    vector_rows = row_halo(vector)
+    image = diagonal * vector - accumulate_terms(
         [
             conduct_face * exceeding_part
-            for conduct_face, exceeding_part in zip(transmissibility, row_faces(vector))
+            for conduct_face, exceeding_part in zip(transmissibility, extended_faces(vector_rows))
         ]
     )
+    return image, vector_rows
 
 
 def solve_pressure(source_rate, diagonal, transmissibility):
@@ -207,17 +213,17 @@
     solution = None
     for sweep_no in range(CG_ITERS):
         precond = residual / diagonal
-        image = apply_operator(diagonal, transmissibility, precond)
+        image, precond_rows = apply_operator(diagonal, transmissibility, precond)
         rho_next, curvature = global_sums([jnp.sum(residual * precond), jnp.sum(precond * image)])
         if sweep_no == 0:
             step_len = rho_next / curvature
-            direction = precond
+            direction = precond_rows
             applied = image
             solution = step_len * direction
         else:
             ratio = rho_next / rho_now
             step_len = rho_next / (curvature - ratio * rho_next / step_len)
-            direction = precond + ratio * direction
+            direction = precond_rows + ratio * direction
             applied = image + ratio * applied
             solution = solution + step_len * direction
         if sweep_no + 1 < CG_ITERS:
@@ -226,16 +232,20 @@
     return solution
 
 
-def fine_step(sat_old, permeability, porosity, source_rate, water_end, oil_end):
-    water_mobility, oil_mobility = mobilities(sat_old, water_end, oil_end)
-    transport_field = permeability * (water_mobility + oil_mobility)
+def fine_step(sat_old, permeability, porosity, source_rate, water_end, oil_end, beside_fields):
+    permeability_rows, water_rows, oil_rows, present_rows = beside_fields
+    sat_rows = row_halo(sat_old)
+    water_mobility, oil_mobility = mobilities(sat_rows, water_rows, oil_rows)
+    transport_rows = permeability_rows * (water_mobility + oil_mobility)
+    transport_field = transport_rows[1:-1]
     transmissibility = [
         0.5 * (transport_field + exceeding_part)
-        for exceeding_part in face_mobility_values(transport_field)
+        for exceeding_part in extended_faces(transport_rows)
     ]
     diagonal = compress + accumulate_terms(transmissibility)
-    pressure = solve_pressure(source_rate, diagonal, transmissibility)
-    beside = pressure_faces(pressure)
+    pressure_rows = solve_pressure(source_rate, diagonal, transmissibility)
+    pressure = pressure_rows[1:-1]
+    beside = extended_faces(pressure_rows)
     outflows = [
         conduct_face * (pressure - exceeding_part)
         for conduct_face, exceeding_part in zip(transmissibility, beside)
@@ -244,7 +254,12 @@
     saturation = sat_old
     for newton_no in range(NEWTON):
         frac, frac_slope = fractional(saturation, water_end, oil_end)
-        flux_sum = upwind(frac, flow_faces(frac), outflows)
+        if newton_no == 0:
+            frac_rows = jnp.where(present_rows, fractional(sat_rows, water_rows, oil_rows)[0], 0.0)
+            frac_beyond = extended_faces(frac_rows)
+        else:
+            frac_beyond = flow_faces(frac)
+        flux_sum = upwind(frac, frac_beyond, outflows)
         balance = (
             porosity * (saturation - sat_old) / step_dt
             + flux_sum
@@ -384,6 +399,12 @@
         jnp.stack([initial_saturation, permeability, porosity, source_rate, water_fine, oil_fine])
     )
     share = initial_rows.shape[0]
+    stacked_rows = row_halo(jnp.stack([permeability, water_fine, oil_fine]).transpose(1, 0, 2, 3))
+    stacked_rows = stacked_rows.transpose(1, 0, 2, 3)
+    count = lax.axis_size("sx") * lax.axis_size("sy")
+    row_number = lax.broadcasted_iota(jnp.int32, (share + 2, 1, 1), 0) - 1 + row_index() * share
+    present_rows = (row_number >= 0) & (row_number < count * share)
+    beside_fields = (stacked_rows[0], stacked_rows[1], stacked_rows[2], present_rows)
     starts = jnp.where(slice_index == 0, initial_rows, prolong_rows(coarse_state, share))
     previous_image = coarse_image
     ends = starts
@@ -391,7 +412,7 @@
     for parareal_no in range(PARAREAL):
         saturation = starts
         saturation, fine_pressure = fine_step(
-            saturation, permeability, porosity, source_rate, water_fine, oil_fine
+            saturation, permeability, porosity, source_rate, water_fine, oil_fine, beside_fields
         )
         pressure = fine_pressure
         corrections = restrict_rows(saturation) - previous_image

time: 655 us -> 615 us (0.939)
  starting transfers between devices: 179 us -> 129 us
  blocking collectives: 96.2 us -> 131 us
  waiting for transfers between devices: 191 us -> 168 us
    all_to_all x4 -> x6, blocking collectives: 87 us -> 122 us  [global_sums(): gathered = lax.all_to_all(packed, ('sx', 'sy'), 0, 0, tiled=True)]
    all_to_all x2 -> x0, starting transfers between devices: 18.6 us -> none  [global_sums(): gathered = lax.all_to_all(packed, ('sx', 'sy'), 0, 0, tiled=True)]
    all_to_all x2, starting transfers between devices: 36.9 us -> 21.1 us  [restrict_rows(): gathered = lax.all_to_all(packed, ROW_AXES, 0, 0, tiled=True)]
    ppermute x14 -> x11, starting transfers between devices: 62.4 us -> 51.6 us  [row_halo(): before = lax.ppermute(volume[-1:], ROW_AXES, up)]
    ppermute x14 -> x11, waiting for transfers between devices: 11.2 us -> 2.92 us  [row_halo(): after = lax.ppermute(volume[:1], ROW_AXES, down)]
    all_to_all x1, waiting for transfers between devices: 36.9 us -> 29.1 us  [gather_grid(): gathered = lax.all_to_all(packed, ('sx', 'sy'), 0, 0, tiled=True)]
    all_to_all x2 -> x0, waiting for transfers between devices: 6.6 us -> none  [global_sums(): gathered = lax.all_to_all(packed, ('sx', 'sy'), 0, 0, tiled=True)]
    ppermute x14 -> x11, starting transfers between devices: 18.4 us -> 14.2 us  [row_halo(): after = lax.ppermute(volume[:1], ROW_AXES, down)]
  transfers between devices with their start and end apart: 49 -> 41, of which waited for: 43 -> 38; matrix products, arithmetic and copies ran while one was open for 2% -> 5% of each run, Pallas kernels for 0% -> 0%
where the time goes in v8:
time: 615 us; the launch traced here: 610 us
  waiting for transfers between devices  168 us (27%)
  blocking collectives  131 us (21%)
  starting transfers between devices  129 us (21%)
  other arithmetic  128 us (21%)
  local copies, waits for them, and re-layouts  26.8 us (4%)
  between operations  21.5 us (3%)
    all_to_all x6, blocking collectives, global_sums(): gathered = lax.all_to_all(packed, ('sx', 'sy'), 0, 0, tiled=True)  122 us
    ppermute x15, waiting for transfers between devices, passed_along(): lax.ppermute(value, axis, [(source, source + steps) for source in range(i...  88.7 us
    ppermute x11, starting transfers between devices, row_halo(): before = lax.ppermute(volume[-1:], ROW_AXES, up)  51.6 us
    add x14, other arithmetic, relay_round(): return passed_along(coarse_step(coarse_state) + corrections, 'tm', 1)  33.9 us
    all_to_all x1, waiting for transfers between devices, gather_grid(): gathered = lax.all_to_all(packed, ('sx', 'sy'), 0, 0, tiled=True)  29.1 us
    ppermute x15, starting transfers between devices, passed_along(): lax.ppermute(value, axis, [(source, source + steps) for source in range(i...  28.7 us
    div x24, other arithmetic, fractional(): water_mobility / mobility  27.3 us
    all_to_all x2, waiting for transfers between devices, restrict_rows(): gathered = lax.all_to_all(packed, ROW_AXES, 0, 0, tiled=True)  24.3 us
  transfers between devices with their start and end apart: 41, of which 38 were waited for; matrix products, arithmetic and copies ran while one was open for 5% of the time, Pallas kernels for 0%

profile of v8, /device:TPU:6, one launch (start us, length us, event | category | flops | bytes accessed | tf_op | source)
XLA Modules:
  0.0 610.4 jit_solution(1325626438341427423)
XLA Ops:
  21.8 7.6 %all-to-all-done.1 = f32[4,6,1,16,256]{4,3,1,2,0:T(8,128)S(1)} async-done(((f32[4,6,1,16,256]{4,3,1,2,0:T(8,128)}), f32[4,6,1,16,256]{4,3,1,2,0:T(8,128)S(1)}, u32[]{:S(2)}, u32[]{:S(2)}) %all-to-all-start.1) | async-done | bytes 393248 | tf_op jit(solution)/shard_map/all_to_all | solution.py:296
  30.8 9.5 %all-to-all-start = ((f32[32,6,2,8,128]{4,3,2,1,0:T(8,128)}), f32[32,6,2,8,128]{4,3,2,1,0:T(8,128)S(1)}, u32[]{:S(2)}, u32[]{:S(2)}) async-start(f32[32,6,2,8,128]{4,3,2,1,0:T(8,128)} %broadcast_in_dim.139), calls=%async_computation | async-start | bytes 3145728 | tf_op jit(solution)/shard_map/all_to_all | solution.py:279
  43.6 5.2 collective-permute-start.2
  48.8 29.1 %all-to-all-done = f32[32,6,2,8,128]{4,3,2,1,0:T(8,128)S(1)} async-done(((f32[32,6,2,8,128]{4,3,2,1,0:T(8,128)}), f32[32,6,2,8,128]{4,3,2,1,0:T(8,128)S(1)}, u32[]{:S(2)}, u32[]{:S(2)}) %all-to-all-start) | async-done | bytes 1572896 | tf_op jit(solution)/shard_map/all_to_all | solution.py:279
  81.6 20.1 %while.37 = (s32[]{:T(128)}, f32[16,32,128]{2,1,0:T(8,128)}, s32[]{:T(128)}, f32[16,32,128]{2,1,0:T(8,128)S(1)}, f32[16,32,128]{2,1,0:T(8,128)S(1)}, /*index=5*/...) while((s32[]{:T(128)}, f32[16,32,128]{2,1,0:T(8,128)}, ...), condition=%wide.region_2.3_spmd, body=%wide.region_1.2_spmd.sunk | while | flops 4784130 | bytes 4980885 | solution.py:393
  123.5 23.8 %all_to_all.61 = f32[32,1,2]{2,1,0:T(1,128)S(1)} all-to-all(f32[32,1,2]{2,1,0:T(1,128)S(1)} %broadcast_in_dim.144), channel_id=1, replica_groups=mesh['tm'=8,'sx'=8,'sy'=4] {'sx','sy'}, dimensions={0} | all-to-all | bytes 512 | tf_op jit(solution)/shard_map/all_to_all | solution.py:191
  163.0 18.9 %all_to_all.62 = f32[32,1,2]{2,1,0:T(1,128)S(1)} all-to-all(f32[32,1,2]{2,1,0:T(1,128)S(1)} %broadcast_in_dim.145), channel_id=1, replica_groups=mesh['tm'=8,'sx'=8,'sy'=4] {'sx','sy'}, dimensions={0} | all-to-all | bytes 512 | tf_op jit(solution)/shard_map/all_to_all | solution.py:191
  199.7 18.9 %all_to_all.63 = f32[32,1,2]{2,1,0:T(1,128)S(1)} all-to-all(f32[32,1,2]{2,1,0:T(1,128)S(1)} %broadcast_in_dim.146), channel_id=1, replica_groups=mesh['tm'=8,'sx'=8,'sy'=4] {'sx','sy'}, dimensions={0} | all-to-all | bytes 512 | tf_op jit(solution)/shard_map/all_to_all | solution.py:191
  237.5 9.6 %all-to-all-start.5 = ((f32[32,1,32,128]{3,2,1,0:T(8,128)}), f32[32,1,32,128]{3,2,1,0:T(8,128)}, u32[]{:S(2)}, u32[]{:S(2)}) async-start(f32[32,1,32,128]{3,2,1,0:T(8,128)} %broadcast_in_dim.150), calls=%async_computation.5 | async-start | bytes 1048576 | tf_op jit(solution)/shard_map/all_to_all | solution.py:318
  249.6 11.2 %all-to-all-done.5 = f32[32,1,32,128]{3,2,1,0:T(8,128)} async-done(((f32[32,1,32,128]{3,2,1,0:T(8,128)}), f32[32,1,32,128]{3,2,1,0:T(8,128)}, u32[]{:S(2)}, u32[]{:S(2)}) %all-to-all-start.5) | async-done | bytes 524320 | tf_op jit(solution)/shard_map/all_to_all | solution.py:318
  266.2 80.3 %while.38 = (s32[]{:T(128)}, f32[16,32,128]{2,1,0:T(8,128)}, pred[]{:T(512)}, f32[16,32,128]{2,1,0:T(8,128)S(1)}, f32[16,32,128]{2,1,0:T(8,128)S(1)}, /*index=5*...) while((s32[]{:T(128)}, f32[16,32,128]{2,1,0:T(8,128)}, ...), condition=%wide.region_14.16_spmd, body=%wide.region_13.15_spmd.sunk | while | flops 4980738 | bytes 6815951 | solution.py:389
  271.6 6.1 collective-permute-done
  283.1 6.1 collective-permute-done
  294.5 6.1 collective-permute-done
  306.0 6.1 collective-permute-done
  317.5 6.1 collective-permute-done
  329.0 6.1 collective-permute-done
  340.4 6.1 collective-permute-done
  375.3 22.8 %all_to_all.64 = f32[32,1,2]{2,1,0:T(1,128)S(1)} all-to-all(f32[32,1,2]{2,1,0:T(1,128)S(1)} %broadcast_in_dim.151), channel_id=1, replica_groups=mesh['tm'=8,'sx'=8,'sy'=4] {'sx','sy'}, dimensions={0} | all-to-all | bytes 512 | tf_op jit(solution)/shard_map/all_to_all | solution.py:191
  413.7 18.9 %all_to_all.65 = f32[32,1,2]{2,1,0:T(1,128)S(1)} all-to-all(f32[32,1,2]{2,1,0:T(1,128)S(1)} %broadcast_in_dim.152), channel_id=1, replica_groups=mesh['tm'=8,'sx'=8,'sy'=4] {'sx','sy'}, dimensions={0} | all-to-all | bytes 512 | tf_op jit(solution)/shard_map/all_to_all | solution.py:191
  450.6 18.9 %all_to_all.66 = f32[32,1,2]{2,1,0:T(1,128)S(1)} all-to-all(f32[32,1,2]{2,1,0:T(1,128)S(1)} %broadcast_in_dim.153), channel_id=1, replica_groups=mesh['tm'=8,'sx'=8,'sy'=4] {'sx','sy'}, dimensions={0} | all-to-all | bytes 512 | tf_op jit(solution)/shard_map/all_to_all | solution.py:191
  489.0 11.4 %all-to-all-start.9 = ((f32[32,1,32,128]{3,2,1,0:T(8,128)}), f32[32,1,32,128]{3,2,1,0:T(8,128)}, u32[]{:S(2)}, u32[]{:S(2)}) async-start(f32[32,1,32,128]{3,2,1,0:T(8,128)} %broadcast_in_dim.155), calls=%async_computation.9 | async-start | bytes 1048576 | tf_op jit(solution)/shard_map/all_to_all | solution.py:318
  501.1 13.1 %all-to-all-done.9 = f32[32,1,32,128]{3,2,1,0:T(8,128)} async-done(((f32[32,1,32,128]{3,2,1,0:T(8,128)}), f32[32,1,32,128]{3,2,1,0:T(8,128)}, u32[]{:S(2)}, u32[]{:S(2)}) %all-to-all-start.9) | async-done | bytes 524320 | tf_op jit(solution)/shard_map/all_to_all | solution.py:318
  517.0 80.5 %while.39 = (s32[]{:T(128)}, f32[16,32,128]{2,1,0:T(8,128)}, pred[]{:T(512)}, f32[16,32,128]{2,1,0:T(8,128)S(1)}, f32[16,32,128]{2,1,0:T(8,128)S(1)}, /*index=5*...) while((s32[]{:T(128)}, f32[16,32,128]{2,1,0:T(8,128)}, ...), condition=%wide.region_26.28_spmd, body=%wide.region_25.27_spmd.sunk | while | flops 4980738 | bytes 6815951 | solution.py:389
  522.4 6.1 collective-permute-done.1
  533.9 6.1 collective-permute-done.1
  545.4 6.1 collective-permute-done.1
  556.9 6.1 collective-permute-done.1
  568.4 6.1 collective-permute-done.1
  579.9 6.1 collective-permute-done.1
  591.4 6.1 collective-permute-done.1
  600.7 9.1 %all_to_all.67 = f32[4,2,1,16,256]{4,3,2,1,0:T(8,128)S(1)} all-to-all(f32[4,2,1,16,256]{4,3,2,1,0:T(8,128)S(1)} %maximum_bitcast_fusion.2), channel_id=1, replica_groups=mesh['tm'=8,'sx'=8,'sy'=4] {'sy'}, dimensions={0} | all-to-all | bytes 262144 | tf_op jit(solution)/shard_map/all_to_all | solution.py:305
  (414 shorter events, 275.7 us)
Async XLA Ops:
  16.9 12.5 %all-to-all-start.1 = ((f32[4,6,1,16,256]{4,3,1,2,0:T(8,128)}), f32[4,6,1,16,256]{4,3,1,2,0:T(8,128)S(1)}, u32[]{:S(2)}, u32[]{:S(2)}) async-start(f32[4,6,1,16,256]{4,3,1,2,0:T(8,128)} %bitcast.39), calls=%async_computation.1 | async-start | bytes 786432 | tf_op jit(solution)/shard_map/all_to_all | solution.py:296
  30.8 47.1 %all-to-all-start = ((f32[32,6,2,8,128]{4,3,2,1,0:T(8,128)}), f32[32,6,2,8,128]{4,3,2,1,0:T(8,128)S(1)}, u32[]{:S(2)}, u32[]{:S(2)}) async-start(f32[32,6,2,8,128]{4,3,2,1,0:T(8,128)} %broadcast_in_dim.139), calls=%async_computation | async-start | bytes 3145728 | tf_op jit(solution)/shard_map/all_to_all | solution.py:279
  42.3 66.5 %collective-permute-start.3 = (f32[1,3,64,256]{3,2,0,1:T(8,128)}, f32[1,3,64,256]{3,2,0,1:T(8,128)}, u32[]{:S(2)}, u32[]{:S(2)}) collective-permute-start(f32[1,3,64,256]{3,2,0,1:T(8,128)} %maximum_bitcast_fusion.1), channel_id=1, source_target_pairs={{1,0},{2,1},{3,2},{4,3},{5,4},{6,5},{7,6},{8,7},{9,8},{10,9},{11,1... | collective-permute-start | bytes 589832 | tf_op jit(solution)/shard_map/ppermute | solution.py:123
  43.6 65.2 %collective-permute-start.2 = (f32[1,3,64,256]{3,2,0,1:T(8,128)}, f32[1,3,64,256]{3,2,0,1:T(8,128)}, u32[]{:S(2)}, u32[]{:S(2)}) collective-permute-start(f32[1,3,64,256]{3,2,0,1:T(8,128)} %maximum_bitcast_fusion.1), channel_id=1, source_target_pairs={{0,1},{1,2},{2,3},{3,4},{4,5},{5,6},{6,7},{7,8},{8,9},{9,10},{10,1... | collective-permute-start | bytes 589832 | tf_op jit(solution)/shard_map/ppermute | solution.py:122
  102.9 7.1 %collective-permute-start.5 = (f32[1,64,256]{2,1,0:T(8,128)S(1)}, f32[1,64,256]{2,1,0:T(8,128)S(1)}, u32[]{:S(2)}, u32[]{:S(2)}) collective-permute-start(f32[1,64,256]{2,1,0:T(8,128)S(1)} %fusion.71), channel_id=1, source_target_pairs={{1,0},{2,1},{3,2},{4,3},{5,4},{6,5},{7,6},{8,7},{9,8},{10,9},{11,1... | collective-permute-start | bytes 196616 | tf_op jit(solution)/shard_map/ppermute | solution.py:123
  104.2 6.7 %collective-permute-start.4 = (f32[1,64,256]{2,1,0:T(8,128)S(1)}, f32[1,64,256]{2,1,0:T(8,128)S(1)}, u32[]{:S(2)}, u32[]{:S(2)}) collective-permute-start(f32[1,64,256]{2,1,0:T(8,128)S(1)} %fusion.71), channel_id=1, source_target_pairs={{0,1},{1,2},{2,3},{3,4},{4,5},{5,6},{6,7},{7,8},{8,9},{9,10},{10,1... | collective-permute-start | bytes 196616 | tf_op jit(solution)/shard_map/ppermute | solution.py:122
  112.5 6.8 %collective-permute-start.6 = (f32[1,64,256]{2,1,0:T(8,128)S(1)}, f32[1,64,256]{2,1,0:T(8,128)S(1)}, u32[]{:S(2)}, u32[]{:S(2)}) collective-permute-start(f32[1,64,256]{2,1,0:T(8,128)S(1)} %get-tuple-element.751), channel_id=1, source_target_pairs={{1,0},{2,1},{3,2},{4,3},{5,4},{6,5},{7,6},{8,7},{9,8},{10,9},{11,1... | collective-permute-start | bytes 196616 | tf_op jit(solution)/shard_map/ppermute | solution.py:123
  113.8 6.9 %collective-permute-start.7 = (f32[1,64,256]{2,1,0:T(8,128)S(1)}, f32[1,64,256]{2,1,0:T(8,128)S(1)}, u32[]{:S(2)}, u32[]{:S(2)}) collective-permute-start(f32[1,64,256]{2,1,0:T(8,128)S(1)} %get-tuple-element.751), channel_id=1, source_target_pairs={{0,1},{1,2},{2,3},{3,4},{4,5},{5,6},{6,7},{7,8},{8,9},{9,10},{10,1... | collective-permute-start | bytes 196616 | tf_op jit(solution)/shard_map/ppermute | solution.py:122
  152.7 6.4 %collective-permute-start.9 = (f32[1,64,256]{2,1,0:T(8,128)S(1)}, f32[1,64,256]{2,1,0:T(8,128)S(1)}, u32[]{:S(2)}, u32[]{:S(2)}) collective-permute-start(f32[1,64,256]{2,1,0:T(8,128)S(1)} %fusion.405), channel_id=1, source_target_pairs={{0,1},{1,2},{2,3},{3,4},{4,5},{5,6},{6,7},{7,8},{8,9},{9,10},{10,1... | collective-permute-start | bytes 196616 | tf_op jit(solution)/shard_map/ppermute | solution.py:122
  190.2 6.4 %collective-permute-start.11 = (f32[1,64,256]{2,1,0:T(8,128)S(1)}, f32[1,64,256]{2,1,0:T(8,128)S(1)}, u32[]{:S(2)}, u32[]{:S(2)}) collective-permute-start(f32[1,64,256]{2,1,0:T(8,128)S(1)} %get-tuple-element.747), channel_id=1, source_target_pairs={{0,1},{1,2},{2,3},{3,4},{4,5},{5,6},{6,7},{7,8},{8,9},{9,10},{10,1... | collective-permute-start | bytes 196616 | tf_op jit(solution)/shard_map/ppermute | solution.py:122
  228.7 6.4 %collective-permute-start.13 = (f32[1,64,256]{2,1,0:T(8,128)S(1)}, f32[1,64,256]{2,1,0:T(8,128)S(1)}, u32[]{:S(2)}, u32[]{:S(2)}) collective-permute-start(f32[1,64,256]{2,1,0:T(8,128)S(1)} %get-tuple-element.745), channel_id=1, source_target_pairs={{0,1},{1,2},{2,3},{3,4},{4,5},{5,6},{6,7},{7,8},{8,9},{9,10},{10,1... | collective-permute-start | bytes 196616 | tf_op jit(solution)/shard_map/ppermute | solution.py:122
  237.5 23.3 %all-to-all-start.5 = ((f32[32,1,32,128]{3,2,1,0:T(8,128)}), f32[32,1,32,128]{3,2,1,0:T(8,128)}, u32[]{:S(2)}, u32[]{:S(2)}) async-start(f32[32,1,32,128]{3,2,1,0:T(8,128)} %broadcast_in_dim.150), calls=%async_computation.5 | async-start | bytes 1048576 | tf_op jit(solution)/shard_map/all_to_all | solution.py:318
  269.7 8.0 %collective-permute-start = (f32[16,32,128]{2,1,0:T(8,128)}, f32[16,32,128]{2,1,0:T(8,128)}, u32[]{:S(2)}, u32[]{:S(2)}) collective-permute-start(f32[16,32,128]{2,1,0:T(8,128)} %fusion.534), channel_id=1, source_target_pairs={{0,32},{32,64},{64,96},{96,128},{128,160},{160,192},{192,224},{1,3... | collective-permute-start | bytes 786440 | tf_op jit(solution)/shard_map/while/body/eval_jaxpr/ppermute | solution.py:37
  281.1 8.0 %collective-permute-start = (f32[16,32,128]{2,1,0:T(8,128)}, f32[16,32,128]{2,1,0:T(8,128)}, u32[]{:S(2)}, u32[]{:S(2)}) collective-permute-start(f32[16,32,128]{2,1,0:T(8,128)} %fusion.534), channel_id=1, source_target_pairs={{0,32},{32,64},{64,96},{96,128},{128,160},{160,192},{192,224},{1,3... | collective-permute-start | bytes 786440 | tf_op jit(solution)/shard_map/while/body/eval_jaxpr/ppermute | solution.py:37
  292.6 8.0 %collective-permute-start = (f32[16,32,128]{2,1,0:T(8,128)}, f32[16,32,128]{2,1,0:T(8,128)}, u32[]{:S(2)}, u32[]{:S(2)}) collective-permute-start(f32[16,32,128]{2,1,0:T(8,128)} %fusion.534), channel_id=1, source_target_pairs={{0,32},{32,64},{64,96},{96,128},{128,160},{160,192},{192,224},{1,3... | collective-permute-start | bytes 786440 | tf_op jit(solution)/shard_map/while/body/eval_jaxpr/ppermute | solution.py:37
  304.1 8.0 %collective-permute-start = (f32[16,32,128]{2,1,0:T(8,128)}, f32[16,32,128]{2,1,0:T(8,128)}, u32[]{:S(2)}, u32[]{:S(2)}) collective-permute-start(f32[16,32,128]{2,1,0:T(8,128)} %fusion.534), channel_id=1, source_target_pairs={{0,32},{32,64},{64,96},{96,128},{128,160},{160,192},{192,224},{1,3... | collective-permute-start | bytes 786440 | tf_op jit(solution)/shard_map/while/body/eval_jaxpr/ppermute | solution.py:37
  315.6 8.0 %collective-permute-start = (f32[16,32,128]{2,1,0:T(8,128)}, f32[16,32,128]{2,1,0:T(8,128)}, u32[]{:S(2)}, u32[]{:S(2)}) collective-permute-start(f32[16,32,128]{2,1,0:T(8,128)} %fusion.534), channel_id=1, source_target_pairs={{0,32},{32,64},{64,96},{96,128},{128,160},{160,192},{192,224},{1,3... | collective-permute-start | bytes 786440 | tf_op jit(solution)/shard_map/while/body/eval_jaxpr/ppermute | solution.py:37
  327.1 8.0 %collective-permute-start = (f32[16,32,128]{2,1,0:T(8,128)}, f32[16,32,128]{2,1,0:T(8,128)}, u32[]{:S(2)}, u32[]{:S(2)}) collective-permute-start(f32[16,32,128]{2,1,0:T(8,128)} %fusion.534), channel_id=1, source_target_pairs={{0,32},{32,64},{64,96},{96,128},{128,160},{160,192},{192,224},{1,3... | collective-permute-start | bytes 786440 | tf_op jit(solution)/shard_map/while/body/eval_jaxpr/ppermute | solution.py:37
  338.5 8.0 %collective-permute-start = (f32[16,32,128]{2,1,0:T(8,128)}, f32[16,32,128]{2,1,0:T(8,128)}, u32[]{:S(2)}, u32[]{:S(2)}) collective-permute-start(f32[16,32,128]{2,1,0:T(8,128)} %fusion.534), channel_id=1, source_target_pairs={{0,32},{32,64},{64,96},{96,128},{128,160},{160,192},{192,224},{1,3... | collective-permute-start | bytes 786440 | tf_op jit(solution)/shard_map/while/body/eval_jaxpr/ppermute | solution.py:37
  357.0 6.4 %collective-permute-start.15 = (f32[1,64,256]{2,1,0:T(8,128)S(1)}, f32[1,64,256]{2,1,0:T(8,128)S(1)}, u32[]{:S(2)}, u32[]{:S(2)}) collective-permute-start(f32[1,64,256]{2,1,0:T(8,128)S(1)} %broadcast_select_fusion.4), channel_id=1, source_target_pairs={{0,1},{1,2},{2,3},{3,4},{4,5},{5,6},{6,7},{7,8},{8,9},{9,10},{10,1... | collective-permute-start | bytes 196616 | tf_op jit(solution)/shard_map/ppermute | solution.py:122
  364.4 6.5 %collective-permute-start.17 = (f32[1,64,256]{2,1,0:T(8,128)S(1)}, f32[1,64,256]{2,1,0:T(8,128)S(1)}, u32[]{:S(2)}, u32[]{:S(2)}) collective-permute-start(f32[1,64,256]{2,1,0:T(8,128)S(1)} %get-tuple-element.735), channel_id=1, source_target_pairs={{1,0},{2,1},{3,2},{4,3},{5,4},{6,5},{7,6},{8,7},{9,8},{10,9},{11,1... | collective-permute-start | bytes 196616 | tf_op jit(solution)/shard_map/ppermute | solution.py:123
  365.8 6.8 %collective-permute-start.18 = (f32[1,64,256]{2,1,0:T(8,128)S(1)}, f32[1,64,256]{2,1,0:T(8,128)S(1)}, u32[]{:S(2)}, u32[]{:S(2)}) collective-permute-start(f32[1,64,256]{2,1,0:T(8,128)S(1)} %get-tuple-element.735), channel_id=1, source_target_pairs={{0,1},{1,2},{2,3},{3,4},{4,5},{5,6},{6,7},{7,8},{8,9},{9,10},{10,1... | collective-permute-start | bytes 196616 | tf_op jit(solution)/shard_map/ppermute | solution.py:122
  403.5 6.4 %collective-permute-start.20 = (f32[1,64,256]{2,1,0:T(8,128)S(1)}, f32[1,64,256]{2,1,0:T(8,128)S(1)}, u32[]{:S(2)}, u32[]{:S(2)}) collective-permute-start(f32[1,64,256]{2,1,0:T(8,128)S(1)} %fusion.406), channel_id=1, source_target_pairs={{0,1},{1,2},{2,3},{3,4},{4,5},{5,6},{6,7},{7,8},{8,9},{9,10},{10,1... | collective-permute-start | bytes 196616 | tf_op jit(solution)/shard_map/ppermute | solution.py:122
  480.0 6.5 %collective-permute-start.24 = (f32[1,64,256]{2,1,0:T(8,128)S(1)}, f32[1,64,256]{2,1,0:T(8,128)S(1)}, u32[]{:S(2)}, u32[]{:S(2)}) collective-permute-start(f32[1,64,256]{2,1,0:T(8,128)S(1)} %get-tuple-element.729), channel_id=1, source_target_pairs={{0,1},{1,2},{2,3},{3,4},{4,5},{5,6},{6,7},{7,8},{8,9},{9,10},{10,1... | collective-permute-start | bytes 196616 | tf_op jit(solution)/shard_map/ppermute | solution.py:122
  489.0 25.3 %all-to-all-start.9 = ((f32[32,1,32,128]{3,2,1,0:T(8,128)}), f32[32,1,32,128]{3,2,1,0:T(8,128)}, u32[]{:S(2)}, u32[]{:S(2)}) async-start(f32[32,1,32,128]{3,2,1,0:T(8,128)} %broadcast_in_dim.155), calls=%async_computation.9 | async-start | bytes 1048576 | tf_op jit(solution)/shard_map/all_to_all | solution.py:318
  520.5 8.0 %collective-permute-start.1 = (f32[16,32,128]{2,1,0:T(8,128)}, f32[16,32,128]{2,1,0:T(8,128)}, u32[]{:S(2)}, u32[]{:S(2)}) collective-permute-start(f32[16,32,128]{2,1,0:T(8,128)} %fusion.535), channel_id=1, source_target_pairs={{0,32},{32,64},{64,96},{96,128},{128,160},{160,192},{192,224},{1,3... | collective-permute-start | bytes 786440 | tf_op jit(solution)/shard_map/while/body/eval_jaxpr/ppermute | solution.py:37
  532.0 8.0 %collective-permute-start.1 = (f32[16,32,128]{2,1,0:T(8,128)}, f32[16,32,128]{2,1,0:T(8,128)}, u32[]{:S(2)}, u32[]{:S(2)}) collective-permute-start(f32[16,32,128]{2,1,0:T(8,128)} %fusion.535), channel_id=1, source_target_pairs={{0,32},{32,64},{64,96},{96,128},{128,160},{160,192},{192,224},{1,3... | collective-permute-start | bytes 786440 | tf_op jit(solution)/shard_map/while/body/eval_jaxpr/ppermute | solution.py:37
  543.5 8.0 %collective-permute-start.1 = (f32[16,32,128]{2,1,0:T(8,128)}, f32[16,32,128]{2,1,0:T(8,128)}, u32[]{:S(2)}, u32[]{:S(2)}) collective-permute-start(f32[16,32,128]{2,1,0:T(8,128)} %fusion.535), channel_id=1, source_target_pairs={{0,32},{32,64},{64,96},{96,128},{128,160},{160,192},{192,224},{1,3... | collective-permute-start | bytes 786440 | tf_op jit(solution)/shard_map/while/body/eval_jaxpr/ppermute | solution.py:37
  555.0 8.0 %collective-permute-start.1 = (f32[16,32,128]{2,1,0:T(8,128)}, f32[16,32,128]{2,1,0:T(8,128)}, u32[]{:S(2)}, u32[]{:S(2)}) collective-permute-start(f32[16,32,128]{2,1,0:T(8,128)} %fusion.535), channel_id=1, source_target_pairs={{0,32},{32,64},{64,96},{96,128},{128,160},{160,192},{192,224},{1,3... | collective-permute-start | bytes 786440 | tf_op jit(solution)/shard_map/while/body/eval_jaxpr/ppermute | solution.py:37
  566.5 8.0 %collective-permute-start.1 = (f32[16,32,128]{2,1,0:T(8,128)}, f32[16,32,128]{2,1,0:T(8,128)}, u32[]{:S(2)}, u32[]{:S(2)}) collective-permute-start(f32[16,32,128]{2,1,0:T(8,128)} %fusion.535), channel_id=1, source_target_pairs={{0,32},{32,64},{64,96},{96,128},{128,160},{160,192},{192,224},{1,3... | collective-permute-start | bytes 786440 | tf_op jit(solution)/shard_map/while/body/eval_jaxpr/ppermute | solution.py:37
  578.0 8.0 %collective-permute-start.1 = (f32[16,32,128]{2,1,0:T(8,128)}, f32[16,32,128]{2,1,0:T(8,128)}, u32[]{:S(2)}, u32[]{:S(2)}) collective-permute-start(f32[16,32,128]{2,1,0:T(8,128)} %fusion.535), channel_id=1, source_target_pairs={{0,32},{32,64},{64,96},{96,128},{128,160},{160,192},{192,224},{1,3... | collective-permute-start | bytes 786440 | tf_op jit(solution)/shard_map/while/body/eval_jaxpr/ppermute | solution.py:37
  589.5 8.0 %collective-permute-start.1 = (f32[16,32,128]{2,1,0:T(8,128)}, f32[16,32,128]{2,1,0:T(8,128)}, u32[]{:S(2)}, u32[]{:S(2)}) collective-permute-start(f32[16,32,128]{2,1,0:T(8,128)} %fusion.535), channel_id=1, source_target_pairs={{0,32},{32,64},{64,96},{96,128},{128,160},{160,192},{192,224},{1,3... | collective-permute-start | bytes 786440 | tf_op jit(solution)/shard_map/while/body/eval_jaxpr/ppermute | solution.py:37
  (103 other events, 1206.7 us)

commit v9 on v8

--- a/solution.py
+++ b/solution.py
@@ -381,13 +381,13 @@
         return coarse_state - balance / slope_sum
 
     def chain(corrections):
-
-        def relay_round(turn_no, arrived):
-            coarse_state = jnp.where(slice_index == 0, start_coarse, arrived)
-            return passed_along(coarse_step(coarse_state) + corrections, "tm", 1)
-
-        arrived = lax.fori_loop(0, slices - 1, relay_round, start_coarse)
-        coarse_state = jnp.where(slice_index == 0, start_coarse, arrived)
+        packed = jnp.broadcast_to(corrections[None], (slices,) + corrections.shape)
+        every = lax.all_to_all(packed, "tm", 0, 0, tiled=True)
+
+        def corrected_step(turn_no, coarse_state):
+            return coarse_step(coarse_state) + every[turn_no]
+
+        coarse_state = lax.fori_loop(0, slice_index, corrected_step, start_coarse)
         return (coarse_state, coarse_step(coarse_state))
 
     coarse_state = lax.fori_loop(

time: 615 us -> 545 us (0.89)
  waiting for transfers between devices: 168 us -> 123 us
  starting transfers between devices: 129 us -> 98.8 us
  blocking collectives: 131 us -> 157 us
  other arithmetic: 128 us -> 107 us
    ppermute x15 -> x1, waiting for transfers between devices: 88.7 us -> 0.88 us  [passed_along(): lax.ppermute(value, axis, [(source, source + steps) for source in range(i...]
    all_to_all x0 -> x2, waiting for transfers between devices: none -> 48.2 us  [chain(): every = lax.all_to_all(packed, 'tm', 0, 0, tiled=True)]
    ppermute x15 -> x1, starting transfers between devices: 28.7 us -> 4.89 us  [passed_along(): lax.ppermute(value, axis, [(source, source + steps) for source in range(i...]
    all_to_all x0 -> x1, blocking collectives: none -> 22.7 us  [restrict_rows(): gathered = lax.all_to_all(packed, ROW_AXES, 0, 0, tiled=True)]
    all_to_all x2 -> x1, waiting for transfers between devices: 24.3 us -> 12.1 us  [restrict_rows(): gathered = lax.all_to_all(packed, ROW_AXES, 0, 0, tiled=True)]
    all_to_all x2 -> x1, starting transfers between devices: 21.1 us -> 9.44 us  [restrict_rows(): gathered = lax.all_to_all(packed, ROW_AXES, 0, 0, tiled=True)]
    add x14 -> x12, other arithmetic: 33.9 us -> 24.2 us  [corrected_step(): return coarse_step(coarse_state) + every[turn_no]]
    all_to_all x0 -> x2, starting transfers between devices: none -> 9.02 us  [chain(): every = lax.all_to_all(packed, 'tm', 0, 0, tiled=True)]
  transfers between devices with their start and end apart: 41 -> 28, of which waited for: 38 -> 25; matrix products, arithmetic and copies ran while one was open for 5% -> 6% of each run, Pallas kernels for 0% -> 0%
where the time goes in v9:
time: 545 us; the launch traced here: 541 us
  blocking collectives  157 us (29%)
  waiting for transfers between devices  123 us (23%)
  other arithmetic  107 us (20%)
  starting transfers between devices  98.8 us (18%)
  local copies, waits for them, and re-layouts  27.7 us (5%)
  between operations  21.4 us (4%)
  matrix products  5.93 us (1%)
    all_to_all x6, blocking collectives, global_sums(): gathered = lax.all_to_all(packed, ('sx', 'sy'), 0, 0, tiled=True)  124 us
    all_to_all x2, waiting for transfers between devices, chain(): every = lax.all_to_all(packed, 'tm', 0, 0, tiled=True)  48.2 us
    ppermute x11, starting transfers between devices, row_halo(): before = lax.ppermute(volume[-1:], ROW_AXES, up)  47.3 us
    all_to_all x1, waiting for transfers between devices, gather_grid(): gathered = lax.all_to_all(packed, ('sx', 'sy'), 0, 0, tiled=True)  30 us
    add x12, other arithmetic, corrected_step(): return coarse_step(coarse_state) + every[turn_no]  24.2 us
    all_to_all x1, blocking collectives, restrict_rows(): gathered = lax.all_to_all(packed, ROW_AXES, 0, 0, tiled=True)  22.7 us
    div x22, other arithmetic, fractional(): water_mobility / mobility  19.3 us
    sub x7, other arithmetic, coarse_step(): return coarse_state - balance / slope_sum  15.5 us
  transfers between devices with their start and end apart: 28, of which 25 were waited for; matrix products, arithmetic and copies ran while one was open for 6% of the time, Pallas kernels for 0%

profile of v9, /device:TPU:6, one launch (start us, length us, event | category | flops | bytes accessed | tf_op | source)
XLA Modules:
  0.0 540.5 jit_solution(14496229808965452609)
XLA Ops:
  17.1 4.5 all-to-all-start.1
  22.0 7.6 %all-to-all-done.1 = f32[4,6,1,16,256]{4,3,1,2,0:T(8,128)S(1)} async-done(((f32[4,6,1,16,256]{4,3,1,2,0:T(8,128)}), f32[4,6,1,16,256]{4,3,1,2,0:T(8,128)S(1)}, u32[]{:S(2)}, u32[]{:S(2)}) %all-to-all-start.1) | async-done | bytes 393248 | tf_op jit(solution)/shard_map/all_to_all | solution.py:296
  31.0 9.5 %all-to-all-start = ((f32[32,6,2,8,128]{4,3,2,1,0:T(8,128)}), f32[32,6,2,8,128]{4,3,2,1,0:T(8,128)S(1)}, u32[]{:S(2)}, u32[]{:S(2)}) async-start(f32[32,6,2,8,128]{4,3,2,1,0:T(8,128)} %broadcast_in_dim.151), calls=%async_computation | async-start | bytes 3145728 | tf_op jit(solution)/shard_map/all_to_all | solution.py:279
  42.4 4.4 collective-permute-start
  48.1 30.0 %all-to-all-done = f32[32,6,2,8,128]{4,3,2,1,0:T(8,128)S(1)} async-done(((f32[32,6,2,8,128]{4,3,2,1,0:T(8,128)}), f32[32,6,2,8,128]{4,3,2,1,0:T(8,128)S(1)}, u32[]{:S(2)}, u32[]{:S(2)}) %all-to-all-start) | async-done | bytes 1572896 | tf_op jit(solution)/shard_map/all_to_all | solution.py:279
  81.8 20.1 %while.37 = (s32[]{:T(128)}, f32[16,32,128]{2,1,0:T(8,128)}, s32[]{:T(128)}, f32[16,32,128]{2,1,0:T(8,128)S(1)}, f32[16,32,128]{2,1,0:T(8,128)S(1)}, /*index=5*/...) while((s32[]{:T(128)}, f32[16,32,128]{2,1,0:T(8,128)}, ...), condition=%wide.region_2.3_spmd, body=%wide.region_1.2_spmd.sunk | while | flops 4784130 | bytes 4980885 | solution.py:393
  115.6 5.3 collective-permute-start.5
  125.6 24.1 %all_to_all.71 = f32[32,1,2]{2,1,0:T(1,128)S(1)} all-to-all(f32[32,1,2]{2,1,0:T(1,128)S(1)} %broadcast_in_dim.156), channel_id=1, replica_groups=mesh['tm'=8,'sx'=8,'sy'=4] {'sx','sy'}, dimensions={0} | all-to-all | bytes 512 | tf_op jit(solution)/shard_map/all_to_all | solution.py:191
  155.2 4.5 collective-permute-start.7
  165.3 18.9 %all_to_all.72 = f32[32,1,2]{2,1,0:T(1,128)S(1)} all-to-all(f32[32,1,2]{2,1,0:T(1,128)S(1)} %broadcast_in_dim.157), channel_id=1, replica_groups=mesh['tm'=8,'sx'=8,'sy'=4] {'sx','sy'}, dimensions={0} | all-to-all | bytes 512 | tf_op jit(solution)/shard_map/all_to_all | solution.py:191
  192.7 4.5 collective-permute-start.9
  202.4 18.9 %all_to_all.73 = f32[32,1,2]{2,1,0:T(1,128)S(1)} all-to-all(f32[32,1,2]{2,1,0:T(1,128)S(1)} %broadcast_in_dim.158), channel_id=1, replica_groups=mesh['tm'=8,'sx'=8,'sy'=4] {'sx','sy'}, dimensions={0} | all-to-all | bytes 512 | tf_op jit(solution)/shard_map/all_to_all | solution.py:191
  231.2 4.5 collective-permute-start.11
  240.1 9.4 %all-to-all-start.5 = ((f32[32,1,32,128]{3,2,1,0:T(8,128)}), f32[32,1,32,128]{3,2,1,0:T(8,128)}, u32[]{:S(2)}, u32[]{:S(2)}) async-start(f32[32,1,32,128]{3,2,1,0:T(8,128)} %broadcast_in_dim.162), calls=%async_computation.5 | async-start | bytes 1048576 | tf_op jit(solution)/shard_map/all_to_all | solution.py:318
  251.3 12.1 %all-to-all-done.5 = f32[32,1,32,128]{3,2,1,0:T(8,128)} async-done(((f32[32,1,32,128]{3,2,1,0:T(8,128)}), f32[32,1,32,128]{3,2,1,0:T(8,128)}, u32[]{:S(2)}, u32[]{:S(2)}) %all-to-all-start.5) | async-done | bytes 524320 | tf_op jit(solution)/shard_map/all_to_all | solution.py:318
  269.5 4.5 all-to-all-start.6
  276.2 23.0 %all-to-all-done.6 = f32[8,16,32,128]{3,2,1,0:T(8,128)} async-done(((f32[8,16,32,128]{3,2,1,0:T(8,128)}), f32[8,16,32,128]{3,2,1,0:T(8,128)}, u32[]{:S(2)}, u32[]{:S(2)}) %all-to-all-start.6) | async-done | bytes 2097184 | tf_op jit(solution)/shard_map/all_to_all | solution.py:385
  299.2 20.6 %while.38 = (s32[]{:T(128)}, f32[16,32,128]{2,1,0:T(8,128)}, s32[]{:T(128)}, f32[16,32,128]{2,1,0:T(8,128)S(1)}, f32[16,32,128]{2,1,0:T(8,128)S(1)}, /*index=5*/...) while((s32[]{:T(128)}, f32[16,32,128]{2,1,0:T(8,128)}, ...), condition=%wide.region_14.16_spmd, body=%wide.region_13.15_spmd.sunk | while | flops 4849669 | bytes 5243091 | solution.py:390
  323.4 4.9 collective-permute-start.12
  333.6 4.3 collective-permute-done.14
  340.2 4.5 collective-permute-start.16
  349.3 24.5 %all_to_all.74 = f32[32,1,2]{2,1,0:T(1,128)S(1)} all-to-all(f32[32,1,2]{2,1,0:T(1,128)S(1)} %broadcast_in_dim.164), channel_id=1, replica_groups=mesh['tm'=8,'sx'=8,'sy'=4] {'sx','sy'}, dimensions={0} | all-to-all | bytes 512 | tf_op jit(solution)/shard_map/all_to_all | solution.py:191
  379.2 4.5 collective-permute-start.18
  389.3 18.9 %all_to_all.75 = f32[32,1,2]{2,1,0:T(1,128)S(1)} all-to-all(f32[32,1,2]{2,1,0:T(1,128)S(1)} %broadcast_in_dim.165), channel_id=1, replica_groups=mesh['tm'=8,'sx'=8,'sy'=4] {'sx','sy'}, dimensions={0} | all-to-all | bytes 512 | tf_op jit(solution)/shard_map/all_to_all | solution.py:191
  416.7 4.5 collective-permute-start.20
  426.4 18.9 %all_to_all.76 = f32[32,1,2]{2,1,0:T(1,128)S(1)} all-to-all(f32[32,1,2]{2,1,0:T(1,128)S(1)} %broadcast_in_dim.166), channel_id=1, replica_groups=mesh['tm'=8,'sx'=8,'sy'=4] {'sx','sy'}, dimensions={0} | all-to-all | bytes 512 | tf_op jit(solution)/shard_map/all_to_all | solution.py:191
  455.8 4.5 collective-permute-start.22
  463.5 22.7 %all_to_all.77 = f32[32,1,32,128]{3,2,1,0:T(8,128)S(1)} all-to-all(f32[32,1,32,128]{3,2,1,0:T(8,128)S(1)} %broadcast_in_dim.168), channel_id=1, replica_groups=mesh['tm'=8,'sx'=8,'sy'=4] {'sx','sy'}, dimensions={0} | all-to-all | bytes 1048576 | tf_op jit(solution)/shard_map/all_to_all | solution.py:318
  488.0 4.5 all-to-all-start.11
  492.5 25.2 %all-to-all-done.11 = f32[8,16,32,128]{3,2,1,0:T(8,128)} async-done(((f32[8,16,32,128]{3,2,1,0:T(8,128)}), f32[8,16,32,128]{3,2,1,0:T(8,128)}, u32[]{:S(2)}, u32[]{:S(2)}) %all-to-all-start.11) | async-done | bytes 2097184 | tf_op jit(solution)/shard_map/all_to_all | solution.py:385
  517.7 10.5 %while.39 = (s32[]{:T(128)}, f32[16,32,128]{2,1,0:T(8,128)S(1)}, s32[]{:T(128)}, f32[16,32,128]{2,1,0:T(8,128)S(1)}, f32[16,32,128]{2,1,0:T(8,128)S(1)}, /*index...) while((s32[]{:T(128)}, f32[16,32,128]{2,1,0:T(8,128)S(1)}, ...), condition=%wide.region_26.28_spmd, body=%wide.region_25.27_spmd.sunk | while | flops 4849669 | bytes 5243091 | solution.py:390
  530.1 9.8 %all_to_all.78 = f32[4,2,1,16,256]{4,3,2,1,0:T(8,128)S(1)} all-to-all(f32[4,2,1,16,256]{4,3,2,1,0:T(8,128)S(1)} %maximum_bitcast_fusion.2), channel_id=1, replica_groups=mesh['tm'=8,'sx'=8,'sy'=4] {'sy'}, dimensions={0} | all-to-all | bytes 262144 | tf_op jit(solution)/shard_map/all_to_all | solution.py:305
  (383 shorter events, 181.4 us)
Async XLA Ops:
  0.7 101.2 %copy-start.79 = (s32[256]{0:T(256)}, s32[256]{0:T(256)S(1)}, u32[]{:S(2)}) copy-start(s32[256]{0:T(256)S(1)} %get-tuple-element.794) | copy-start | bytes 3076
  17.1 12.5 %all-to-all-start.1 = ((f32[4,6,1,16,256]{4,3,1,2,0:T(8,128)}), f32[4,6,1,16,256]{4,3,1,2,0:T(8,128)S(1)}, u32[]{:S(2)}, u32[]{:S(2)}) async-start(f32[4,6,1,16,256]{4,3,1,2,0:T(8,128)} %bitcast.41), calls=%async_computation.1 | async-start | bytes 786432 | tf_op jit(solution)/shard_map/all_to_all | solution.py:296
  31.0 47.1 %all-to-all-start = ((f32[32,6,2,8,128]{4,3,2,1,0:T(8,128)}), f32[32,6,2,8,128]{4,3,2,1,0:T(8,128)S(1)}, u32[]{:S(2)}, u32[]{:S(2)}) async-start(f32[32,6,2,8,128]{4,3,2,1,0:T(8,128)} %broadcast_in_dim.151), calls=%async_computation | async-start | bytes 3145728 | tf_op jit(solution)/shard_map/all_to_all | solution.py:279
  40.5 62.3 %copy-start.70 = (pred[64]{0:T(512)(128)(4,1)}, pred[64]{0:T(512)(128)(4,1)S(1)}, u32[]{:S(2)}) copy-start(pred[64]{0:T(512)(128)(4,1)S(1)} %compare_and_fusion.1) | copy-start | bytes 196
  41.0 61.8 %copy-start.73 = (s32[64]{0:T(128)}, s32[64]{0:T(128)S(1)}, u32[]{:S(2)}) copy-start(s32[64]{0:T(128)S(1)} %get-tuple-element.798) | copy-start | bytes 772
  41.0 61.8 %copy-start.76 = (s32[64]{0:T(128)}, s32[64]{0:T(128)S(1)}, u32[]{:S(2)}) copy-start(s32[64]{0:T(128)S(1)} %get-tuple-element.799) | copy-start | bytes 772
  42.4 65.3 %collective-permute-start = (f32[1,3,64,256]{3,2,0,1:T(8,128)}, f32[1,3,64,256]{3,2,0,1:T(8,128)}, u32[]{:S(2)}, u32[]{:S(2)}) collective-permute-start(f32[1,3,64,256]{3,2,0,1:T(8,128)} %maximum_bitcast_fusion.1), channel_id=1, source_target_pairs={{0,1},{1,2},{2,3},{3,4},{4,5},{5,6},{6,7},{7,8},{8,9},{9,10},{10,1... | collective-permute-start | bytes 589832 | tf_op jit(solution)/shard_map/ppermute | solution.py:122
  46.8 61.0 %collective-permute-start.1 = (f32[1,3,64,256]{3,2,0,1:T(8,128)}, f32[1,3,64,256]{3,2,0,1:T(8,128)}, u32[]{:S(2)}, u32[]{:S(2)}) collective-permute-start(f32[1,3,64,256]{3,2,0,1:T(8,128)} %maximum_bitcast_fusion.1), channel_id=1, source_target_pairs={{1,0},{2,1},{3,2},{4,3},{5,4},{6,5},{7,6},{8,7},{9,8},{10,9},{11,1... | collective-permute-start | bytes 589832 | tf_op jit(solution)/shard_map/ppermute | solution.py:123
  103.1 5.9 %collective-permute-start.2 = (f32[1,64,256]{2,1,0:T(8,128)S(1)}, f32[1,64,256]{2,1,0:T(8,128)S(1)}, u32[]{:S(2)}, u32[]{:S(2)}) collective-permute-start(f32[1,64,256]{2,1,0:T(8,128)S(1)} %fusion.71), channel_id=1, source_target_pairs={{0,1},{1,2},{2,3},{3,4},{4,5},{5,6},{6,7},{7,8},{8,9},{9,10},{10,1... | collective-permute-start | bytes 196616 | tf_op jit(solution)/shard_map/ppermute | solution.py:122
  106.5 6.2 %collective-permute-start.3 = (f32[1,64,256]{2,1,0:T(8,128)S(1)}, f32[1,64,256]{2,1,0:T(8,128)S(1)}, u32[]{:S(2)}, u32[]{:S(2)}) collective-permute-start(f32[1,64,256]{2,1,0:T(8,128)S(1)} %fusion.71), channel_id=1, source_target_pairs={{1,0},{2,1},{3,2},{4,3},{5,4},{6,5},{7,6},{8,7},{9,8},{10,9},{11,1... | collective-permute-start | bytes 196616 | tf_op jit(solution)/shard_map/ppermute | solution.py:123
  114.3 6.9 %collective-permute-start.4 = (f32[1,64,256]{2,1,0:T(8,128)S(1)}, f32[1,64,256]{2,1,0:T(8,128)S(1)}, u32[]{:S(2)}, u32[]{:S(2)}) collective-permute-start(f32[1,64,256]{2,1,0:T(8,128)S(1)} %get-tuple-element.724), channel_id=1, source_target_pairs={{1,0},{2,1},{3,2},{4,3},{5,4},{6,5},{7,6},{8,7},{9,8},{10,9},{11,1... | collective-permute-start | bytes 196616 | tf_op jit(solution)/shard_map/ppermute | solution.py:123
  115.6 7.2 %collective-permute-start.5 = (f32[1,64,256]{2,1,0:T(8,128)S(1)}, f32[1,64,256]{2,1,0:T(8,128)S(1)}, u32[]{:S(2)}, u32[]{:S(2)}) collective-permute-start(f32[1,64,256]{2,1,0:T(8,128)S(1)} %get-tuple-element.724), channel_id=1, source_target_pairs={{0,1},{1,2},{2,3},{3,4},{4,5},{5,6},{6,7},{7,8},{8,9},{9,10},{10,1... | collective-permute-start | bytes 196616 | tf_op jit(solution)/shard_map/ppermute | solution.py:122
  153.9 6.2 %collective-permute-start.6 = (f32[1,64,256]{2,1,0:T(8,128)S(1)}, f32[1,64,256]{2,1,0:T(8,128)S(1)}, u32[]{:S(2)}, u32[]{:S(2)}) collective-permute-start(f32[1,64,256]{2,1,0:T(8,128)S(1)} %fusion.405), channel_id=1, source_target_pairs={{1,0},{2,1},{3,2},{4,3},{5,4},{6,5},{7,6},{8,7},{9,8},{10,9},{11,1... | collective-permute-start | bytes 196616 | tf_op jit(solution)/shard_map/ppermute | solution.py:123
  155.2 6.4 %collective-permute-start.7 = (f32[1,64,256]{2,1,0:T(8,128)S(1)}, f32[1,64,256]{2,1,0:T(8,128)S(1)}, u32[]{:S(2)}, u32[]{:S(2)}) collective-permute-start(f32[1,64,256]{2,1,0:T(8,128)S(1)} %fusion.405), channel_id=1, source_target_pairs={{0,1},{1,2},{2,3},{3,4},{4,5},{5,6},{6,7},{7,8},{8,9},{9,10},{10,1... | collective-permute-start | bytes 196616 | tf_op jit(solution)/shard_map/ppermute | solution.py:122
  191.4 6.2 %collective-permute-start.8 = (f32[1,64,256]{2,1,0:T(8,128)S(1)}, f32[1,64,256]{2,1,0:T(8,128)S(1)}, u32[]{:S(2)}, u32[]{:S(2)}) collective-permute-start(f32[1,64,256]{2,1,0:T(8,128)S(1)} %get-tuple-element.720), channel_id=1, source_target_pairs={{1,0},{2,1},{3,2},{4,3},{5,4},{6,5},{7,6},{8,7},{9,8},{10,9},{11,1... | collective-permute-start | bytes 196616 | tf_op jit(solution)/shard_map/ppermute | solution.py:123
  192.7 6.4 %collective-permute-start.9 = (f32[1,64,256]{2,1,0:T(8,128)S(1)}, f32[1,64,256]{2,1,0:T(8,128)S(1)}, u32[]{:S(2)}, u32[]{:S(2)}) collective-permute-start(f32[1,64,256]{2,1,0:T(8,128)S(1)} %get-tuple-element.720), channel_id=1, source_target_pairs={{0,1},{1,2},{2,3},{3,4},{4,5},{5,6},{6,7},{7,8},{8,9},{9,10},{10,1... | collective-permute-start | bytes 196616 | tf_op jit(solution)/shard_map/ppermute | solution.py:122
  229.9 6.2 %collective-permute-start.10 = (f32[1,64,256]{2,1,0:T(8,128)S(1)}, f32[1,64,256]{2,1,0:T(8,128)S(1)}, u32[]{:S(2)}, u32[]{:S(2)}) collective-permute-start(f32[1,64,256]{2,1,0:T(8,128)S(1)} %get-tuple-element.718), channel_id=1, source_target_pairs={{1,0},{2,1},{3,2},{4,3},{5,4},{6,5},{7,6},{8,7},{9,8},{10,9},{11,1... | collective-permute-start | bytes 196616 | tf_op jit(solution)/shard_map/ppermute | solution.py:123
  231.2 6.4 %collective-permute-start.11 = (f32[1,64,256]{2,1,0:T(8,128)S(1)}, f32[1,64,256]{2,1,0:T(8,128)S(1)}, u32[]{:S(2)}, u32[]{:S(2)}) collective-permute-start(f32[1,64,256]{2,1,0:T(8,128)S(1)} %get-tuple-element.718), channel_id=1, source_target_pairs={{0,1},{1,2},{2,3},{3,4},{4,5},{5,6},{6,7},{7,8},{8,9},{9,10},{10,1... | collective-permute-start | bytes 196616 | tf_op jit(solution)/shard_map/ppermute | solution.py:122
  240.1 23.3 %all-to-all-start.5 = ((f32[32,1,32,128]{3,2,1,0:T(8,128)}), f32[32,1,32,128]{3,2,1,0:T(8,128)}, u32[]{:S(2)}, u32[]{:S(2)}) async-start(f32[32,1,32,128]{3,2,1,0:T(8,128)} %broadcast_in_dim.162), calls=%async_computation.5 | async-start | bytes 1048576 | tf_op jit(solution)/shard_map/all_to_all | solution.py:318
  269.5 29.7 %all-to-all-start.6 = ((f32[8,16,32,128]{3,2,1,0:T(8,128)}), f32[8,16,32,128]{3,2,1,0:T(8,128)}, u32[]{:S(2)}, u32[]{:S(2)}) async-start(f32[8,16,32,128]{3,2,1,0:T(8,128)} %broadcast_in_dim.163), calls=%async_computation.6 | async-start | bytes 4194304 | tf_op jit(solution)/shard_map/all_to_all | solution.py:385
  323.4 5.8 %collective-permute-start.12 = (f32[1,64,256]{2,1,0:T(8,128)S(1)}, f32[1,64,256]{2,1,0:T(8,128)S(1)}, u32[]{:S(2)}, u32[]{:S(2)}) collective-permute-start(f32[1,64,256]{2,1,0:T(8,128)S(1)} %fusion.70), channel_id=1, source_target_pairs={{0,32},{32,64},{64,96},{96,128},{128,160},{160,192},{192,224},{1,3... | collective-permute-start | bytes 196616 | tf_op jit(solution)/shard_map/ppermute | solution.py:37
  329.2 4.4 collective-permute-start.13
  331.7 6.2 %collective-permute-start.14 = (f32[1,64,256]{2,1,0:T(8,128)S(1)}, f32[1,64,256]{2,1,0:T(8,128)S(1)}, u32[]{:S(2)}, u32[]{:S(2)}) collective-permute-start(f32[1,64,256]{2,1,0:T(8,128)S(1)} %broadcast_select_fusion), channel_id=1, source_target_pairs={{1,0},{2,1},{3,2},{4,3},{5,4},{6,5},{7,6},{8,7},{9,8},{10,9},{11,1... | collective-permute-start | bytes 196616 | tf_op jit(solution)/shard_map/ppermute | solution.py:123
  338.9 6.2 %collective-permute-start.15 = (f32[1,64,256]{2,1,0:T(8,128)S(1)}, f32[1,64,256]{2,1,0:T(8,128)S(1)}, u32[]{:S(2)}, u32[]{:S(2)}) collective-permute-start(f32[1,64,256]{2,1,0:T(8,128)S(1)} %get-tuple-element.708), channel_id=1, source_target_pairs={{1,0},{2,1},{3,2},{4,3},{5,4},{6,5},{7,6},{8,7},{9,8},{10,9},{11,1... | collective-permute-start | bytes 196616 | tf_op jit(solution)/shard_map/ppermute | solution.py:123
  340.2 6.4 %collective-permute-start.16 = (f32[1,64,256]{2,1,0:T(8,128)S(1)}, f32[1,64,256]{2,1,0:T(8,128)S(1)}, u32[]{:S(2)}, u32[]{:S(2)}) collective-permute-start(f32[1,64,256]{2,1,0:T(8,128)S(1)} %get-tuple-element.708), channel_id=1, source_target_pairs={{0,1},{1,2},{2,3},{3,4},{4,5},{5,6},{6,7},{7,8},{8,9},{9,10},{10,1... | collective-permute-start | bytes 196616 | tf_op jit(solution)/shard_map/ppermute | solution.py:122
  377.9 6.2 %collective-permute-start.17 = (f32[1,64,256]{2,1,0:T(8,128)S(1)}, f32[1,64,256]{2,1,0:T(8,128)S(1)}, u32[]{:S(2)}, u32[]{:S(2)}) collective-permute-start(f32[1,64,256]{2,1,0:T(8,128)S(1)} %fusion.406), channel_id=1, source_target_pairs={{1,0},{2,1},{3,2},{4,3},{5,4},{6,5},{7,6},{8,7},{9,8},{10,9},{11,1... | collective-permute-start | bytes 196616 | tf_op jit(solution)/shard_map/ppermute | solution.py:123
  379.2 6.4 %collective-permute-start.18 = (f32[1,64,256]{2,1,0:T(8,128)S(1)}, f32[1,64,256]{2,1,0:T(8,128)S(1)}, u32[]{:S(2)}, u32[]{:S(2)}) collective-permute-start(f32[1,64,256]{2,1,0:T(8,128)S(1)} %fusion.406), channel_id=1, source_target_pairs={{0,1},{1,2},{2,3},{3,4},{4,5},{5,6},{6,7},{7,8},{8,9},{9,10},{10,1... | collective-permute-start | bytes 196616 | tf_op jit(solution)/shard_map/ppermute | solution.py:122
  415.4 6.2 %collective-permute-start.19 = (f32[1,64,256]{2,1,0:T(8,128)S(1)}, f32[1,64,256]{2,1,0:T(8,128)S(1)}, u32[]{:S(2)}, u32[]{:S(2)}) collective-permute-start(f32[1,64,256]{2,1,0:T(8,128)S(1)} %get-tuple-element.704), channel_id=1, source_target_pairs={{1,0},{2,1},{3,2},{4,3},{5,4},{6,5},{7,6},{8,7},{9,8},{10,9},{11,1... | collective-permute-start | bytes 196616 | tf_op jit(solution)/shard_map/ppermute | solution.py:123
  416.7 6.4 %collective-permute-start.20 = (f32[1,64,256]{2,1,0:T(8,128)S(1)}, f32[1,64,256]{2,1,0:T(8,128)S(1)}, u32[]{:S(2)}, u32[]{:S(2)}) collective-permute-start(f32[1,64,256]{2,1,0:T(8,128)S(1)} %get-tuple-element.704), channel_id=1, source_target_pairs={{0,1},{1,2},{2,3},{3,4},{4,5},{5,6},{6,7},{7,8},{8,9},{9,10},{10,1... | collective-permute-start | bytes 196616 | tf_op jit(solution)/shard_map/ppermute | solution.py:122
  454.5 6.1 %collective-permute-start.21 = (f32[1,64,256]{2,1,0:T(8,128)S(1)}, f32[1,64,256]{2,1,0:T(8,128)S(1)}, u32[]{:S(2)}, u32[]{:S(2)}) collective-permute-start(f32[1,64,256]{2,1,0:T(8,128)S(1)} %get-tuple-element.702), channel_id=1, source_target_pairs={{1,0},{2,1},{3,2},{4,3},{5,4},{6,5},{7,6},{8,7},{9,8},{10,9},{11,1... | collective-permute-start | bytes 196616 | tf_op jit(solution)/shard_map/ppermute | solution.py:123
  455.8 6.7 %collective-permute-start.22 = (f32[1,64,256]{2,1,0:T(8,128)S(1)}, f32[1,64,256]{2,1,0:T(8,128)S(1)}, u32[]{:S(2)}, u32[]{:S(2)}) collective-permute-start(f32[1,64,256]{2,1,0:T(8,128)S(1)} %get-tuple-element.702), channel_id=1, source_target_pairs={{0,1},{1,2},{2,3},{3,4},{4,5},{5,6},{6,7},{7,8},{8,9},{9,10},{10,1... | collective-permute-start | bytes 196616 | tf_op jit(solution)/shard_map/ppermute | solution.py:122
  488.0 29.7 %all-to-all-start.11 = ((f32[8,16,32,128]{3,2,1,0:T(8,128)}), f32[8,16,32,128]{3,2,1,0:T(8,128)}, u32[]{:S(2)}, u32[]{:S(2)}) async-start(f32[8,16,32,128]{3,2,1,0:T(8,128)} %broadcast_in_dim.169), calls=%async_computation.11 | async-start | bytes 4194304 | tf_op jit(solution)/shard_map/all_to_all | solution.py:385
  (89 other events, 915.3 us)

commit v10 on v9

--- a/solution.py
+++ b/solution.py
@@ -381,13 +381,22 @@
         return coarse_state - balance / slope_sum
 
     def chain(corrections):
-        packed = jnp.broadcast_to(corrections[None], (slices,) + corrections.shape)
-        every = lax.all_to_all(packed, "tm", 0, 0, tiled=True)
-
-        def corrected_step(turn_no, coarse_state):
-            return coarse_step(coarse_state) + every[turn_no]
-
-        coarse_state = lax.fori_loop(0, slice_index, corrected_step, start_coarse)
+        ahead = corrections[None]
+        collected = [jnp.zeros_like(ahead)]
+        steps = 1
+        while steps < slices:
+            arrived = passed_along(ahead, "tm", steps)
+            collected.insert(1, arrived)
+            ahead = jnp.concatenate([arrived, ahead])
+            steps *= 2
+        ahead = jnp.concatenate(collected)
+        offset = ahead.shape[0] - 1 - slice_index
+
+        def corrected_step(turn_no, coarse_image):
+            return coarse_step(coarse_image + ahead[turn_no + offset])
+
+        coarse_image = lax.fori_loop(0, slice_index, corrected_step, start_coarse)
+        coarse_state = coarse_image + ahead[slice_index + offset]
         return (coarse_state, coarse_step(coarse_state))
 
     coarse_state = lax.fori_loop(

time: 545 us -> 598 us (1.097)
  waiting for transfers between devices: 123 us -> 160 us
  other arithmetic: 107 us -> 125 us
    ppermute x1 -> x7, waiting for transfers between devices: 0.88 us -> 86.7 us  [passed_along(): lax.ppermute(value, axis, [(source, source + steps) for source in range(i...]
    all_to_all x2 -> x0, waiting for transfers between devices: 48.2 us -> none  [chain(): every = lax.all_to_all(packed, 'tm', 0, 0, tiled=True)]
    sub x7 -> x19, other arithmetic: 15.5 us -> 40 us  [coarse_step(): return coarse_state - balance / slope_sum]
    add x12 -> x0, other arithmetic: 24.2 us -> none  [corrected_step(): return coarse_step(coarse_state) + every[turn_no]]
    all_to_all x2 -> x0, starting transfers between devices: 9.02 us -> none  [chain(): every = lax.all_to_all(packed, 'tm', 0, 0, tiled=True)]
    concatenate x0 -> x6, other arithmetic: none -> 8.66 us  [the longest x2 6.36 us: chain(): ahead = jnp.concatenate(collected)]
    div x22, other arithmetic: 19.3 us -> 25.8 us  [fractional(): water_mobility / mobility]
    ppermute x1 -> x7, starting transfers between devices: 4.89 us -> 10.9 us  [passed_along(): lax.ppermute(value, axis, [(source, source + steps) for source in range(i...]
  transfers between devices with their start and end apart: 28 -> 32, of which waited for: 25 -> 29; matrix products, arithmetic and copies ran while one was open for 6% -> 5% of each run, Pallas kernels for 0% -> 0%
where the time goes in v10:
time: 598 us; the launch traced here: 593 us
  waiting for transfers between devices  160 us (27%)
  blocking collectives  159 us (27%)
  other arithmetic  125 us (21%)
  starting transfers between devices  95.9 us (16%)
  local copies, waits for them, and re-layouts  24.8 us (4%)
  between operations  23 us (4%)
    all_to_all x6, blocking collectives, global_sums(): gathered = lax.all_to_all(packed, ('sx', 'sy'), 0, 0, tiled=True)  124 us
    ppermute x7, waiting for transfers between devices, passed_along(): lax.ppermute(value, axis, [(source, source + steps) for source in range(i...  86.7 us
    ppermute x11, starting transfers between devices, row_halo(): before = lax.ppermute(volume[-1:], ROW_AXES, up)  47.4 us
    sub x19, other arithmetic, coarse_step(): return coarse_state - balance / slope_sum  40 us
    all_to_all x1, waiting for transfers between devices, gather_grid(): gathered = lax.all_to_all(packed, ('sx', 'sy'), 0, 0, tiled=True)  29.9 us
    div x22, other arithmetic, fractional(): water_mobility / mobility  25.8 us
    all_to_all x1, blocking collectives, restrict_rows(): gathered = lax.all_to_all(packed, ROW_AXES, 0, 0, tiled=True)  25.7 us
    ppermute x11, starting transfers between devices, row_halo(): after = lax.ppermute(volume[:1], ROW_AXES, down)  14.2 us
  transfers between devices with their start and end apart: 32, of which 29 were waited for; matrix products, arithmetic and copies ran while one was open for 5% of the time, Pallas kernels for 0%

profile of v10, /device:TPU:6, one launch (start us, length us, event | category | flops | bytes accessed | tf_op | source)
XLA Modules:
  0.0 593.2 jit_solution(15201353536118024956)
XLA Ops:
  17.1 4.5 all-to-all-start.1
  22.0 7.6 %all-to-all-done.1 = f32[4,6,1,16,256]{4,3,1,2,0:T(8,128)S(1)} async-done(((f32[4,6,1,16,256]{4,3,1,2,0:T(8,128)}), f32[4,6,1,16,256]{4,3,1,2,0:T(8,128)S(1)}, u32[]{:S(2)}, u32[]{:S(2)}) %all-to-all-start.1) | async-done | bytes 393248 | tf_op jit(solution)/shard_map/all_to_all | solution.py:296
  30.9 9.5 %all-to-all-start = ((f32[32,6,2,8,128]{4,3,2,1,0:T(8,128)}), f32[32,6,2,8,128]{4,3,2,1,0:T(8,128)S(1)}, u32[]{:S(2)}, u32[]{:S(2)}) async-start(f32[32,6,2,8,128]{4,3,2,1,0:T(8,128)} %broadcast_in_dim.145), calls=%async_computation | async-start | bytes 3145728 | tf_op jit(solution)/shard_map/all_to_all | solution.py:279
  42.5 4.4 collective-permute-start
  48.1 29.9 %all-to-all-done = f32[32,6,2,8,128]{4,3,2,1,0:T(8,128)S(1)} async-done(((f32[32,6,2,8,128]{4,3,2,1,0:T(8,128)}), f32[32,6,2,8,128]{4,3,2,1,0:T(8,128)S(1)}, u32[]{:S(2)}, u32[]{:S(2)}) %all-to-all-start) | async-done | bytes 1572896 | tf_op jit(solution)/shard_map/all_to_all | solution.py:279
  81.8 20.3 %while.37 = (s32[]{:T(128)}, f32[16,32,128]{2,1,0:T(8,128)}, s32[]{:T(128)}, f32[16,32,128]{2,1,0:T(8,128)S(1)}, f32[16,32,128]{2,1,0:T(8,128)S(1)}, /*index=5*/...) while((s32[]{:T(128)}, f32[16,32,128]{2,1,0:T(8,128)}, ...), condition=%wide.region_2.3_spmd, body=%wide.region_1.2_spmd.sunk | while | flops 4784130 | bytes 4980885 | solution.py:402
  115.8 5.3 collective-permute-start.5
  125.7 24.1 %all_to_all.61 = f32[32,1,2]{2,1,0:T(1,128)S(1)} all-to-all(f32[32,1,2]{2,1,0:T(1,128)S(1)} %broadcast_in_dim.150), channel_id=1, replica_groups=mesh['tm'=8,'sx'=8,'sy'=4] {'sx','sy'}, dimensions={0} | all-to-all | bytes 512 | tf_op jit(solution)/shard_map/all_to_all | solution.py:191
  155.4 4.5 collective-permute-start.7
  165.7 18.9 %all_to_all.62 = f32[32,1,2]{2,1,0:T(1,128)S(1)} all-to-all(f32[32,1,2]{2,1,0:T(1,128)S(1)} %broadcast_in_dim.151), channel_id=1, replica_groups=mesh['tm'=8,'sx'=8,'sy'=4] {'sx','sy'}, dimensions={0} | all-to-all | bytes 512 | tf_op jit(solution)/shard_map/all_to_all | solution.py:191
  193.5 4.5 collective-permute-start.9
  203.2 18.9 %all_to_all.63 = f32[32,1,2]{2,1,0:T(1,128)S(1)} all-to-all(f32[32,1,2]{2,1,0:T(1,128)S(1)} %broadcast_in_dim.152), channel_id=1, replica_groups=mesh['tm'=8,'sx'=8,'sy'=4] {'sx','sy'}, dimensions={0} | all-to-all | bytes 512 | tf_op jit(solution)/shard_map/all_to_all | solution.py:191
  232.3 4.5 collective-permute-start.11
  241.1 9.4 %all-to-all-start.5 = ((f32[32,1,32,128]{3,2,1,0:T(8,128)}), f32[32,1,32,128]{3,2,1,0:T(8,128)}, u32[]{:S(2)}, u32[]{:S(2)}) async-start(f32[32,1,32,128]{3,2,1,0:T(8,128)} %broadcast_in_dim.156), calls=%async_computation.5 | async-start | bytes 1048576 | tf_op jit(solution)/shard_map/all_to_all | solution.py:318
  252.3 12.1 %all-to-all-done.5 = f32[32,1,32,128]{3,2,1,0:T(8,128)} async-done(((f32[32,1,32,128]{3,2,1,0:T(8,128)}), f32[32,1,32,128]{3,2,1,0:T(8,128)}, u32[]{:S(2)}, u32[]{:S(2)}) %all-to-all-start.5) | async-done | bytes 524320 | tf_op jit(solution)/shard_map/all_to_all | solution.py:318
  270.9 5.8 collective-permute-done.12
  278.0 12.3 %collective-permute-done.13 = f32[2,16,32,128]{3,2,1,0:T(8,128)S(1)} collective-permute-done((f32[2,16,32,128]{3,2,1,0:T(8,128)S(1)}, f32[2,16,32,128]{3,2,1,0:T(8,128)S(1)}, u32[]{:S(2)}, u32[]{:S(2)}) %collective-permute-start.13) | collective-permute-done | bytes 524320 | tf_op jit(solution)/shard_map/ppermute | solution.py:37
  295.0 22.3 %collective-permute-done.14 = f32[4,16,32,128]{3,2,1,0:T(8,128)} collective-permute-done((f32[4,16,32,128]{3,2,1,0:T(8,128)}, f32[4,16,32,128]{3,2,1,0:T(8,128)}, u32[]{:S(2)}, u32[]{:S(2)}) %collective-permute-start.14) | collective-permute-done | bytes 1048608 | tf_op jit(solution)/shard_map/ppermute | solution.py:37
  320.5 21.3 %while.38 = (s32[]{:T(128)}, f32[16,32,128]{2,1,0:T(8,128)}, s32[]{:T(128)}, s32[]{:T(128)}, f32[8,16,32,128]{3,2,1,0:T(8,128)}, /*index=5*/f32[16,32,128]{2,1,0...) while((s32[]{:T(128)}, f32[16,32,128]{2,1,0:T(8,128)}, ...), condition=%wide.region_14.16_spmd, body=%wide.region_13.15_spmd.sunk | while | flops 4915206 | bytes 5505259 | solution.py:398
  362.1 4.5 collective-permute-start.19
  371.5 24.5 %all_to_all.64 = f32[32,1,2]{2,1,0:T(1,128)S(1)} all-to-all(f32[32,1,2]{2,1,0:T(1,128)S(1)} %broadcast_in_dim.158), channel_id=1, replica_groups=mesh['tm'=8,'sx'=8,'sy'=4] {'sx','sy'}, dimensions={0} | all-to-all | bytes 512 | tf_op jit(solution)/shard_map/all_to_all | solution.py:191
  401.7 4.5 collective-permute-start.21
  412.0 18.9 %all_to_all.65 = f32[32,1,2]{2,1,0:T(1,128)S(1)} all-to-all(f32[32,1,2]{2,1,0:T(1,128)S(1)} %broadcast_in_dim.159), channel_id=1, replica_groups=mesh['tm'=8,'sx'=8,'sy'=4] {'sx','sy'}, dimensions={0} | all-to-all | bytes 512 | tf_op jit(solution)/shard_map/all_to_all | solution.py:191
  439.9 4.5 collective-permute-start.23
  449.6 18.9 %all_to_all.66 = f32[32,1,2]{2,1,0:T(1,128)S(1)} all-to-all(f32[32,1,2]{2,1,0:T(1,128)S(1)} %broadcast_in_dim.160), channel_id=1, replica_groups=mesh['tm'=8,'sx'=8,'sy'=4] {'sx','sy'}, dimensions={0} | all-to-all | bytes 512 | tf_op jit(solution)/shard_map/all_to_all | solution.py:191
  479.1 4.5 collective-permute-start.25
  486.6 25.7 %all_to_all.67 = f32[32,1,32,128]{3,2,1,0:T(8,128)S(1)} all-to-all(f32[32,1,32,128]{3,2,1,0:T(8,128)S(1)} %broadcast_in_dim.162), channel_id=1, replica_groups=mesh['tm'=8,'sx'=8,'sy'=4] {'sx','sy'}, dimensions={0} | all-to-all | bytes 1048576 | tf_op jit(solution)/shard_map/all_to_all | solution.py:318
  514.4 5.8 collective-permute-done.26
  521.5 12.3 %collective-permute-done.27 = f32[2,16,32,128]{3,2,1,0:T(8,128)S(1)} collective-permute-done((f32[2,16,32,128]{3,2,1,0:T(8,128)S(1)}, f32[2,16,32,128]{3,2,1,0:T(8,128)S(1)}, u32[]{:S(2)}, u32[]{:S(2)}) %collective-permute-start.27) | collective-permute-done | bytes 524320 | tf_op jit(solution)/shard_map/ppermute | solution.py:37
  536.3 24.5 %collective-permute-done.28 = f32[4,16,32,128]{3,2,1,0:T(8,128)} collective-permute-done((f32[4,16,32,128]{3,2,1,0:T(8,128)}, f32[4,16,32,128]{3,2,1,0:T(8,128)}, u32[]{:S(2)}, u32[]{:S(2)}) %collective-permute-start.28) | collective-permute-done | bytes 1048608 | tf_op jit(solution)/shard_map/ppermute | solution.py:37
  564.0 16.3 %while.39 = (s32[]{:T(128)}, f32[16,32,128]{2,1,0:T(8,128)S(1)}, s32[]{:T(128)}, s32[]{:T(128)}, f32[8,16,32,128]{3,2,1,0:T(8,128)}, /*index=5*/f32[16,32,128]{2...) while((s32[]{:T(128)}, f32[16,32,128]{2,1,0:T(8,128)S(1)}, ...), condition=%wide.region_26.28_spmd, body=%wide.region_25.27_spmd.sunk | while | flops 4915206 | bytes 5505259 | solution.py:398
  583.4 9.1 %all_to_all.68 = f32[4,2,1,16,256]{4,3,2,1,0:T(8,128)S(1)} all-to-all(f32[4,2,1,16,256]{4,3,2,1,0:T(8,128)S(1)} %maximum_bitcast_fusion.2), channel_id=1, replica_groups=mesh['tm'=8,'sx'=8,'sy'=4] {'sy'}, dimensions={0} | all-to-all | bytes 262144 | tf_op jit(solution)/shard_map/all_to_all | solution.py:305
  (409 shorter events, 213.5 us)
Async XLA Ops:
  17.1 12.5 %all-to-all-start.1 = ((f32[4,6,1,16,256]{4,3,1,2,0:T(8,128)}), f32[4,6,1,16,256]{4,3,1,2,0:T(8,128)S(1)}, u32[]{:S(2)}, u32[]{:S(2)}) async-start(f32[4,6,1,16,256]{4,3,1,2,0:T(8,128)} %bitcast.35), calls=%async_computation.1 | async-start | bytes 786432 | tf_op jit(solution)/shard_map/all_to_all | solution.py:296
  30.9 47.1 %all-to-all-start = ((f32[32,6,2,8,128]{4,3,2,1,0:T(8,128)}), f32[32,6,2,8,128]{4,3,2,1,0:T(8,128)S(1)}, u32[]{:S(2)}, u32[]{:S(2)}) async-start(f32[32,6,2,8,128]{4,3,2,1,0:T(8,128)} %broadcast_in_dim.145), calls=%async_computation | async-start | bytes 3145728 | tf_op jit(solution)/shard_map/all_to_all | solution.py:279
  42.5 65.5 %collective-permute-start = (f32[1,3,64,256]{3,2,0,1:T(8,128)}, f32[1,3,64,256]{3,2,0,1:T(8,128)}, u32[]{:S(2)}, u32[]{:S(2)}) collective-permute-start(f32[1,3,64,256]{3,2,0,1:T(8,128)} %maximum_bitcast_fusion.1), channel_id=1, source_target_pairs={{0,1},{1,2},{2,3},{3,4},{4,5},{5,6},{6,7},{7,8},{8,9},{9,10},{10,1... | collective-permute-start | bytes 589832 | tf_op jit(solution)/shard_map/ppermute | solution.py:122
  46.8 61.2 %collective-permute-start.1 = (f32[1,3,64,256]{3,2,0,1:T(8,128)}, f32[1,3,64,256]{3,2,0,1:T(8,128)}, u32[]{:S(2)}, u32[]{:S(2)}) collective-permute-start(f32[1,3,64,256]{3,2,0,1:T(8,128)} %maximum_bitcast_fusion.1), channel_id=1, source_target_pairs={{1,0},{2,1},{3,2},{4,3},{5,4},{6,5},{7,6},{8,7},{9,8},{10,9},{11,1... | collective-permute-start | bytes 589832 | tf_op jit(solution)/shard_map/ppermute | solution.py:123
  103.3 5.9 collective-permute-start.2
  106.7 6.2 %collective-permute-start.3 = (f32[1,64,256]{2,1,0:T(8,128)S(1)}, f32[1,64,256]{2,1,0:T(8,128)S(1)}, u32[]{:S(2)}, u32[]{:S(2)}) collective-permute-start(f32[1,64,256]{2,1,0:T(8,128)S(1)} %fusion.69), channel_id=1, source_target_pairs={{1,0},{2,1},{3,2},{4,3},{5,4},{6,5},{7,6},{8,7},{9,8},{10,9},{11,1... | collective-permute-start | bytes 196616 | tf_op jit(solution)/shard_map/ppermute | solution.py:123
  114.5 6.9 %collective-permute-start.4 = (f32[1,64,256]{2,1,0:T(8,128)S(1)}, f32[1,64,256]{2,1,0:T(8,128)S(1)}, u32[]{:S(2)}, u32[]{:S(2)}) collective-permute-start(f32[1,64,256]{2,1,0:T(8,128)S(1)} %get-tuple-element.753), channel_id=1, source_target_pairs={{1,0},{2,1},{3,2},{4,3},{5,4},{6,5},{7,6},{8,7},{9,8},{10,9},{11,1... | collective-permute-start | bytes 196616 | tf_op jit(solution)/shard_map/ppermute | solution.py:123
  115.8 7.2 %collective-permute-start.5 = (f32[1,64,256]{2,1,0:T(8,128)S(1)}, f32[1,64,256]{2,1,0:T(8,128)S(1)}, u32[]{:S(2)}, u32[]{:S(2)}) collective-permute-start(f32[1,64,256]{2,1,0:T(8,128)S(1)} %get-tuple-element.753), channel_id=1, source_target_pairs={{0,1},{1,2},{2,3},{3,4},{4,5},{5,6},{6,7},{7,8},{8,9},{9,10},{10,1... | collective-permute-start | bytes 196616 | tf_op jit(solution)/shard_map/ppermute | solution.py:122
  154.1 6.2 %collective-permute-start.6 = (f32[1,64,256]{2,1,0:T(8,128)S(1)}, f32[1,64,256]{2,1,0:T(8,128)S(1)}, u32[]{:S(2)}, u32[]{:S(2)}) collective-permute-start(f32[1,64,256]{2,1,0:T(8,128)S(1)} %fusion.403), channel_id=1, source_target_pairs={{1,0},{2,1},{3,2},{4,3},{5,4},{6,5},{7,6},{8,7},{9,8},{10,9},{11,1... | collective-permute-start | bytes 196616 | tf_op jit(solution)/shard_map/ppermute | solution.py:123
  155.4 6.4 %collective-permute-start.7 = (f32[1,64,256]{2,1,0:T(8,128)S(1)}, f32[1,64,256]{2,1,0:T(8,128)S(1)}, u32[]{:S(2)}, u32[]{:S(2)}) collective-permute-start(f32[1,64,256]{2,1,0:T(8,128)S(1)} %fusion.403), channel_id=1, source_target_pairs={{0,1},{1,2},{2,3},{3,4},{4,5},{5,6},{6,7},{7,8},{8,9},{9,10},{10,1... | collective-permute-start | bytes 196616 | tf_op jit(solution)/shard_map/ppermute | solution.py:122
  192.2 6.2 %collective-permute-start.8 = (f32[1,64,256]{2,1,0:T(8,128)S(1)}, f32[1,64,256]{2,1,0:T(8,128)S(1)}, u32[]{:S(2)}, u32[]{:S(2)}) collective-permute-start(f32[1,64,256]{2,1,0:T(8,128)S(1)} %get-tuple-element.749), channel_id=1, source_target_pairs={{1,0},{2,1},{3,2},{4,3},{5,4},{6,5},{7,6},{8,7},{9,8},{10,9},{11,1... | collective-permute-start | bytes 196616 | tf_op jit(solution)/shard_map/ppermute | solution.py:123
  193.5 6.4 %collective-permute-start.9 = (f32[1,64,256]{2,1,0:T(8,128)S(1)}, f32[1,64,256]{2,1,0:T(8,128)S(1)}, u32[]{:S(2)}, u32[]{:S(2)}) collective-permute-start(f32[1,64,256]{2,1,0:T(8,128)S(1)} %get-tuple-element.749), channel_id=1, source_target_pairs={{0,1},{1,2},{2,3},{3,4},{4,5},{5,6},{6,7},{7,8},{8,9},{9,10},{10,1... | collective-permute-start | bytes 196616 | tf_op jit(solution)/shard_map/ppermute | solution.py:122
  231.0 6.2 %collective-permute-start.10 = (f32[1,64,256]{2,1,0:T(8,128)S(1)}, f32[1,64,256]{2,1,0:T(8,128)S(1)}, u32[]{:S(2)}, u32[]{:S(2)}) collective-permute-start(f32[1,64,256]{2,1,0:T(8,128)S(1)} %get-tuple-element.747), channel_id=1, source_target_pairs={{1,0},{2,1},{3,2},{4,3},{5,4},{6,5},{7,6},{8,7},{9,8},{10,9},{11,1... | collective-permute-start | bytes 196616 | tf_op jit(solution)/shard_map/ppermute | solution.py:123
  232.3 6.4 %collective-permute-start.11 = (f32[1,64,256]{2,1,0:T(8,128)S(1)}, f32[1,64,256]{2,1,0:T(8,128)S(1)}, u32[]{:S(2)}, u32[]{:S(2)}) collective-permute-start(f32[1,64,256]{2,1,0:T(8,128)S(1)} %get-tuple-element.747), channel_id=1, source_target_pairs={{0,1},{1,2},{2,3},{3,4},{4,5},{5,6},{6,7},{7,8},{8,9},{9,10},{10,1... | collective-permute-start | bytes 196616 | tf_op jit(solution)/shard_map/ppermute | solution.py:122
  241.1 23.3 %all-to-all-start.5 = ((f32[32,1,32,128]{3,2,1,0:T(8,128)}), f32[32,1,32,128]{3,2,1,0:T(8,128)}, u32[]{:S(2)}, u32[]{:S(2)}) async-start(f32[32,1,32,128]{3,2,1,0:T(8,128)} %broadcast_in_dim.156), calls=%async_computation.5 | async-start | bytes 1048576 | tf_op jit(solution)/shard_map/all_to_all | solution.py:318
  269.0 7.7 %collective-permute-start.12 = (f32[1,16,32,128]{3,2,1,0:T(8,128)S(1)}, f32[1,16,32,128]{3,2,1,0:T(8,128)S(1)}, u32[]{:S(2)}, u32[]{:S(2)}) collective-permute-start(f32[1,16,32,128]{3,2,1,0:T(8,128)S(1)} %get-tuple-element.745), channel_id=1, source_target_pairs={{0,32},{32,64},{64,96},{96,128},{128,160},{160,192},{192,224},{1,3... | collective-permute-start | bytes 786440 | tf_op jit(solution)/shard_map/ppermute | solution.py:37
  276.7 13.6 %collective-permute-start.13 = (f32[2,16,32,128]{3,2,1,0:T(8,128)S(1)}, f32[2,16,32,128]{3,2,1,0:T(8,128)S(1)}, u32[]{:S(2)}, u32[]{:S(2)}) collective-permute-start(f32[2,16,32,128]{3,2,1,0:T(8,128)S(1)} %pad_maximum_fusion.4), channel_id=1, source_target_pairs={{0,64},{32,96},{64,128},{96,160},{128,192},{160,224},{1,65},{33,97... | collective-permute-start | bytes 1572872 | tf_op jit(solution)/shard_map/ppermute | solution.py:37
  291.5 25.8 %collective-permute-start.14 = (f32[4,16,32,128]{3,2,1,0:T(8,128)}, f32[4,16,32,128]{3,2,1,0:T(8,128)}, u32[]{:S(2)}, u32[]{:S(2)}) collective-permute-start(f32[4,16,32,128]{3,2,1,0:T(8,128)} %pad_maximum_fusion.2), channel_id=1, source_target_pairs={{0,128},{32,160},{64,192},{96,224},{1,129},{33,161},{65,193},{97,2... | collective-permute-start | bytes 3145736 | tf_op jit(solution)/shard_map/ppermute | solution.py:37
  345.6 5.6 collective-permute-start.15
  351.2 4.4 collective-permute-start.16
  353.7 6.2 %collective-permute-start.17 = (f32[1,64,256]{2,1,0:T(8,128)S(1)}, f32[1,64,256]{2,1,0:T(8,128)S(1)}, u32[]{:S(2)}, u32[]{:S(2)}) collective-permute-start(f32[1,64,256]{2,1,0:T(8,128)S(1)} %broadcast_select_fusion), channel_id=1, source_target_pairs={{1,0},{2,1},{3,2},{4,3},{5,4},{6,5},{7,6},{8,7},{9,8},{10,9},{11,1... | collective-permute-start | bytes 196616 | tf_op jit(solution)/shard_map/ppermute | solution.py:123
  360.8 6.2 %collective-permute-start.18 = (f32[1,64,256]{2,1,0:T(8,128)S(1)}, f32[1,64,256]{2,1,0:T(8,128)S(1)}, u32[]{:S(2)}, u32[]{:S(2)}) collective-permute-start(f32[1,64,256]{2,1,0:T(8,128)S(1)} %get-tuple-element.737), channel_id=1, source_target_pairs={{1,0},{2,1},{3,2},{4,3},{5,4},{6,5},{7,6},{8,7},{9,8},{10,9},{11,1... | collective-permute-start | bytes 196616 | tf_op jit(solution)/shard_map/ppermute | solution.py:123
  362.1 6.4 %collective-permute-start.19 = (f32[1,64,256]{2,1,0:T(8,128)S(1)}, f32[1,64,256]{2,1,0:T(8,128)S(1)}, u32[]{:S(2)}, u32[]{:S(2)}) collective-permute-start(f32[1,64,256]{2,1,0:T(8,128)S(1)} %get-tuple-element.737), channel_id=1, source_target_pairs={{0,1},{1,2},{2,3},{3,4},{4,5},{5,6},{6,7},{7,8},{8,9},{9,10},{10,1... | collective-permute-start | bytes 196616 | tf_op jit(solution)/shard_map/ppermute | solution.py:122
  400.4 6.2 %collective-permute-start.20 = (f32[1,64,256]{2,1,0:T(8,128)S(1)}, f32[1,64,256]{2,1,0:T(8,128)S(1)}, u32[]{:S(2)}, u32[]{:S(2)}) collective-permute-start(f32[1,64,256]{2,1,0:T(8,128)S(1)} %fusion.404), channel_id=1, source_target_pairs={{1,0},{2,1},{3,2},{4,3},{5,4},{6,5},{7,6},{8,7},{9,8},{10,9},{11,1... | collective-permute-start | bytes 196616 | tf_op jit(solution)/shard_map/ppermute | solution.py:123
  401.7 6.4 %collective-permute-start.21 = (f32[1,64,256]{2,1,0:T(8,128)S(1)}, f32[1,64,256]{2,1,0:T(8,128)S(1)}, u32[]{:S(2)}, u32[]{:S(2)}) collective-permute-start(f32[1,64,256]{2,1,0:T(8,128)S(1)} %fusion.404), channel_id=1, source_target_pairs={{0,1},{1,2},{2,3},{3,4},{4,5},{5,6},{6,7},{7,8},{8,9},{9,10},{10,1... | collective-permute-start | bytes 196616 | tf_op jit(solution)/shard_map/ppermute | solution.py:122
  438.6 6.2 %collective-permute-start.22 = (f32[1,64,256]{2,1,0:T(8,128)S(1)}, f32[1,64,256]{2,1,0:T(8,128)S(1)}, u32[]{:S(2)}, u32[]{:S(2)}) collective-permute-start(f32[1,64,256]{2,1,0:T(8,128)S(1)} %get-tuple-element.733), channel_id=1, source_target_pairs={{1,0},{2,1},{3,2},{4,3},{5,4},{6,5},{7,6},{8,7},{9,8},{10,9},{11,1... | collective-permute-start | bytes 196616 | tf_op jit(solution)/shard_map/ppermute | solution.py:123
  439.9 6.4 %collective-permute-start.23 = (f32[1,64,256]{2,1,0:T(8,128)S(1)}, f32[1,64,256]{2,1,0:T(8,128)S(1)}, u32[]{:S(2)}, u32[]{:S(2)}) collective-permute-start(f32[1,64,256]{2,1,0:T(8,128)S(1)} %get-tuple-element.733), channel_id=1, source_target_pairs={{0,1},{1,2},{2,3},{3,4},{4,5},{5,6},{6,7},{7,8},{8,9},{9,10},{10,1... | collective-permute-start | bytes 196616 | tf_op jit(solution)/shard_map/ppermute | solution.py:122
  477.8 6.1 %collective-permute-start.24 = (f32[1,64,256]{2,1,0:T(8,128)S(1)}, f32[1,64,256]{2,1,0:T(8,128)S(1)}, u32[]{:S(2)}, u32[]{:S(2)}) collective-permute-start(f32[1,64,256]{2,1,0:T(8,128)S(1)} %get-tuple-element.731), channel_id=1, source_target_pairs={{1,0},{2,1},{3,2},{4,3},{5,4},{6,5},{7,6},{8,7},{9,8},{10,9},{11,1... | collective-permute-start | bytes 196616 | tf_op jit(solution)/shard_map/ppermute | solution.py:123
  479.1 6.5 %collective-permute-start.25 = (f32[1,64,256]{2,1,0:T(8,128)S(1)}, f32[1,64,256]{2,1,0:T(8,128)S(1)}, u32[]{:S(2)}, u32[]{:S(2)}) collective-permute-start(f32[1,64,256]{2,1,0:T(8,128)S(1)} %get-tuple-element.731), channel_id=1, source_target_pairs={{0,1},{1,2},{2,3},{3,4},{4,5},{5,6},{6,7},{7,8},{8,9},{9,10},{10,1... | collective-permute-start | bytes 196616 | tf_op jit(solution)/shard_map/ppermute | solution.py:122
  512.5 7.7 %collective-permute-start.26 = (f32[1,16,32,128]{3,2,1,0:T(8,128)S(1)}, f32[1,16,32,128]{3,2,1,0:T(8,128)S(1)}, u32[]{:S(2)}, u32[]{:S(2)}) collective-permute-start(f32[1,16,32,128]{3,2,1,0:T(8,128)S(1)} %subtract_bitcast_fusion), channel_id=1, source_target_pairs={{0,32},{32,64},{64,96},{96,128},{128,160},{160,192},{192,224},{1,3... | collective-permute-start | bytes 786440 | tf_op jit(solution)/shard_map/ppermute | solution.py:37
  520.2 13.6 %collective-permute-start.27 = (f32[2,16,32,128]{3,2,1,0:T(8,128)S(1)}, f32[2,16,32,128]{3,2,1,0:T(8,128)S(1)}, u32[]{:S(2)}, u32[]{:S(2)}) collective-permute-start(f32[2,16,32,128]{3,2,1,0:T(8,128)S(1)} %pad_maximum_fusion.5), channel_id=1, source_target_pairs={{0,64},{32,96},{64,128},{96,160},{128,192},{160,224},{1,65},{33,97... | collective-permute-start | bytes 1572872 | tf_op jit(solution)/shard_map/ppermute | solution.py:37
  535.0 25.8 %collective-permute-start.28 = (f32[4,16,32,128]{3,2,1,0:T(8,128)}, f32[4,16,32,128]{3,2,1,0:T(8,128)}, u32[]{:S(2)}, u32[]{:S(2)}) collective-permute-start(f32[4,16,32,128]{3,2,1,0:T(8,128)} %pad_maximum_fusion.3), channel_id=1, source_target_pairs={{0,128},{32,160},{64,192},{96,224},{1,129},{33,161},{65,193},{97,2... | collective-permute-start | bytes 3145736 | tf_op jit(solution)/shard_map/ppermute | solution.py:37
  (99 other events, 1316.9 us)

commit v11 on v9

--- a/solution.py
+++ b/solution.py
@@ -384,10 +384,14 @@
         packed = jnp.broadcast_to(corrections[None], (slices,) + corrections.shape)
         every = lax.all_to_all(packed, "tm", 0, 0, tiled=True)
 
-        def corrected_step(turn_no, coarse_state):
-            return coarse_step(coarse_state) + every[turn_no]
-
-        coarse_state = lax.fori_loop(0, slice_index, corrected_step, start_coarse)
+        def correction_before(turn_no):
+            return jnp.where(turn_no > 0, every[jnp.maximum(turn_no - 1, 0)], 0.0)
+
+        def corrected_step(turn_no, coarse_image):
+            return coarse_step(coarse_image + correction_before(turn_no))
+
+        coarse_image = lax.fori_loop(0, slice_index, corrected_step, start_coarse)
+        coarse_state = coarse_image + correction_before(slice_index)
         return (coarse_state, coarse_step(coarse_state))
 
     coarse_state = lax.fori_loop(

time: 545 us -> 555 us (1.018)
  other arithmetic: 107 us -> 116 us
    sub x7 -> x19, other arithmetic: 15.5 us -> 39.9 us  [coarse_step(): return coarse_state - balance / slope_sum]
    add x12 -> x0, other arithmetic: 24.2 us -> none  [corrected_step(): return coarse_step(coarse_state) + every[turn_no]]
    div x22, other arithmetic: 19.3 us -> 26.1 us  [fractional(): water_mobility / mobility]
where the time goes in v11:
time: 555 us; the launch traced here: 549 us
  blocking collectives  156 us (28%)
  waiting for transfers between devices  123 us (22%)
  other arithmetic  116 us (21%)
  starting transfers between devices  98.9 us (18%)
  local copies, waits for them, and re-layouts  27.8 us (5%)
  between operations  21.8 us (4%)
  matrix products  5.93 us (1%)
    all_to_all x6, blocking collectives, global_sums(): gathered = lax.all_to_all(packed, ('sx', 'sy'), 0, 0, tiled=True)  124 us
    all_to_all x2, waiting for transfers between devices, chain(): every = lax.all_to_all(packed, 'tm', 0, 0, tiled=True)  48.2 us
    ppermute x11, starting transfers between devices, row_halo(): before = lax.ppermute(volume[-1:], ROW_AXES, up)  47.3 us
    sub x19, other arithmetic, coarse_step(): return coarse_state - balance / slope_sum  39.9 us
    all_to_all x1, waiting for transfers between devices, gather_grid(): gathered = lax.all_to_all(packed, ('sx', 'sy'), 0, 0, tiled=True)  30 us
    div x22, other arithmetic, fractional(): water_mobility / mobility  26.1 us
    all_to_all x1, blocking collectives, restrict_rows(): gathered = lax.all_to_all(packed, ROW_AXES, 0, 0, tiled=True)  22.7 us
    ppermute x11, starting transfers between devices, row_halo(): after = lax.ppermute(volume[:1], ROW_AXES, down)  14.2 us
  transfers between devices with their start and end apart: 28, of which 25 were waited for; matrix products, arithmetic and copies ran while one was open for 6% of the time, Pallas kernels for 0%

profile of v11, /device:TPU:6, one launch (start us, length us, event | category | flops | bytes accessed | tf_op | source)
XLA Modules:
  0.0 549.0 jit_solution(9725131640454300476)
XLA Ops:
  17.1 4.5 all-to-all-start.1
  22.0 7.6 %all-to-all-done.1 = f32[4,6,1,16,256]{4,3,1,2,0:T(8,128)S(1)} async-done(((f32[4,6,1,16,256]{4,3,1,2,0:T(8,128)}), f32[4,6,1,16,256]{4,3,1,2,0:T(8,128)S(1)}, u32[]{:S(2)}, u32[]{:S(2)}) %all-to-all-start.1) | async-done | bytes 393248 | tf_op jit(solution)/shard_map/all_to_all | solution.py:296
  31.0 9.5 %all-to-all-start = ((f32[32,6,2,8,128]{4,3,2,1,0:T(8,128)}), f32[32,6,2,8,128]{4,3,2,1,0:T(8,128)S(1)}, u32[]{:S(2)}, u32[]{:S(2)}) async-start(f32[32,6,2,8,128]{4,3,2,1,0:T(8,128)} %broadcast_in_dim.171), calls=%async_computation | async-start | bytes 3145728 | tf_op jit(solution)/shard_map/all_to_all | solution.py:279
  42.5 4.4 collective-permute-start
  48.2 30.0 %all-to-all-done = f32[32,6,2,8,128]{4,3,2,1,0:T(8,128)S(1)} async-done(((f32[32,6,2,8,128]{4,3,2,1,0:T(8,128)}), f32[32,6,2,8,128]{4,3,2,1,0:T(8,128)S(1)}, u32[]{:S(2)}, u32[]{:S(2)}) %all-to-all-start) | async-done | bytes 1572896 | tf_op jit(solution)/shard_map/all_to_all | solution.py:279
  81.8 20.1 %while.37 = (s32[]{:T(128)}, f32[16,32,128]{2,1,0:T(8,128)}, s32[]{:T(128)}, f32[16,32,128]{2,1,0:T(8,128)S(1)}, f32[16,32,128]{2,1,0:T(8,128)S(1)}, /*index=5*/...) while((s32[]{:T(128)}, f32[16,32,128]{2,1,0:T(8,128)}, ...), condition=%wide.region_2.3_spmd, body=%wide.region_1.2_spmd.sunk | while | flops 4784130 | bytes 4980885 | solution.py:397
  115.7 5.3 collective-permute-start.5
  125.7 24.1 %all_to_all.71 = f32[32,1,2]{2,1,0:T(1,128)S(1)} all-to-all(f32[32,1,2]{2,1,0:T(1,128)S(1)} %broadcast_in_dim.176), channel_id=1, replica_groups=mesh['tm'=8,'sx'=8,'sy'=4] {'sx','sy'}, dimensions={0} | all-to-all | bytes 512 | tf_op jit(solution)/shard_map/all_to_all | solution.py:191
  155.2 4.5 collective-permute-start.7
  165.6 18.9 %all_to_all.72 = f32[32,1,2]{2,1,0:T(1,128)S(1)} all-to-all(f32[32,1,2]{2,1,0:T(1,128)S(1)} %broadcast_in_dim.177), channel_id=1, replica_groups=mesh['tm'=8,'sx'=8,'sy'=4] {'sx','sy'}, dimensions={0} | all-to-all | bytes 512 | tf_op jit(solution)/shard_map/all_to_all | solution.py:191
  193.1 4.5 collective-permute-start.9
  202.7 18.9 %all_to_all.73 = f32[32,1,2]{2,1,0:T(1,128)S(1)} all-to-all(f32[32,1,2]{2,1,0:T(1,128)S(1)} %broadcast_in_dim.178), channel_id=1, replica_groups=mesh['tm'=8,'sx'=8,'sy'=4] {'sx','sy'}, dimensions={0} | all-to-all | bytes 512 | tf_op jit(solution)/shard_map/all_to_all | solution.py:191
  231.5 4.5 collective-permute-start.11
  240.4 9.4 %all-to-all-start.5 = ((f32[32,1,32,128]{3,2,1,0:T(8,128)}), f32[32,1,32,128]{3,2,1,0:T(8,128)}, u32[]{:S(2)}, u32[]{:S(2)}) async-start(f32[32,1,32,128]{3,2,1,0:T(8,128)} %broadcast_in_dim.182), calls=%async_computation.5 | async-start | bytes 1048576 | tf_op jit(solution)/shard_map/all_to_all | solution.py:318
  251.6 12.0 %all-to-all-done.5 = f32[32,1,32,128]{3,2,1,0:T(8,128)} async-done(((f32[32,1,32,128]{3,2,1,0:T(8,128)}), f32[32,1,32,128]{3,2,1,0:T(8,128)}, u32[]{:S(2)}, u32[]{:S(2)}) %all-to-all-start.5) | async-done | bytes 524320 | tf_op jit(solution)/shard_map/all_to_all | solution.py:318
  270.0 4.5 all-to-all-start.6
  276.7 23.0 %all-to-all-done.6 = f32[8,16,32,128]{3,2,1,0:T(8,128)} async-done(((f32[8,16,32,128]{3,2,1,0:T(8,128)}), f32[8,16,32,128]{3,2,1,0:T(8,128)}, u32[]{:S(2)}, u32[]{:S(2)}) %all-to-all-start.6) | async-done | bytes 2097184 | tf_op jit(solution)/shard_map/all_to_all | solution.py:385
  299.7 21.4 %while.38 = (s32[]{:T(128)}, f32[16,32,128]{2,1,0:T(8,128)}, s32[]{:T(128)}, f32[8,16,32,128]{3,2,1,0:T(8,128)}, f32[16,32,128]{2,1,0:T(8,128)S(1)}, /*index=5*/...) while((s32[]{:T(128)}, f32[16,32,128]{2,1,0:T(8,128)}, ...), condition=%wide.region_14.16_spmd, body=%wide.region_13.15_spmd.sunk | while | flops 5046277 | bytes 5505240 | solution.py:393
  324.9 5.0 collective-permute-start.12
  335.3 4.3 collective-permute-done.14
  341.8 4.5 collective-permute-start.16
  351.1 24.5 %all_to_all.74 = f32[32,1,2]{2,1,0:T(1,128)S(1)} all-to-all(f32[32,1,2]{2,1,0:T(1,128)S(1)} %broadcast_in_dim.184), channel_id=1, replica_groups=mesh['tm'=8,'sx'=8,'sy'=4] {'sx','sy'}, dimensions={0} | all-to-all | bytes 512 | tf_op jit(solution)/shard_map/all_to_all | solution.py:191
  381.0 4.5 collective-permute-start.18
  391.4 18.9 %all_to_all.75 = f32[32,1,2]{2,1,0:T(1,128)S(1)} all-to-all(f32[32,1,2]{2,1,0:T(1,128)S(1)} %broadcast_in_dim.185), channel_id=1, replica_groups=mesh['tm'=8,'sx'=8,'sy'=4] {'sx','sy'}, dimensions={0} | all-to-all | bytes 512 | tf_op jit(solution)/shard_map/all_to_all | solution.py:191
  418.8 4.5 collective-permute-start.20
  428.4 18.9 %all_to_all.76 = f32[32,1,2]{2,1,0:T(1,128)S(1)} all-to-all(f32[32,1,2]{2,1,0:T(1,128)S(1)} %broadcast_in_dim.186), channel_id=1, replica_groups=mesh['tm'=8,'sx'=8,'sy'=4] {'sx','sy'}, dimensions={0} | all-to-all | bytes 512 | tf_op jit(solution)/shard_map/all_to_all | solution.py:191
  458.0 4.5 collective-permute-start.22
  465.7 22.7 %all_to_all.77 = f32[32,1,32,128]{3,2,1,0:T(8,128)S(1)} all-to-all(f32[32,1,32,128]{3,2,1,0:T(8,128)S(1)} %broadcast_in_dim.188), channel_id=1, replica_groups=mesh['tm'=8,'sx'=8,'sy'=4] {'sx','sy'}, dimensions={0} | all-to-all | bytes 1048576 | tf_op jit(solution)/shard_map/all_to_all | solution.py:318
  490.1 4.5 all-to-all-start.11
  494.6 25.2 %all-to-all-done.11 = f32[8,16,32,128]{3,2,1,0:T(8,128)} async-done(((f32[8,16,32,128]{3,2,1,0:T(8,128)}), f32[8,16,32,128]{3,2,1,0:T(8,128)}, u32[]{:S(2)}, u32[]{:S(2)}) %all-to-all-start.11) | async-done | bytes 2097184 | tf_op jit(solution)/shard_map/all_to_all | solution.py:385
  519.8 16.4 %while.39 = (s32[]{:T(128)}, f32[16,32,128]{2,1,0:T(8,128)S(1)}, s32[]{:T(128)}, f32[8,16,32,128]{3,2,1,0:T(8,128)}, f32[16,32,128]{2,1,0:T(8,128)S(1)}, /*index...) while((s32[]{:T(128)}, f32[16,32,128]{2,1,0:T(8,128)S(1)}, ...), condition=%wide.region_26.28_spmd, body=%wide.region_25.27_spmd.sunk | while | flops 5046277 | bytes 5505240 | solution.py:393
  539.2 9.1 %all_to_all.78 = f32[4,2,1,16,256]{4,3,2,1,0:T(8,128)S(1)} all-to-all(f32[4,2,1,16,256]{4,3,2,1,0:T(8,128)S(1)} %maximum_bitcast_fusion.2), channel_id=1, replica_groups=mesh['tm'=8,'sx'=8,'sy'=4] {'sy'}, dimensions={0} | all-to-all | bytes 262144 | tf_op jit(solution)/shard_map/all_to_all | solution.py:305
  (384 shorter events, 190.2 us)
Async XLA Ops:
  0.7 101.2 %copy-start.79 = (s32[256]{0:T(256)}, s32[256]{0:T(256)S(1)}, u32[]{:S(2)}) copy-start(s32[256]{0:T(256)S(1)} %get-tuple-element.797) | copy-start | bytes 3076
  17.1 12.5 %all-to-all-start.1 = ((f32[4,6,1,16,256]{4,3,1,2,0:T(8,128)}), f32[4,6,1,16,256]{4,3,1,2,0:T(8,128)S(1)}, u32[]{:S(2)}, u32[]{:S(2)}) async-start(f32[4,6,1,16,256]{4,3,1,2,0:T(8,128)} %bitcast.35), calls=%async_computation.1 | async-start | bytes 786432 | tf_op jit(solution)/shard_map/all_to_all | solution.py:296
  31.0 47.1 %all-to-all-start = ((f32[32,6,2,8,128]{4,3,2,1,0:T(8,128)}), f32[32,6,2,8,128]{4,3,2,1,0:T(8,128)S(1)}, u32[]{:S(2)}, u32[]{:S(2)}) async-start(f32[32,6,2,8,128]{4,3,2,1,0:T(8,128)} %broadcast_in_dim.171), calls=%async_computation | async-start | bytes 3145728 | tf_op jit(solution)/shard_map/all_to_all | solution.py:279
  40.5 62.3 %copy-start.70 = (pred[64]{0:T(512)(128)(4,1)}, pred[64]{0:T(512)(128)(4,1)S(1)}, u32[]{:S(2)}) copy-start(pred[64]{0:T(512)(128)(4,1)S(1)} %compare_and_fusion.1) | copy-start | bytes 196
  41.1 61.7 %copy-start.73 = (s32[64]{0:T(128)}, s32[64]{0:T(128)S(1)}, u32[]{:S(2)}) copy-start(s32[64]{0:T(128)S(1)} %get-tuple-element.801) | copy-start | bytes 772
  41.1 61.7 %copy-start.76 = (s32[64]{0:T(128)}, s32[64]{0:T(128)S(1)}, u32[]{:S(2)}) copy-start(s32[64]{0:T(128)S(1)} %get-tuple-element.802) | copy-start | bytes 772
  42.5 65.3 %collective-permute-start = (f32[1,3,64,256]{3,2,0,1:T(8,128)}, f32[1,3,64,256]{3,2,0,1:T(8,128)}, u32[]{:S(2)}, u32[]{:S(2)}) collective-permute-start(f32[1,3,64,256]{3,2,0,1:T(8,128)} %maximum_bitcast_fusion.1), channel_id=1, source_target_pairs={{0,1},{1,2},{2,3},{3,4},{4,5},{5,6},{6,7},{7,8},{8,9},{9,10},{10,1... | collective-permute-start | bytes 589832 | tf_op jit(solution)/shard_map/ppermute | solution.py:122
  46.9 60.9 %collective-permute-start.1 = (f32[1,3,64,256]{3,2,0,1:T(8,128)}, f32[1,3,64,256]{3,2,0,1:T(8,128)}, u32[]{:S(2)}, u32[]{:S(2)}) collective-permute-start(f32[1,3,64,256]{3,2,0,1:T(8,128)} %maximum_bitcast_fusion.1), channel_id=1, source_target_pairs={{1,0},{2,1},{3,2},{4,3},{5,4},{6,5},{7,6},{8,7},{9,8},{10,9},{11,1... | collective-permute-start | bytes 589832 | tf_op jit(solution)/shard_map/ppermute | solution.py:123
  103.1 5.9 %collective-permute-start.2 = (f32[1,64,256]{2,1,0:T(8,128)S(1)}, f32[1,64,256]{2,1,0:T(8,128)S(1)}, u32[]{:S(2)}, u32[]{:S(2)}) collective-permute-start(f32[1,64,256]{2,1,0:T(8,128)S(1)} %fusion.69), channel_id=1, source_target_pairs={{0,1},{1,2},{2,3},{3,4},{4,5},{5,6},{6,7},{7,8},{8,9},{9,10},{10,1... | collective-permute-start | bytes 196616 | tf_op jit(solution)/shard_map/ppermute | solution.py:122
  106.5 6.2 %collective-permute-start.3 = (f32[1,64,256]{2,1,0:T(8,128)S(1)}, f32[1,64,256]{2,1,0:T(8,128)S(1)}, u32[]{:S(2)}, u32[]{:S(2)}) collective-permute-start(f32[1,64,256]{2,1,0:T(8,128)S(1)} %fusion.69), channel_id=1, source_target_pairs={{1,0},{2,1},{3,2},{4,3},{5,4},{6,5},{7,6},{8,7},{9,8},{10,9},{11,1... | collective-permute-start | bytes 196616 | tf_op jit(solution)/shard_map/ppermute | solution.py:123
  114.4 6.9 %collective-permute-start.4 = (f32[1,64,256]{2,1,0:T(8,128)S(1)}, f32[1,64,256]{2,1,0:T(8,128)S(1)}, u32[]{:S(2)}, u32[]{:S(2)}) collective-permute-start(f32[1,64,256]{2,1,0:T(8,128)S(1)} %get-tuple-element.727), channel_id=1, source_target_pairs={{1,0},{2,1},{3,2},{4,3},{5,4},{6,5},{7,6},{8,7},{9,8},{10,9},{11,1... | collective-permute-start | bytes 196616 | tf_op jit(solution)/shard_map/ppermute | solution.py:123
  115.7 7.1 %collective-permute-start.5 = (f32[1,64,256]{2,1,0:T(8,128)S(1)}, f32[1,64,256]{2,1,0:T(8,128)S(1)}, u32[]{:S(2)}, u32[]{:S(2)}) collective-permute-start(f32[1,64,256]{2,1,0:T(8,128)S(1)} %get-tuple-element.727), channel_id=1, source_target_pairs={{0,1},{1,2},{2,3},{3,4},{4,5},{5,6},{6,7},{7,8},{8,9},{9,10},{10,1... | collective-permute-start | bytes 196616 | tf_op jit(solution)/shard_map/ppermute | solution.py:122
  153.9 6.2 %collective-permute-start.6 = (f32[1,64,256]{2,1,0:T(8,128)S(1)}, f32[1,64,256]{2,1,0:T(8,128)S(1)}, u32[]{:S(2)}, u32[]{:S(2)}) collective-permute-start(f32[1,64,256]{2,1,0:T(8,128)S(1)} %fusion.403), channel_id=1, source_target_pairs={{1,0},{2,1},{3,2},{4,3},{5,4},{6,5},{7,6},{8,7},{9,8},{10,9},{11,1... | collective-permute-start | bytes 196616 | tf_op jit(solution)/shard_map/ppermute | solution.py:123
  155.2 6.4 %collective-permute-start.7 = (f32[1,64,256]{2,1,0:T(8,128)S(1)}, f32[1,64,256]{2,1,0:T(8,128)S(1)}, u32[]{:S(2)}, u32[]{:S(2)}) collective-permute-start(f32[1,64,256]{2,1,0:T(8,128)S(1)} %fusion.403), channel_id=1, source_target_pairs={{0,1},{1,2},{2,3},{3,4},{4,5},{5,6},{6,7},{7,8},{8,9},{9,10},{10,1... | collective-permute-start | bytes 196616 | tf_op jit(solution)/shard_map/ppermute | solution.py:122
  191.8 6.2 %collective-permute-start.8 = (f32[1,64,256]{2,1,0:T(8,128)S(1)}, f32[1,64,256]{2,1,0:T(8,128)S(1)}, u32[]{:S(2)}, u32[]{:S(2)}) collective-permute-start(f32[1,64,256]{2,1,0:T(8,128)S(1)} %get-tuple-element.723), channel_id=1, source_target_pairs={{1,0},{2,1},{3,2},{4,3},{5,4},{6,5},{7,6},{8,7},{9,8},{10,9},{11,1... | collective-permute-start | bytes 196616 | tf_op jit(solution)/shard_map/ppermute | solution.py:123
  193.1 6.4 %collective-permute-start.9 = (f32[1,64,256]{2,1,0:T(8,128)S(1)}, f32[1,64,256]{2,1,0:T(8,128)S(1)}, u32[]{:S(2)}, u32[]{:S(2)}) collective-permute-start(f32[1,64,256]{2,1,0:T(8,128)S(1)} %get-tuple-element.723), channel_id=1, source_target_pairs={{0,1},{1,2},{2,3},{3,4},{4,5},{5,6},{6,7},{7,8},{8,9},{9,10},{10,1... | collective-permute-start | bytes 196616 | tf_op jit(solution)/shard_map/ppermute | solution.py:122
  230.2 6.2 %collective-permute-start.10 = (f32[1,64,256]{2,1,0:T(8,128)S(1)}, f32[1,64,256]{2,1,0:T(8,128)S(1)}, u32[]{:S(2)}, u32[]{:S(2)}) collective-permute-start(f32[1,64,256]{2,1,0:T(8,128)S(1)} %get-tuple-element.721), channel_id=1, source_target_pairs={{1,0},{2,1},{3,2},{4,3},{5,4},{6,5},{7,6},{8,7},{9,8},{10,9},{11,1... | collective-permute-start | bytes 196616 | tf_op jit(solution)/shard_map/ppermute | solution.py:123
  231.5 6.4 %collective-permute-start.11 = (f32[1,64,256]{2,1,0:T(8,128)S(1)}, f32[1,64,256]{2,1,0:T(8,128)S(1)}, u32[]{:S(2)}, u32[]{:S(2)}) collective-permute-start(f32[1,64,256]{2,1,0:T(8,128)S(1)} %get-tuple-element.721), channel_id=1, source_target_pairs={{0,1},{1,2},{2,3},{3,4},{4,5},{5,6},{6,7},{7,8},{8,9},{9,10},{10,1... | collective-permute-start | bytes 196616 | tf_op jit(solution)/shard_map/ppermute | solution.py:122
  240.4 23.3 %all-to-all-start.5 = ((f32[32,1,32,128]{3,2,1,0:T(8,128)}), f32[32,1,32,128]{3,2,1,0:T(8,128)}, u32[]{:S(2)}, u32[]{:S(2)}) async-start(f32[32,1,32,128]{3,2,1,0:T(8,128)} %broadcast_in_dim.182), calls=%async_computation.5 | async-start | bytes 1048576 | tf_op jit(solution)/shard_map/all_to_all | solution.py:318
  270.0 29.7 %all-to-all-start.6 = ((f32[8,16,32,128]{3,2,1,0:T(8,128)}), f32[8,16,32,128]{3,2,1,0:T(8,128)}, u32[]{:S(2)}, u32[]{:S(2)}) async-start(f32[8,16,32,128]{3,2,1,0:T(8,128)} %broadcast_in_dim.183), calls=%async_computation.6 | async-start | bytes 4194304 | tf_op jit(solution)/shard_map/all_to_all | solution.py:385
  324.9 5.9 %collective-permute-start.12 = (f32[1,64,256]{2,1,0:T(8,128)S(1)}, f32[1,64,256]{2,1,0:T(8,128)S(1)}, u32[]{:S(2)}, u32[]{:S(2)}) collective-permute-start(f32[1,64,256]{2,1,0:T(8,128)S(1)} %fusion.68), channel_id=1, source_target_pairs={{0,32},{32,64},{64,96},{96,128},{128,160},{160,192},{192,224},{1,3... | collective-permute-start | bytes 196616 | tf_op jit(solution)/shard_map/ppermute | solution.py:37
  330.9 4.4 collective-permute-start.13
  333.4 6.2 %collective-permute-start.14 = (f32[1,64,256]{2,1,0:T(8,128)S(1)}, f32[1,64,256]{2,1,0:T(8,128)S(1)}, u32[]{:S(2)}, u32[]{:S(2)}) collective-permute-start(f32[1,64,256]{2,1,0:T(8,128)S(1)} %broadcast_select_fusion), channel_id=1, source_target_pairs={{1,0},{2,1},{3,2},{4,3},{5,4},{6,5},{7,6},{8,7},{9,8},{10,9},{11,1... | collective-permute-start | bytes 196616 | tf_op jit(solution)/shard_map/ppermute | solution.py:123
  340.5 6.2 %collective-permute-start.15 = (f32[1,64,256]{2,1,0:T(8,128)S(1)}, f32[1,64,256]{2,1,0:T(8,128)S(1)}, u32[]{:S(2)}, u32[]{:S(2)}) collective-permute-start(f32[1,64,256]{2,1,0:T(8,128)S(1)} %get-tuple-element.711), channel_id=1, source_target_pairs={{1,0},{2,1},{3,2},{4,3},{5,4},{6,5},{7,6},{8,7},{9,8},{10,9},{11,1... | collective-permute-start | bytes 196616 | tf_op jit(solution)/shard_map/ppermute | solution.py:123
  341.8 6.4 %collective-permute-start.16 = (f32[1,64,256]{2,1,0:T(8,128)S(1)}, f32[1,64,256]{2,1,0:T(8,128)S(1)}, u32[]{:S(2)}, u32[]{:S(2)}) collective-permute-start(f32[1,64,256]{2,1,0:T(8,128)S(1)} %get-tuple-element.711), channel_id=1, source_target_pairs={{0,1},{1,2},{2,3},{3,4},{4,5},{5,6},{6,7},{7,8},{8,9},{9,10},{10,1... | collective-permute-start | bytes 196616 | tf_op jit(solution)/shard_map/ppermute | solution.py:122
  379.7 6.2 %collective-permute-start.17 = (f32[1,64,256]{2,1,0:T(8,128)S(1)}, f32[1,64,256]{2,1,0:T(8,128)S(1)}, u32[]{:S(2)}, u32[]{:S(2)}) collective-permute-start(f32[1,64,256]{2,1,0:T(8,128)S(1)} %fusion.404), channel_id=1, source_target_pairs={{1,0},{2,1},{3,2},{4,3},{5,4},{6,5},{7,6},{8,7},{9,8},{10,9},{11,1... | collective-permute-start | bytes 196616 | tf_op jit(solution)/shard_map/ppermute | solution.py:123
  381.0 6.4 %collective-permute-start.18 = (f32[1,64,256]{2,1,0:T(8,128)S(1)}, f32[1,64,256]{2,1,0:T(8,128)S(1)}, u32[]{:S(2)}, u32[]{:S(2)}) collective-permute-start(f32[1,64,256]{2,1,0:T(8,128)S(1)} %fusion.404), channel_id=1, source_target_pairs={{0,1},{1,2},{2,3},{3,4},{4,5},{5,6},{6,7},{7,8},{8,9},{9,10},{10,1... | collective-permute-start | bytes 196616 | tf_op jit(solution)/shard_map/ppermute | solution.py:122
  417.5 6.2 %collective-permute-start.19 = (f32[1,64,256]{2,1,0:T(8,128)S(1)}, f32[1,64,256]{2,1,0:T(8,128)S(1)}, u32[]{:S(2)}, u32[]{:S(2)}) collective-permute-start(f32[1,64,256]{2,1,0:T(8,128)S(1)} %get-tuple-element.707), channel_id=1, source_target_pairs={{1,0},{2,1},{3,2},{4,3},{5,4},{6,5},{7,6},{8,7},{9,8},{10,9},{11,1... | collective-permute-start | bytes 196616 | tf_op jit(solution)/shard_map/ppermute | solution.py:123
  418.8 6.4 %collective-permute-start.20 = (f32[1,64,256]{2,1,0:T(8,128)S(1)}, f32[1,64,256]{2,1,0:T(8,128)S(1)}, u32[]{:S(2)}, u32[]{:S(2)}) collective-permute-start(f32[1,64,256]{2,1,0:T(8,128)S(1)} %get-tuple-element.707), channel_id=1, source_target_pairs={{0,1},{1,2},{2,3},{3,4},{4,5},{5,6},{6,7},{7,8},{8,9},{9,10},{10,1... | collective-permute-start | bytes 196616 | tf_op jit(solution)/shard_map/ppermute | solution.py:122
  456.7 6.1 %collective-permute-start.21 = (f32[1,64,256]{2,1,0:T(8,128)S(1)}, f32[1,64,256]{2,1,0:T(8,128)S(1)}, u32[]{:S(2)}, u32[]{:S(2)}) collective-permute-start(f32[1,64,256]{2,1,0:T(8,128)S(1)} %get-tuple-element.705), channel_id=1, source_target_pairs={{1,0},{2,1},{3,2},{4,3},{5,4},{6,5},{7,6},{8,7},{9,8},{10,9},{11,1... | collective-permute-start | bytes 196616 | tf_op jit(solution)/shard_map/ppermute | solution.py:123
  458.0 6.7 %collective-permute-start.22 = (f32[1,64,256]{2,1,0:T(8,128)S(1)}, f32[1,64,256]{2,1,0:T(8,128)S(1)}, u32[]{:S(2)}, u32[]{:S(2)}) collective-permute-start(f32[1,64,256]{2,1,0:T(8,128)S(1)} %get-tuple-element.705), channel_id=1, source_target_pairs={{0,1},{1,2},{2,3},{3,4},{4,5},{5,6},{6,7},{7,8},{8,9},{9,10},{10,1... | collective-permute-start | bytes 196616 | tf_op jit(solution)/shard_map/ppermute | solution.py:122
  490.1 29.7 %all-to-all-start.11 = ((f32[8,16,32,128]{3,2,1,0:T(8,128)}), f32[8,16,32,128]{3,2,1,0:T(8,128)}, u32[]{:S(2)}, u32[]{:S(2)}) async-start(f32[8,16,32,128]{3,2,1,0:T(8,128)} %broadcast_in_dim.189), calls=%async_computation.11 | async-start | bytes 4194304 | tf_op jit(solution)/shard_map/all_to_all | solution.py:385
  (89 other events, 916.2 us)

commit v12 on v9

--- a/solution.py
+++ b/solution.py
@@ -337,12 +337,18 @@
     water_block = lookup(rock_type, water_endpoint)
     oil_block = lookup(rock_type, oil_endpoint)
     restricted = restrict_blocks(jnp.stack([initial_saturation, permeability, porosity, source_rate]))
-    whole = gather_grid(jnp.concatenate([restricted, jnp.stack([water_block, oil_block])]))
-    start_coarse, permeability_upscaled, poro_coarse, source_coarse, water_coarse, oil_coarse = (
-        whole[k] for k in range(6)
-    )
-    water_mobility, oil_mobility = mobilities(start_coarse, water_coarse, oil_coarse)
-    transport_field_upscaled = permeability_upscaled * (water_mobility + oil_mobility)
+    water_mobility, oil_mobility = mobilities(restricted[0], water_block, oil_block)
+    transport_block = restricted[1] * (water_mobility + oil_mobility)
+    whole = gather_grid(
+        jnp.stack(
+            [restricted[0], transport_block, restricted[2], restricted[3], rock_type.astype(jnp.float32)]
+        )
+    )
+    start_coarse, transport_field_upscaled, poro_coarse, source_coarse, rock_coarse = (
+        whole[k] for k in range(5)
+    )
+    water_coarse = lookup(rock_coarse, water_endpoint)
+    oil_coarse = lookup(rock_coarse, oil_endpoint)
     transmissibility_upscaled = [
         (transport_field_upscaled + exceeding_part) / 8.0
         for exceeding_part in whole_faces(transport_field_upscaled)

time: 545 us -> 552 us (1.013)
  other arithmetic: 107 us -> 119 us
  transfers between devices with their start and end apart: 28 -> 28, of which waited for: 25 -> 25; matrix products, arithmetic and copies ran while one was open for 6% -> 7% of each run, Pallas kernels for 0% -> 0%
where the time goes in v12:
time: 552 us; the launch traced here: 548 us
  blocking collectives  157 us (28%)
  other arithmetic  119 us (22%)
  waiting for transfers between devices  118 us (21%)
  starting transfers between devices  98.4 us (18%)
  local copies, waits for them, and re-layouts  27.6 us (5%)
  between operations  22.1 us (4%)
  matrix products  5.93 us (1%)
    all_to_all x6, blocking collectives, global_sums(): gathered = lax.all_to_all(packed, ('sx', 'sy'), 0, 0, tiled=True)  124 us
    all_to_all x2, waiting for transfers between devices, chain(): every = lax.all_to_all(packed, 'tm', 0, 0, tiled=True)  48.2 us
    ppermute x11, starting transfers between devices, row_halo(): before = lax.ppermute(volume[-1:], ROW_AXES, up)  46.9 us
    all_to_all x1, waiting for transfers between devices, gather_grid(): gathered = lax.all_to_all(packed, ('sx', 'sy'), 0, 0, tiled=True)  24.8 us
    add x12, other arithmetic, corrected_step(): return coarse_step(coarse_state) + every[turn_no]  24.1 us
    all_to_all x1, blocking collectives, restrict_rows(): gathered = lax.all_to_all(packed, ROW_AXES, 0, 0, tiled=True)  22.7 us
    div x22, other arithmetic, fractional(): water_mobility / mobility  19.3 us
    sub x7, other arithmetic, coarse_step(): return coarse_state - balance / slope_sum  15.7 us
  transfers between devices with their start and end apart: 28, of which 25 were waited for; matrix products, arithmetic and copies ran while one was open for 7% of the time, Pallas kernels for 0%

profile of v12, /device:TPU:6, one launch (start us, length us, event | category | flops | bytes accessed | tf_op | source)
XLA Modules:
  0.0 547.7 jit_solution(906007918995456691)
XLA Ops:
  6.4 5.7 %fusion.431 = (f32[1,2,8,128]{3,2,1,0:T(8,128)S(1)}, pred[2,8,128]{2,1,0:T(8,128)(4,1)S(1)}, pred[2,8,128]{2,1,0:T(8,128)(4,1)S(1)}, pred[2,8,128]{2,1,0:T(8,128...) fusion(f32[8,8,128]{2,1,0:T(8,128)S(1)} %fusion.72, f32[]{:T(128)} %bitcast.20, f32[]{:T(128)} %bitcast.19, ...), kind=kLoop, calls=%fused_computation.681 | loop fusion | flops 53248 | bytes 49184 | tf_op jit(solution)/shard_map/stack | solution.py:343
  12.1 5.0 fusion.459
  23.3 4.5 all-to-all-start.1
  27.8 8.0 %all-to-all-done.1 = f32[4,6,1,16,256]{4,3,1,2,0:T(8,128)S(1)} async-done(((f32[4,6,1,16,256]{4,3,1,2,0:T(8,128)}), f32[4,6,1,16,256]{4,3,1,2,0:T(8,128)S(1)}, u32[]{:S(2)}, u32[]{:S(2)}) %all-to-all-start.1) | async-done | bytes 393248 | tf_op jit(solution)/shard_map/all_to_all | solution.py:296
  37.0 9.5 %all-to-all-start = ((f32[32,5,2,8,128]{4,3,2,1,0:T(8,128)}), f32[32,5,2,8,128]{4,3,2,1,0:T(8,128)S(1)}, u32[]{:S(2)}, u32[]{:S(2)}) async-start(f32[32,5,2,8,128]{4,3,2,1,0:T(8,128)} %broadcast_in_dim.185), calls=%async_computation | async-start | bytes 2621440 | tf_op jit(solution)/shard_map/all_to_all | solution.py:279
  54.1 24.8 %all-to-all-done = f32[32,5,2,8,128]{4,3,2,1,0:T(8,128)S(1)} async-done(((f32[32,5,2,8,128]{4,3,2,1,0:T(8,128)}), f32[32,5,2,8,128]{4,3,2,1,0:T(8,128)S(1)}, u32[]{:S(2)}, u32[]{:S(2)}) %all-to-all-start) | async-done | bytes 1310752 | tf_op jit(solution)/shard_map/all_to_all | solution.py:279
  87.6 20.3 %while.37 = (s32[]{:T(128)}, f32[16,32,128]{2,1,0:T(8,128)}, s32[]{:T(128)}, f32[16,32,128]{2,1,0:T(8,128)S(1)}, f32[16,32,128]{2,1,0:T(8,128)S(1)}, /*index=5*/...) while((s32[]{:T(128)}, f32[16,32,128]{2,1,0:T(8,128)}, ...), condition=%wide.region_2.3_spmd, body=%wide.region_1.2_spmd.sunk | while | flops 4784130 | bytes 4980885 | solution.py:399
  121.2 5.1 collective-permute-start.5
  131.1 24.3 %all_to_all.71 = f32[32,1,2]{2,1,0:T(1,128)S(1)} all-to-all(f32[32,1,2]{2,1,0:T(1,128)S(1)} %broadcast_in_dim.198), channel_id=1, replica_groups=mesh['tm'=8,'sx'=8,'sy'=4] {'sx','sy'}, dimensions={0} | all-to-all | bytes 512 | tf_op jit(solution)/shard_map/all_to_all | solution.py:191
  160.9 4.5 collective-permute-start.7
  171.3 18.9 %all_to_all.72 = f32[32,1,2]{2,1,0:T(1,128)S(1)} all-to-all(f32[32,1,2]{2,1,0:T(1,128)S(1)} %broadcast_in_dim.199), channel_id=1, replica_groups=mesh['tm'=8,'sx'=8,'sy'=4] {'sx','sy'}, dimensions={0} | all-to-all | bytes 512 | tf_op jit(solution)/shard_map/all_to_all | solution.py:191
  198.9 4.5 collective-permute-start.9
  208.6 18.9 %all_to_all.73 = f32[32,1,2]{2,1,0:T(1,128)S(1)} all-to-all(f32[32,1,2]{2,1,0:T(1,128)S(1)} %broadcast_in_dim.200), channel_id=1, replica_groups=mesh['tm'=8,'sx'=8,'sy'=4] {'sx','sy'}, dimensions={0} | all-to-all | bytes 512 | tf_op jit(solution)/shard_map/all_to_all | solution.py:191
  237.5 4.5 collective-permute-start.11
  246.4 9.4 %all-to-all-start.5 = ((f32[32,1,32,128]{3,2,1,0:T(8,128)}), f32[32,1,32,128]{3,2,1,0:T(8,128)}, u32[]{:S(2)}, u32[]{:S(2)}) async-start(f32[32,1,32,128]{3,2,1,0:T(8,128)} %broadcast_in_dim.204), calls=%async_computation.5 | async-start | bytes 1048576 | tf_op jit(solution)/shard_map/all_to_all | solution.py:318
  257.5 12.1 %all-to-all-done.5 = f32[32,1,32,128]{3,2,1,0:T(8,128)} async-done(((f32[32,1,32,128]{3,2,1,0:T(8,128)}), f32[32,1,32,128]{3,2,1,0:T(8,128)}, u32[]{:S(2)}, u32[]{:S(2)}) %all-to-all-start.5) | async-done | bytes 524320 | tf_op jit(solution)/shard_map/all_to_all | solution.py:318
  275.8 4.5 all-to-all-start.6
  282.5 23.0 %all-to-all-done.6 = f32[8,16,32,128]{3,2,1,0:T(8,128)} async-done(((f32[8,16,32,128]{3,2,1,0:T(8,128)}), f32[8,16,32,128]{3,2,1,0:T(8,128)}, u32[]{:S(2)}, u32[]{:S(2)}) %all-to-all-start.6) | async-done | bytes 2097184 | tf_op jit(solution)/shard_map/all_to_all | solution.py:391
  305.5 20.6 %while.38 = (s32[]{:T(128)}, f32[16,32,128]{2,1,0:T(8,128)}, s32[]{:T(128)}, f32[16,32,128]{2,1,0:T(8,128)S(1)}, f32[16,32,128]{2,1,0:T(8,128)S(1)}, /*index=5*/...) while((s32[]{:T(128)}, f32[16,32,128]{2,1,0:T(8,128)}, ...), condition=%wide.region_14.16_spmd, body=%wide.region_13.15_spmd.sunk | while | flops 4849669 | bytes 5243091 | solution.py:396
  329.6 4.9 collective-permute-start.12
  346.4 4.5 collective-permute-start.16
  355.8 24.5 %all_to_all.74 = f32[32,1,2]{2,1,0:T(1,128)S(1)} all-to-all(f32[32,1,2]{2,1,0:T(1,128)S(1)} %broadcast_in_dim.206), channel_id=1, replica_groups=mesh['tm'=8,'sx'=8,'sy'=4] {'sx','sy'}, dimensions={0} | all-to-all | bytes 512 | tf_op jit(solution)/shard_map/all_to_all | solution.py:191
  385.8 4.5 collective-permute-start.18
  396.1 18.9 %all_to_all.75 = f32[32,1,2]{2,1,0:T(1,128)S(1)} all-to-all(f32[32,1,2]{2,1,0:T(1,128)S(1)} %broadcast_in_dim.207), channel_id=1, replica_groups=mesh['tm'=8,'sx'=8,'sy'=4] {'sx','sy'}, dimensions={0} | all-to-all | bytes 512 | tf_op jit(solution)/shard_map/all_to_all | solution.py:191
  423.7 4.5 collective-permute-start.20
  433.4 18.9 %all_to_all.76 = f32[32,1,2]{2,1,0:T(1,128)S(1)} all-to-all(f32[32,1,2]{2,1,0:T(1,128)S(1)} %broadcast_in_dim.208), channel_id=1, replica_groups=mesh['tm'=8,'sx'=8,'sy'=4] {'sx','sy'}, dimensions={0} | all-to-all | bytes 512 | tf_op jit(solution)/shard_map/all_to_all | solution.py:191
  462.9 4.5 collective-permute-start.22
  470.6 22.7 %all_to_all.77 = f32[32,1,32,128]{3,2,1,0:T(8,128)S(1)} all-to-all(f32[32,1,32,128]{3,2,1,0:T(8,128)S(1)} %broadcast_in_dim.210), channel_id=1, replica_groups=mesh['tm'=8,'sx'=8,'sy'=4] {'sx','sy'}, dimensions={0} | all-to-all | bytes 1048576 | tf_op jit(solution)/shard_map/all_to_all | solution.py:318
  495.0 4.5 all-to-all-start.11
  499.5 25.2 %all-to-all-done.11 = f32[8,16,32,128]{3,2,1,0:T(8,128)} async-done(((f32[8,16,32,128]{3,2,1,0:T(8,128)}), f32[8,16,32,128]{3,2,1,0:T(8,128)}, u32[]{:S(2)}, u32[]{:S(2)}) %all-to-all-start.11) | async-done | bytes 2097184 | tf_op jit(solution)/shard_map/all_to_all | solution.py:391
  524.7 10.5 %while.39 = (s32[]{:T(128)}, f32[16,32,128]{2,1,0:T(8,128)S(1)}, s32[]{:T(128)}, f32[16,32,128]{2,1,0:T(8,128)S(1)}, f32[16,32,128]{2,1,0:T(8,128)S(1)}, /*index...) while((s32[]{:T(128)}, f32[16,32,128]{2,1,0:T(8,128)S(1)}, ...), condition=%wide.region_26.28_spmd, body=%wide.region_25.27_spmd.sunk | while | flops 4849669 | bytes 5243091 | solution.py:396
  537.2 9.8 %all_to_all.78 = f32[4,2,1,16,256]{4,3,2,1,0:T(8,128)S(1)} all-to-all(f32[4,2,1,16,256]{4,3,2,1,0:T(8,128)S(1)} %maximum_bitcast_fusion.2), channel_id=1, replica_groups=mesh['tm'=8,'sx'=8,'sy'=4] {'sy'}, dimensions={0} | all-to-all | bytes 262144 | tf_op jit(solution)/shard_map/all_to_all | solution.py:305
  (379 shorter events, 190.6 us)
Async XLA Ops:
  0.7 107.2 %copy-start.76 = (s32[256]{0:T(256)}, s32[256]{0:T(256)S(1)}, u32[]{:S(2)}) copy-start(s32[256]{0:T(256)S(1)} %get-tuple-element.800) | copy-start | bytes 3076
  23.3 12.5 %all-to-all-start.1 = ((f32[4,6,1,16,256]{4,3,1,2,0:T(8,128)}), f32[4,6,1,16,256]{4,3,1,2,0:T(8,128)S(1)}, u32[]{:S(2)}, u32[]{:S(2)}) async-start(f32[4,6,1,16,256]{4,3,1,2,0:T(8,128)} %bitcast.44), calls=%async_computation.1 | async-start | bytes 786432 | tf_op jit(solution)/shard_map/all_to_all | solution.py:296
  37.0 41.9 %all-to-all-start = ((f32[32,5,2,8,128]{4,3,2,1,0:T(8,128)}), f32[32,5,2,8,128]{4,3,2,1,0:T(8,128)S(1)}, u32[]{:S(2)}, u32[]{:S(2)}) async-start(f32[32,5,2,8,128]{4,3,2,1,0:T(8,128)} %broadcast_in_dim.185), calls=%async_computation | async-start | bytes 2621440 | tf_op jit(solution)/shard_map/all_to_all | solution.py:279
  46.5 62.2 %copy-start.67 = (pred[64]{0:T(512)(128)(4,1)}, pred[64]{0:T(512)(128)(4,1)S(1)}, u32[]{:S(2)}) copy-start(pred[64]{0:T(512)(128)(4,1)S(1)} %compare_and_fusion.1) | copy-start | bytes 196
  47.1 61.7 %copy-start.70 = (s32[64]{0:T(128)}, s32[64]{0:T(128)S(1)}, u32[]{:S(2)}) copy-start(s32[64]{0:T(128)S(1)} %get-tuple-element.804) | copy-start | bytes 772
  47.1 61.7 %copy-start.73 = (s32[64]{0:T(128)}, s32[64]{0:T(128)S(1)}, u32[]{:S(2)}) copy-start(s32[64]{0:T(128)S(1)} %get-tuple-element.805) | copy-start | bytes 772
  48.5 65.0 %collective-permute-start = (f32[1,3,64,256]{3,2,0,1:T(8,128)}, f32[1,3,64,256]{3,2,0,1:T(8,128)}, u32[]{:S(2)}, u32[]{:S(2)}) collective-permute-start(f32[1,3,64,256]{3,2,0,1:T(8,128)} %maximum_bitcast_fusion.1), channel_id=1, source_target_pairs={{0,1},{1,2},{2,3},{3,4},{4,5},{5,6},{6,7},{7,8},{8,9},{9,10},{10,1... | collective-permute-start | bytes 589832 | tf_op jit(solution)/shard_map/ppermute | solution.py:122
  52.8 60.6 %collective-permute-start.1 = (f32[1,3,64,256]{3,2,0,1:T(8,128)}, f32[1,3,64,256]{3,2,0,1:T(8,128)}, u32[]{:S(2)}, u32[]{:S(2)}) collective-permute-start(f32[1,3,64,256]{3,2,0,1:T(8,128)} %maximum_bitcast_fusion.1), channel_id=1, source_target_pairs={{1,0},{2,1},{3,2},{4,3},{5,4},{6,5},{7,6},{8,7},{9,8},{10,9},{11,1... | collective-permute-start | bytes 589832 | tf_op jit(solution)/shard_map/ppermute | solution.py:123
  109.0 5.6 %collective-permute-start.2 = (f32[1,64,256]{2,1,0:T(8,128)S(1)}, f32[1,64,256]{2,1,0:T(8,128)S(1)}, u32[]{:S(2)}, u32[]{:S(2)}) collective-permute-start(f32[1,64,256]{2,1,0:T(8,128)S(1)} %fusion.71), channel_id=1, source_target_pairs={{0,1},{1,2},{2,3},{3,4},{4,5},{5,6},{6,7},{7,8},{8,9},{9,10},{10,1... | collective-permute-start | bytes 196616 | tf_op jit(solution)/shard_map/ppermute | solution.py:122
  112.1 6.2 %collective-permute-start.3 = (f32[1,64,256]{2,1,0:T(8,128)S(1)}, f32[1,64,256]{2,1,0:T(8,128)S(1)}, u32[]{:S(2)}, u32[]{:S(2)}) collective-permute-start(f32[1,64,256]{2,1,0:T(8,128)S(1)} %fusion.71), channel_id=1, source_target_pairs={{1,0},{2,1},{3,2},{4,3},{5,4},{6,5},{7,6},{8,7},{9,8},{10,9},{11,1... | collective-permute-start | bytes 196616 | tf_op jit(solution)/shard_map/ppermute | solution.py:123
  119.9 6.7 %collective-permute-start.4 = (f32[1,64,256]{2,1,0:T(8,128)S(1)}, f32[1,64,256]{2,1,0:T(8,128)S(1)}, u32[]{:S(2)}, u32[]{:S(2)}) collective-permute-start(f32[1,64,256]{2,1,0:T(8,128)S(1)} %get-tuple-element.724), channel_id=1, source_target_pairs={{1,0},{2,1},{3,2},{4,3},{5,4},{6,5},{7,6},{8,7},{9,8},{10,9},{11,1... | collective-permute-start | bytes 196616 | tf_op jit(solution)/shard_map/ppermute | solution.py:123
  121.2 7.0 %collective-permute-start.5 = (f32[1,64,256]{2,1,0:T(8,128)S(1)}, f32[1,64,256]{2,1,0:T(8,128)S(1)}, u32[]{:S(2)}, u32[]{:S(2)}) collective-permute-start(f32[1,64,256]{2,1,0:T(8,128)S(1)} %get-tuple-element.724), channel_id=1, source_target_pairs={{0,1},{1,2},{2,3},{3,4},{4,5},{5,6},{6,7},{7,8},{8,9},{9,10},{10,1... | collective-permute-start | bytes 196616 | tf_op jit(solution)/shard_map/ppermute | solution.py:122
  159.7 6.2 %collective-permute-start.6 = (f32[1,64,256]{2,1,0:T(8,128)S(1)}, f32[1,64,256]{2,1,0:T(8,128)S(1)}, u32[]{:S(2)}, u32[]{:S(2)}) collective-permute-start(f32[1,64,256]{2,1,0:T(8,128)S(1)} %fusion.403), channel_id=1, source_target_pairs={{1,0},{2,1},{3,2},{4,3},{5,4},{6,5},{7,6},{8,7},{9,8},{10,9},{11,1... | collective-permute-start | bytes 196616 | tf_op jit(solution)/shard_map/ppermute | solution.py:123
  160.9 6.4 %collective-permute-start.7 = (f32[1,64,256]{2,1,0:T(8,128)S(1)}, f32[1,64,256]{2,1,0:T(8,128)S(1)}, u32[]{:S(2)}, u32[]{:S(2)}) collective-permute-start(f32[1,64,256]{2,1,0:T(8,128)S(1)} %fusion.403), channel_id=1, source_target_pairs={{0,1},{1,2},{2,3},{3,4},{4,5},{5,6},{6,7},{7,8},{8,9},{9,10},{10,1... | collective-permute-start | bytes 196616 | tf_op jit(solution)/shard_map/ppermute | solution.py:122
  197.6 6.2 %collective-permute-start.8 = (f32[1,64,256]{2,1,0:T(8,128)S(1)}, f32[1,64,256]{2,1,0:T(8,128)S(1)}, u32[]{:S(2)}, u32[]{:S(2)}) collective-permute-start(f32[1,64,256]{2,1,0:T(8,128)S(1)} %get-tuple-element.720), channel_id=1, source_target_pairs={{1,0},{2,1},{3,2},{4,3},{5,4},{6,5},{7,6},{8,7},{9,8},{10,9},{11,1... | collective-permute-start | bytes 196616 | tf_op jit(solution)/shard_map/ppermute | solution.py:123
  198.9 6.4 %collective-permute-start.9 = (f32[1,64,256]{2,1,0:T(8,128)S(1)}, f32[1,64,256]{2,1,0:T(8,128)S(1)}, u32[]{:S(2)}, u32[]{:S(2)}) collective-permute-start(f32[1,64,256]{2,1,0:T(8,128)S(1)} %get-tuple-element.720), channel_id=1, source_target_pairs={{0,1},{1,2},{2,3},{3,4},{4,5},{5,6},{6,7},{7,8},{8,9},{9,10},{10,1... | collective-permute-start | bytes 196616 | tf_op jit(solution)/shard_map/ppermute | solution.py:122
  236.2 6.2 %collective-permute-start.10 = (f32[1,64,256]{2,1,0:T(8,128)S(1)}, f32[1,64,256]{2,1,0:T(8,128)S(1)}, u32[]{:S(2)}, u32[]{:S(2)}) collective-permute-start(f32[1,64,256]{2,1,0:T(8,128)S(1)} %get-tuple-element.718), channel_id=1, source_target_pairs={{1,0},{2,1},{3,2},{4,3},{5,4},{6,5},{7,6},{8,7},{9,8},{10,9},{11,1... | collective-permute-start | bytes 196616 | tf_op jit(solution)/shard_map/ppermute | solution.py:123
  237.5 6.4 %collective-permute-start.11 = (f32[1,64,256]{2,1,0:T(8,128)S(1)}, f32[1,64,256]{2,1,0:T(8,128)S(1)}, u32[]{:S(2)}, u32[]{:S(2)}) collective-permute-start(f32[1,64,256]{2,1,0:T(8,128)S(1)} %get-tuple-element.718), channel_id=1, source_target_pairs={{0,1},{1,2},{2,3},{3,4},{4,5},{5,6},{6,7},{7,8},{8,9},{9,10},{10,1... | collective-permute-start | bytes 196616 | tf_op jit(solution)/shard_map/ppermute | solution.py:122
  246.4 23.2 %all-to-all-start.5 = ((f32[32,1,32,128]{3,2,1,0:T(8,128)}), f32[32,1,32,128]{3,2,1,0:T(8,128)}, u32[]{:S(2)}, u32[]{:S(2)}) async-start(f32[32,1,32,128]{3,2,1,0:T(8,128)} %broadcast_in_dim.204), calls=%async_computation.5 | async-start | bytes 1048576 | tf_op jit(solution)/shard_map/all_to_all | solution.py:318
  275.8 29.7 %all-to-all-start.6 = ((f32[8,16,32,128]{3,2,1,0:T(8,128)}), f32[8,16,32,128]{3,2,1,0:T(8,128)}, u32[]{:S(2)}, u32[]{:S(2)}) async-start(f32[8,16,32,128]{3,2,1,0:T(8,128)} %broadcast_in_dim.205), calls=%async_computation.6 | async-start | bytes 4194304 | tf_op jit(solution)/shard_map/all_to_all | solution.py:391
  329.6 5.8 %collective-permute-start.12 = (f32[1,64,256]{2,1,0:T(8,128)S(1)}, f32[1,64,256]{2,1,0:T(8,128)S(1)}, u32[]{:S(2)}, u32[]{:S(2)}) collective-permute-start(f32[1,64,256]{2,1,0:T(8,128)S(1)} %fusion.70), channel_id=1, source_target_pairs={{0,32},{32,64},{64,96},{96,128},{128,160},{160,192},{192,224},{1,3... | collective-permute-start | bytes 196616 | tf_op jit(solution)/shard_map/ppermute | solution.py:37
  335.4 4.4 collective-permute-start.13
  337.9 6.2 %collective-permute-start.14 = (f32[1,64,256]{2,1,0:T(8,128)S(1)}, f32[1,64,256]{2,1,0:T(8,128)S(1)}, u32[]{:S(2)}, u32[]{:S(2)}) collective-permute-start(f32[1,64,256]{2,1,0:T(8,128)S(1)} %broadcast_select_fusion), channel_id=1, source_target_pairs={{1,0},{2,1},{3,2},{4,3},{5,4},{6,5},{7,6},{8,7},{9,8},{10,9},{11,1... | collective-permute-start | bytes 196616 | tf_op jit(solution)/shard_map/ppermute | solution.py:123
  345.1 6.2 %collective-permute-start.15 = (f32[1,64,256]{2,1,0:T(8,128)S(1)}, f32[1,64,256]{2,1,0:T(8,128)S(1)}, u32[]{:S(2)}, u32[]{:S(2)}) collective-permute-start(f32[1,64,256]{2,1,0:T(8,128)S(1)} %get-tuple-element.708), channel_id=1, source_target_pairs={{1,0},{2,1},{3,2},{4,3},{5,4},{6,5},{7,6},{8,7},{9,8},{10,9},{11,1... | collective-permute-start | bytes 196616 | tf_op jit(solution)/shard_map/ppermute | solution.py:123
  346.4 6.4 %collective-permute-start.16 = (f32[1,64,256]{2,1,0:T(8,128)S(1)}, f32[1,64,256]{2,1,0:T(8,128)S(1)}, u32[]{:S(2)}, u32[]{:S(2)}) collective-permute-start(f32[1,64,256]{2,1,0:T(8,128)S(1)} %get-tuple-element.708), channel_id=1, source_target_pairs={{0,1},{1,2},{2,3},{3,4},{4,5},{5,6},{6,7},{7,8},{8,9},{9,10},{10,1... | collective-permute-start | bytes 196616 | tf_op jit(solution)/shard_map/ppermute | solution.py:122
  384.5 6.2 %collective-permute-start.17 = (f32[1,64,256]{2,1,0:T(8,128)S(1)}, f32[1,64,256]{2,1,0:T(8,128)S(1)}, u32[]{:S(2)}, u32[]{:S(2)}) collective-permute-start(f32[1,64,256]{2,1,0:T(8,128)S(1)} %fusion.404), channel_id=1, source_target_pairs={{1,0},{2,1},{3,2},{4,3},{5,4},{6,5},{7,6},{8,7},{9,8},{10,9},{11,1... | collective-permute-start | bytes 196616 | tf_op jit(solution)/shard_map/ppermute | solution.py:123
  385.8 6.4 %collective-permute-start.18 = (f32[1,64,256]{2,1,0:T(8,128)S(1)}, f32[1,64,256]{2,1,0:T(8,128)S(1)}, u32[]{:S(2)}, u32[]{:S(2)}) collective-permute-start(f32[1,64,256]{2,1,0:T(8,128)S(1)} %fusion.404), channel_id=1, source_target_pairs={{0,1},{1,2},{2,3},{3,4},{4,5},{5,6},{6,7},{7,8},{8,9},{9,10},{10,1... | collective-permute-start | bytes 196616 | tf_op jit(solution)/shard_map/ppermute | solution.py:122
  422.4 6.2 %collective-permute-start.19 = (f32[1,64,256]{2,1,0:T(8,128)S(1)}, f32[1,64,256]{2,1,0:T(8,128)S(1)}, u32[]{:S(2)}, u32[]{:S(2)}) collective-permute-start(f32[1,64,256]{2,1,0:T(8,128)S(1)} %get-tuple-element.704), channel_id=1, source_target_pairs={{1,0},{2,1},{3,2},{4,3},{5,4},{6,5},{7,6},{8,7},{9,8},{10,9},{11,1... | collective-permute-start | bytes 196616 | tf_op jit(solution)/shard_map/ppermute | solution.py:123
  423.7 6.4 %collective-permute-start.20 = (f32[1,64,256]{2,1,0:T(8,128)S(1)}, f32[1,64,256]{2,1,0:T(8,128)S(1)}, u32[]{:S(2)}, u32[]{:S(2)}) collective-permute-start(f32[1,64,256]{2,1,0:T(8,128)S(1)} %get-tuple-element.704), channel_id=1, source_target_pairs={{0,1},{1,2},{2,3},{3,4},{4,5},{5,6},{6,7},{7,8},{8,9},{9,10},{10,1... | collective-permute-start | bytes 196616 | tf_op jit(solution)/shard_map/ppermute | solution.py:122
  461.6 6.1 %collective-permute-start.21 = (f32[1,64,256]{2,1,0:T(8,128)S(1)}, f32[1,64,256]{2,1,0:T(8,128)S(1)}, u32[]{:S(2)}, u32[]{:S(2)}) collective-permute-start(f32[1,64,256]{2,1,0:T(8,128)S(1)} %get-tuple-element.702), channel_id=1, source_target_pairs={{1,0},{2,1},{3,2},{4,3},{5,4},{6,5},{7,6},{8,7},{9,8},{10,9},{11,1... | collective-permute-start | bytes 196616 | tf_op jit(solution)/shard_map/ppermute | solution.py:123
  462.9 6.7 %collective-permute-start.22 = (f32[1,64,256]{2,1,0:T(8,128)S(1)}, f32[1,64,256]{2,1,0:T(8,128)S(1)}, u32[]{:S(2)}, u32[]{:S(2)}) collective-permute-start(f32[1,64,256]{2,1,0:T(8,128)S(1)} %get-tuple-element.702), channel_id=1, source_target_pairs={{0,1},{1,2},{2,3},{3,4},{4,5},{5,6},{6,7},{7,8},{8,9},{9,10},{10,1... | collective-permute-start | bytes 196616 | tf_op jit(solution)/shard_map/ppermute | solution.py:122
  495.0 29.7 %all-to-all-start.11 = ((f32[8,16,32,128]{3,2,1,0:T(8,128)}), f32[8,16,32,128]{3,2,1,0:T(8,128)}, u32[]{:S(2)}, u32[]{:S(2)}) async-start(f32[8,16,32,128]{3,2,1,0:T(8,128)} %broadcast_in_dim.211), calls=%async_computation.11 | async-start | bytes 4194304 | tf_op jit(solution)/shard_map/all_to_all | solution.py:391
  (86 other events, 867.8 us)
